TPU v7x, 32 devices: a whole 2x2x4 slice. The times are simulated.
32 devices in a mesh: dom: 4 (over x, core), fsdp: 8 (over z, y).
Axes of the slice: x: 2, y: 2, z: 4, core: 2. Of those that a mesh axis runs over, the one named last changes fastest.
Arguments:
- acts: bfloat16 [4096, 14336], P(('dom', 'fsdp')), may hold values from -24 to 24
- cotangent: bfloat16 [4096, 4096], P(('dom', 'fsdp')), may hold values from -0.75 to 0.75
- weight: bfloat16 [14336, 4096], P(('dom', 'fsdp')), may hold values from -0.046875 to 0.046875
- moment: float32 [14336, 4096], P(('dom', 'fsdp')), may hold values from -6 to 6
- second: float32 [14336, 4096], P(('dom', 'fsdp')), may hold values from 0.3 to 3
- log_weights: float32 [4], replicated, may hold values from -1 to 1
- domain_ids: int32 [4], replicated, may hold values from 0 to 3, each once
- step_count: int32 [1], replicated, may hold values from 1 to 8
Outputs:
- new_weight: bfloat16 [14336, 4096], P(('dom', 'fsdp'))
- new_moment: float32 [14336, 4096], P(('dom', 'fsdp'))
- new_second: float32 [14336, 4096], P(('dom', 'fsdp'))
- new_domain_weights: float32 [4], replicated
All inputs are finite; a program needn't handle non-finite values.
Results may differ from a plain program's by a relative error of at most 0.001.
Values may be sent and summed in bfloat16 or wider, within the bound.
No kernel may reach another device: no remote copies, remote signals or barrier semaphores. Data moves between devices by JAX's collectives and lax.ppermute only.
A program may use at most 192 MiB of HBM per device.

v0:
```python
import jax
import jax.numpy as jnp
from jax import lax
from jax.sharding import PartitionSpec as P


def on_device(acts, cotangent, weight, moment, second, log_weights, domain_ids, step_count):
    groups = lax.axis_size("dom")
    members = lax.axis_size("fsdp")
    tok_rows = acts.shape[0]
    width = cotangent.shape[1]
    own_rows = weight.shape[0]
    shaped = acts.reshape(tok_rows, groups, members, own_rows)
    columns = lax.all_to_all(shaped, "fsdp", split_axis=2, concat_axis=0, tiled=True)
    selected = columns.reshape(tok_rows * members, groups * own_rows)
    gathered = lax.all_gather(cotangent, "fsdp", axis=0, tiled=True)
    local_grad = lax.dot_general(
        selected, gathered, (((0,), (0,)), ((), ())), preferred_element_type=jnp.float32
    )
    pieces = local_grad.astype(jnp.bfloat16).reshape(groups, own_rows, width)
    owned = lax.all_to_all(pieces, "dom", split_axis=0, concat_axis=0, tiled=True)
    local_gram = jnp.einsum("krd,jrd->kj", owned, owned, preferred_element_type=jnp.float32)
    gram = lax.psum(local_gram, ("dom", "fsdp"))
    score = jnp.sum(gram, axis=1) * (groups / jnp.trace(gram))
    onehot = (domain_ids[:, None] == jnp.arange(groups, dtype=jnp.int32)[None, :]).astype(
        jnp.float32
    )
    logits = log_weights + 2.0 * jnp.sum(onehot * score[:, None], axis=0)
    new_domain_weights = jax.nn.softmax(logits)
    group_w = jnp.sum(onehot * new_domain_weights[None, :], axis=1)
    combined = jnp.zeros((own_rows, width), jnp.float32)
    for group in range(groups):
        combined = combined + group_w[group] * owned[group].astype(jnp.float32)
    steps_f = step_count[0].astype(jnp.float32)
    new_moment = 0.9 * moment + 0.1 * combined
    new_second = 0.95 * second + 0.05 * combined * combined
    fix_one = 1.0 - jnp.exp(steps_f * jnp.log(jnp.float32(0.9)))
    fix_two = 1.0 - jnp.exp(steps_f * jnp.log(jnp.float32(0.95)))
    update = new_moment / fix_one / (jnp.sqrt(new_second / fix_two) + 1e-08)
    new_weight = (weight.astype(jnp.float32) - 0.002 * update).astype(jnp.bfloat16)
    return (new_weight, new_moment, new_second, new_domain_weights)


def solution(mesh):
    return jax.shard_map(
        on_device,
        mesh=mesh,
        in_specs=(
            P(("dom", "fsdp"), None),
            P(("dom", "fsdp"), None),
            P(("dom", "fsdp"), None),
            P(("dom", "fsdp"), None),
            P(("dom", "fsdp"), None),
            P(),
            P(),
            P(),
        ),
        out_specs=(
            P(("dom", "fsdp"), None),
            P(("dom", "fsdp"), None),
            P(("dom", "fsdp"), None),
            P(),
        ),
        check_vma=False,
    )
```

profile of v0, /device:TPU:0, one launch (start us, length us, event | category | flops | bytes accessed | tf_op | source)
XLA Modules:
  0.0 509.5 jit_solution(10704876465588895757)
XLA Ops:
  7.2 0.0 all-gather.2.cloned.1.call-start
  7.2 0.7 all-gather.2.cloned.1.call-update
  7.9 6.1 %copy.16 = bf16[128,14336]{0,1:T(8,128)(2,1)} copy(bf16[128,14336]{1,0:T(8,128)(2,1)} %param.8) | data formatting | bytes 7340032 | tf_op args[0]
  13.9 2.3 copy.17
  16.3 172.2 %all_to_all.20 = bf16[128,4,8,448]{0,3,1,2:T(8,128)(2,1)S(1)} all-to-all(bf16[128,4,8,448]{0,3,1,2:T(8,128)(2,1)S(1)} %copy.17), channel_id=1, replica_groups=mesh['dom'=4,'fsdp'=8] {'fsdp'}, dimensions={2} | all-to-all | bytes 7340032 | tf_op jit(solution)/shard_map/all_to_all | solution.py:14
  188.5 4.2 copy.18
  192.7 13.4 %all-gather.2.cloned.1.call-done = bf16[1024,4096]{1,0:T(8,128)(2,1)} async-done(((bf16[128,4096]{1,0:T(8,128)(2,1)}), bf16[1024,4096]{1,0:T(8,128)(2,1)}) %all-gather.2.cloned.1.call-update) | async-done | bytes 8388624 | tf_op jit(solution)/shard_map/all_gather | solution.py:16
  206.1 21.8 %convolution_convert_fusion = bf16[1792,4096]{1,0:T(8,128)(2,1)} fusion(bf16[1024,4096]{1,0:T(8,128)(2,1)} %all-gather.2.cloned.1.call-done, bf16[224,8,8,128]{3,2,1,0:T(8,128)(2,1)} %bitcast.31), kind=kOutput, calls=%fused_computation | convolution fusion | flops 15039725568 | bytes 26738688 | tf_op jit(solution)/shard_map/dot_general | solution.py:17
  227.9 6.8 %all-to-all-start.1 = ((bf16[4,448,4096]{2,1,0:T(8,128)(2,1)}), bf16[4,448,4096]{2,1,0:T(8,128)(2,1)}, u32[]{:S(2)}, u32[]{:S(2)}) async-start(bf16[4,448,4096]{2,1,0:T(8,128)(2,1)} %bitcast.28), calls=%async_computation.1 | async-start | bytes 29360128 | tf_op jit(solution)/shard_map/all_to_all | solution.py:21
  235.5 0.0 copy-start.1
  235.5 0.0 copy-start
  235.5 159.6 %all-to-all-done.1 = bf16[4,448,4096]{2,1,0:T(8,128)(2,1)} async-done(((bf16[4,448,4096]{2,1,0:T(8,128)(2,1)}), bf16[4,448,4096]{2,1,0:T(8,128)(2,1)}, u32[]{:S(2)}, u32[]{:S(2)}) %all-to-all-start.1) | async-done | bytes 14680096 | tf_op jit(solution)/shard_map/all_to_all | solution.py:21
  395.1 42.2 %fusion.6 = f32[4,4]{1,0:T(4,128)S(1)} fusion(bf16[4,448,4096]{2,1,0:T(8,128)(2,1)} %all-to-all-done.1), kind=kOutput, calls=%fused_computation.11 | convolution fusion | flops 58720256 | bytes 14680128 | tf_op jit(solution)/shard_map/krd,jrd->kj/dot_general | solution.py:22
  437.4 36.8 %psum.7 = f32[4,4]{1,0:T(4,128)S(1)} all-reduce(f32[4,4]{1,0:T(4,128)S(1)} %fusion.6), channel_id=1, replica_groups=mesh['dom'=4,'fsdp'=8] {'dom','fsdp'}, use_global_device_ids=true, to_apply=%region_0.0 | all-reduce | flops 16 | bytes 128 | tf_op jit(solution)/shard_map/psum | solution.py:23
  474.2 0.6 select_reduce_fusion.2
  475.6 0.0 copy-done.1
  475.6 0.1 select_reduce_fusion.1
  475.7 0.0 copy-done
  475.7 0.6 fusion.9
  476.3 1.3 fusion.12
  477.5 0.6 broadcast_divide_fusion
  478.2 0.0 copy-start.2
  478.2 0.2 select_reduce_fusion
  478.4 0.7 fusion.13
  479.1 23.6 %subtract_convert_fusion = (bf16[448,4096]{1,0:T(8,128)(2,1)}, f32[448,4096]{1,0:T(8,128)}, f32[448,4096]{1,0:T(8,128)}) fusion(bf16[448,4096]{1,0:T(8,128)(2,1)} %param.10, f32[]{:T(128)} %bitcast.11, f32[]{:T(128)} %bitcast.10, bf16[4,448,4096]{2,1,0:T(8,128)(2,1)} %all-to-all-done.1, f32[]{:T(128)} %bitcast.8, f32[]{:T(128)} %bitcast.7, f32[]{:T(128)} %bitcast.6, ...), kind=kLoop, calls=%fused_computation.7 | loop fusion | flops 47710208 | bytes 51380248 | tf_op jit(solution)/shard_map/convert_element_type | solution.py:40
  502.7 0.0 copy-done.2
  (1 shorter events, 0.0 us)
Async XLA Ops:
  7.2 199.0 %all-gather.2.cloned.1.call-start = ((), (), s32[]{:S(2)}) async-start(), calls=%async_computation.2 | async-start | bytes 9437184 | tf_op jit(solution)/shard_map/all_gather | solution.py:16
  227.9 167.2 %all-to-all-start.1 = ((bf16[4,448,4096]{2,1,0:T(8,128)(2,1)}), bf16[4,448,4096]{2,1,0:T(8,128)(2,1)}, u32[]{:S(2)}, u32[]{:S(2)}) async-start(bf16[4,448,4096]{2,1,0:T(8,128)(2,1)} %bitcast.28), calls=%async_computation.1 | async-start | bytes 29360128 | tf_op jit(solution)/shard_map/all_to_all | solution.py:21
  235.5 240.1 %copy-start.1 = (s32[4]{0:T(128)S(1)}, s32[4]{0:T(128)}, u32[]{:S(2)}) copy-start(s32[4]{0:T(128)} %param.14) | copy-start | bytes 52
  235.5 240.2 %copy-start = (f32[4]{0:T(128)S(1)}, f32[4]{0:T(128)}, u32[]{:S(2)}) copy-start(f32[4]{0:T(128)} %param.13) | copy-start | bytes 52
  478.2 24.5 %copy-start.2 = (f32[4]{0:T(128)}, f32[4]{0:T(128)S(1)}, u32[]{:S(2)}) copy-start(f32[4]{0:T(128)S(1)} %broadcast_divide_fusion) | copy-start | bytes 52
Sparse Core Ops, SparseCore 0:
  10.1 195.9 all-gather.1
where the time goes:
time: 511 us; the launch traced here: 510 us
  blocking collectives  209 us (41%)
  waiting for transfers between devices  174 us (34%)
  matrix products  64 us (13%)
  other arithmetic  27 us (5%)
  between operations  15.5 us (3%)
  local copies, waits for them, and re-layouts  13.3 us (3%)
  starting transfers between devices  6.86 us (1%)
    all_to_all x1, blocking collectives, on_device(): lax.all_to_all(shaped, 'fsdp', split_axis=2, concat_axis=0, tiled=True)  172 us
    all_to_all x1, waiting for transfers between devices, on_device(): lax.all_to_all(pieces, 'dom', split_axis=0, concat_axis=0, tiled=True)  160 us
    dot_general x1, matrix products, on_device(): jnp.einsum('krd,jrd->kj', owned, owned, preferred_element_type=jnp.float32)  42.2 us
    psum x1, blocking collectives, on_device(): gram = lax.psum(local_gram, ('dom', 'fsdp'))  36.8 us
    convert_element_type x1, other arithmetic, on_device(): (weight.astype(jnp.float32) - 0.002 * update).astype(jnp.bfloat16)  23.6 us
    dot_general x1, matrix products, on_device(): lax.dot_general(selected, gathered, (((0,), (0,)), ((), ())), preferred_e...  21.8 us
    all_gather x1, waiting for transfers between devices, on_device(): gathered = lax.all_gather(cotangent, 'fsdp', axis=0, tiled=True)  13.4 us
  transfers between devices with their start and end apart: 2, of which 2 were waited for; matrix products, arithmetic and copies ran while one was open for 2% of the time, Pallas kernels for 0%

commit v1 on v0

v1 whole, which is shorter than its diff:
```python
import jax
import jax.numpy as jnp
from jax import lax
from jax.sharding import PartitionSpec as P

ALL = ("dom", "fsdp")


def on_device(acts, cotangent, weight, moment, second, log_weights, domain_ids, step_count):
    groups = lax.axis_size("dom")
    devices = lax.axis_size(ALL)
    tok_rows = acts.shape[0]
    width = cotangent.shape[1]
    own_rows = weight.shape[0]
    shaped = acts.reshape(tok_rows, devices, own_rows)
    columns = lax.all_to_all(shaped, ALL, split_axis=1, concat_axis=0, tiled=True)
    columns = columns.reshape(groups, devices // groups * tok_rows, own_rows)
    gathered = lax.all_gather(cotangent, ALL, axis=0, tiled=True)
    gathered = gathered.reshape(groups, devices // groups * tok_rows, width)
    owned = lax.dot_general(
        columns, gathered, (((1,), (1,)), ((0,), (0,))), preferred_element_type=jnp.float32
    ).astype(jnp.bfloat16)
    local_gram = jnp.einsum("krd,jrd->kj", owned, owned, preferred_element_type=jnp.float32)
    gram = lax.psum(local_gram, ALL)
    score = jnp.sum(gram, axis=1) * (groups / jnp.trace(gram))
    onehot = (domain_ids[:, None] == jnp.arange(groups, dtype=jnp.int32)[None, :]).astype(
        jnp.float32
    )
    logits = log_weights + 2.0 * jnp.sum(onehot * score[:, None], axis=0)
    new_domain_weights = jax.nn.softmax(logits)
    group_w = jnp.sum(onehot * new_domain_weights[None, :], axis=1)
    combined = jnp.zeros((own_rows, width), jnp.float32)
    for group in range(groups):
        combined = combined + group_w[group] * owned[group].astype(jnp.float32)
    steps_f = step_count[0].astype(jnp.float32)
    new_moment = 0.9 * moment + 0.1 * combined
    new_second = 0.95 * second + 0.05 * combined * combined
    fix_one = 1.0 - jnp.exp(steps_f * jnp.log(jnp.float32(0.9)))
    fix_two = 1.0 - jnp.exp(steps_f * jnp.log(jnp.float32(0.95)))
    update = new_moment / fix_one / (jnp.sqrt(new_second / fix_two) + 1e-08)
    new_weight = (weight.astype(jnp.float32) - 0.002 * update).astype(jnp.bfloat16)
    return (new_weight, new_moment, new_second, new_domain_weights)


def solution(mesh):
    return jax.shard_map(
        on_device,
        mesh=mesh,
        in_specs=(
            P(ALL, None),
            P(ALL, None),
            P(ALL, None),
            P(ALL, None),
            P(ALL, None),
            P(),
            P(),
            P(),
        ),
        out_specs=(
            P(ALL, None),
            P(ALL, None),
            P(ALL, None),
            P(),
        ),
        check_vma=False,
    )
```

time: 511 us -> 420 us (0.82)
  blocking collectives: 209 us -> 38.4 us
  waiting for transfers between devices: 174 us -> 241 us
  local copies, waits for them, and re-layouts: 13.3 us -> 20.2 us
  matrix products: 64 us -> 70.5 us
    all_to_all x1 -> x0, blocking collectives: 172 us -> none  [on_device(): lax.all_to_all(shaped, 'fsdp', split_axis=2, concat_axis=0, tiled=True)]
    all_gather x1, waiting for transfers between devices: 13.4 us -> 91.2 us  [on_device(): gathered = lax.all_gather(cotangent, ALL, axis=0, tiled=True)]
    all_to_all x1, waiting for transfers between devices: 160 us -> 149 us  [on_device(): lax.all_to_all(shaped, ALL, split_axis=1, concat_axis=0, tiled=True)]
    dot_general x1, matrix products: 21.8 us -> 28.1 us  [on_device(): lax.dot_general(columns, gathered, (((1,), (1,)), ((0,), (0,))), preferre...]
  transfers between devices with their start and end apart: 2 -> 2, of which waited for: 2 -> 2; matrix products, arithmetic and copies ran while one was open for 2% -> 5% of each run, Pallas kernels for 0% -> 0%
where the time goes in v1:
time: 420 us
  waiting for transfers between devices  241 us (57%)
  matrix products  70.5 us (17%)
  blocking collectives  38.4 us (9%)
  other arithmetic  26.8 us (6%)
  local copies, waits for them, and re-layouts  20.2 us (5%)
  between operations  15.5 us (4%)
  starting transfers between devices  7.45 us (2%)
    all_to_all x1, waiting for transfers between devices, on_device(): lax.all_to_all(shaped, ALL, split_axis=1, concat_axis=0, tiled=True)  149 us
    all_gather x1, waiting for transfers between devices, on_device(): gathered = lax.all_gather(cotangent, ALL, axis=0, tiled=True)  91.2 us
    dot_general x1, matrix products, on_device(): jnp.einsum('krd,jrd->kj', owned, owned, preferred_element_type=jnp.float32)  42.4 us
    psum x1, blocking collectives, on_device(): gram = lax.psum(local_gram, ALL)  38.4 us
    dot_general x1, matrix products, on_device(): lax.dot_general(columns, gathered, (((1,), (1,)), ((0,), (0,))), preferre...  28.1 us
    convert_element_type x1, other arithmetic, on_device(): (weight.astype(jnp.float32) - 0.002 * update).astype(jnp.bfloat16)  23.3 us
  transfers between devices with their start and end apart: 2, of which 2 were waited for; matrix products, arithmetic and copies ran while one was open for 5% of the time, Pallas kernels for 0%

profile of v1, /device:TPU:0, one launch (start us, length us, event | category | flops | bytes accessed | tf_op | source)
XLA Modules:
  0.0 419.7 jit_solution(17461181744610449486)
XLA Ops:
  7.2 0.0 all-gather.2.cloned.1.call-start
  7.2 0.7 all-gather.2.cloned.1.call-update
  7.9 6.1 %copy.14 = bf16[128,14336]{0,1:T(8,128)(2,1)} copy(bf16[128,14336]{1,0:T(8,128)(2,1)} %param.8) | data formatting | bytes 7340032 | tf_op args[0]
  13.9 7.4 %all-to-all-start = ((bf16[128,32,448]{0,2,1:T(8,128)(2,1)}), bf16[128,32,448]{0,2,1:T(8,128)(2,1)}, u32[]{:S(2)}, u32[]{:S(2)}) async-start(bf16[128,32,448]{0,2,1:T(8,128)(2,1)} %bitcast.25), calls=%async_computation | async-start | bytes 7340032 | tf_op jit(solution)/shard_map/all_to_all | solution.py:16
  22.1 149.0 %all-to-all-done = bf16[128,32,448]{0,2,1:T(8,128)(2,1)} async-done(((bf16[128,32,448]{0,2,1:T(8,128)(2,1)}), bf16[128,32,448]{0,2,1:T(8,128)(2,1)}, u32[]{:S(2)}, u32[]{:S(2)}) %all-to-all-start) | async-done | bytes 3670048 | tf_op jit(solution)/shard_map/all_to_all | solution.py:16
  171.1 6.8 %copy.15 = bf16[32,128,1,448]{1,0,3,2:T(8,128)(2,1)} copy(bf16[32,128,1,448]{1,3,0,2:T(8,128)(2,1)} %bitcast.2) | data formatting | bytes 7340032 | tf_op jit(solution)/shard_map/all_to_all | solution.py:16
  177.9 6.7 %reshape.51 = bf16[4,1024,448]{1,0,2:T(4,128)(2,1)} reshape(bf16[32,128,1,448]{1,0,3,2:T(8,128)(2,1)} %copy.15) | data formatting | bytes 7340032 | tf_op jit(solution)/shard_map/reshape | solution.py:17
  184.6 91.2 %all-gather.2.cloned.1.call-done = bf16[4096,4096]{1,0:T(8,128)(2,1)} async-done(((bf16[128,4096]{1,0:T(8,128)(2,1)}), bf16[4096,4096]{1,0:T(8,128)(2,1)}) %all-gather.2.cloned.1.call-update) | async-done | bytes 33554448 | tf_op jit(solution)/shard_map/all_gather | solution.py:18
  275.8 28.1 %convolution_convert_fusion = bf16[4,448,4096]{2,1,0:T(8,128)(2,1)} fusion(bf16[4,1024,4096]{2,1,0:T(8,128)(2,1)} %bitcast.26, bf16[4,1024,448]{1,0,2:T(4,128)(2,1)} %reshape.51), kind=kOutput, calls=%fused_computation.3 | convolution fusion | flops 15039725568 | bytes 51904512 | tf_op jit(solution)/shard_map/dot_general | solution.py:20
  303.9 0.0 copy-start.1
  303.9 0.0 copy-start
  303.9 42.4 %fusion.5 = f32[4,4]{1,0:T(4,128)S(1)} fusion(bf16[4,448,4096]{2,1,0:T(8,128)(2,1)} %convolution_convert_fusion), kind=kOutput, calls=%fused_computation.10 | convolution fusion | flops 58720256 | bytes 14680128 | tf_op jit(solution)/shard_map/krd,jrd->kj/dot_general | solution.py:23
  346.3 38.4 %psum.7 = f32[4,4]{1,0:T(4,128)S(1)} all-reduce(f32[4,4]{1,0:T(4,128)S(1)} %fusion.5), channel_id=1, replica_groups=mesh['dom'=4,'fsdp'=8] {'dom','fsdp'}, use_global_device_ids=true, to_apply=%region_0.0 | all-reduce | flops 16 | bytes 128 | tf_op jit(solution)/shard_map/psum | solution.py:24
  384.7 0.6 select_reduce_fusion.2
  386.0 0.0 copy-done.1
  386.0 0.1 select_reduce_fusion.1
  386.1 0.0 copy-done
  386.1 0.6 fusion.8
  386.7 1.3 fusion.11
  388.0 0.6 broadcast_divide_fusion
  388.6 0.0 copy-start.2
  388.6 0.2 select_reduce_fusion
  388.8 0.7 fusion.12
  389.5 23.3 %subtract_convert_fusion = (bf16[448,4096]{1,0:T(8,128)(2,1)}, f32[448,4096]{1,0:T(8,128)}, f32[448,4096]{1,0:T(8,128)}) fusion(bf16[448,4096]{1,0:T(8,128)(2,1)} %param.10, f32[]{:T(128)} %bitcast.11, f32[]{:T(128)} %bitcast.10, bf16[4,448,4096]{2,1,0:T(8,128)(2,1)} %convolution_convert_fusion, f32[]{:T(128)} %bitcast.8, f32[]{:T(128)} %bitcast.7, ...), kind=kLoop, calls=%fused_computation.7 | loop fusion | flops 47710208 | bytes 51380248 | tf_op jit(solution)/shard_map/convert_element_type | solution.py:41
  412.8 0.0 copy-done.2
  (1 shorter events, 0.0 us)
Async XLA Ops:
  7.2 268.6 %all-gather.2.cloned.1.call-start = ((), (), s32[]{:S(2)}) async-start(), calls=%async_computation.1 | async-start | bytes 34603008 | tf_op jit(solution)/shard_map/all_gather | solution.py:18
  13.9 157.1 %all-to-all-start = ((bf16[128,32,448]{0,2,1:T(8,128)(2,1)}), bf16[128,32,448]{0,2,1:T(8,128)(2,1)}, u32[]{:S(2)}, u32[]{:S(2)}) async-start(bf16[128,32,448]{0,2,1:T(8,128)(2,1)} %bitcast.25), calls=%async_computation | async-start | bytes 7340032 | tf_op jit(solution)/shard_map/all_to_all | solution.py:16
  303.9 82.2 %copy-start.1 = (s32[4]{0:T(128)S(1)}, s32[4]{0:T(128)}, u32[]{:S(2)}) copy-start(s32[4]{0:T(128)} %param.14) | copy-start | bytes 52
  303.9 82.3 %copy-start = (f32[4]{0:T(128)S(1)}, f32[4]{0:T(128)}, u32[]{:S(2)}) copy-start(f32[4]{0:T(128)} %param.13) | copy-start | bytes 52
  388.6 24.2 %copy-start.2 = (f32[4]{0:T(128)}, f32[4]{0:T(128)S(1)}, u32[]{:S(2)}) copy-start(f32[4]{0:T(128)S(1)} %broadcast_divide_fusion) | copy-start | bytes 52
Sparse Core Ops, SparseCore 0:
  11.0 264.7 all-gather.1

commit v2 on v1

v2 whole, which is shorter than its diff:
```python
import jax
import jax.numpy as jnp
from jax import lax
from jax.sharding import Mesh, PartitionSpec as P

FLAT = ("x", "core", "fsdp")


def on_device(acts, cotangent, weight, moment, second, log_weights, domain_ids, step_count):
    groups = lax.axis_size("x") * lax.axis_size("core")
    devices = lax.axis_size(FLAT)
    tok_rows = acts.shape[0]
    group_tok = devices // groups * tok_rows
    width = cotangent.shape[1]
    own_rows = weight.shape[0]
    core = lax.axis_index("core")
    shaped = acts.reshape(tok_rows, devices, own_rows)
    columns = lax.all_to_all(shaped, FLAT, split_axis=1, concat_axis=0, tiled=True)
    columns = columns.reshape(groups, group_tok, own_rows)
    mine = lax.all_gather(cotangent, ("x", "fsdp"), axis=0, tiled=True)
    mine = mine.reshape(groups // 2, group_tok, width)
    theirs = lax.ppermute(mine, "core", [(0, 1), (1, 0)])
    half = jnp.arange(groups // 2, dtype=jnp.int32) * 2
    order = jnp.concatenate([half + core, half + 1 - core])
    local_cols = jnp.take(columns, order, axis=0)
    dims = (((1,), (1,)), ((0,), (0,)))
    g_mine = lax.dot_general(local_cols[: groups // 2], mine, dims, preferred_element_type=jnp.float32)
    g_theirs = lax.dot_general(local_cols[groups // 2 :], theirs, dims, preferred_element_type=jnp.float32)
    owned = jnp.concatenate([g_mine, g_theirs]).astype(jnp.bfloat16)
    pairs = {}
    for i in range(groups):
        for j in range(i, groups):
            pairs[i, j] = jnp.sum(
                owned[i].astype(jnp.float32) * owned[j].astype(jnp.float32)
            )
    local_gram = jnp.stack(
        [jnp.stack([pairs[min(i, j), max(i, j)] for j in range(groups)]) for i in range(groups)]
    )
    perm = (order[:, None] == jnp.arange(groups, dtype=jnp.int32)[None, :]).astype(jnp.float32)
    device_gram = jnp.dot(
        perm.T, jnp.dot(local_gram, perm, precision=lax.Precision.HIGHEST),
        precision=lax.Precision.HIGHEST,
    )
    gram = lax.psum(device_gram, FLAT)
    score = jnp.sum(gram, axis=1) * (groups / jnp.trace(gram))
    onehot = (domain_ids[:, None] == jnp.arange(groups, dtype=jnp.int32)[None, :]).astype(
        jnp.float32
    )
    logits = log_weights + 2.0 * jnp.sum(onehot * score[:, None], axis=0)
    new_domain_weights = jax.nn.softmax(logits)
    group_w = jnp.sum(onehot * new_domain_weights[None, :], axis=1)
    local_w = jnp.take(group_w, order)
    combined = jnp.zeros((own_rows, width), jnp.float32)
    for group in range(groups):
        combined = combined + local_w[group] * owned[group].astype(jnp.float32)
    steps_f = step_count[0].astype(jnp.float32)
    new_moment = 0.9 * moment + 0.1 * combined
    new_second = 0.95 * second + 0.05 * combined * combined
    fix_one = 1.0 - jnp.exp(steps_f * jnp.log(jnp.float32(0.9)))
    fix_two = 1.0 - jnp.exp(steps_f * jnp.log(jnp.float32(0.95)))
    update = new_moment / fix_one / (jnp.sqrt(new_second / fix_two) + 1e-08)
    new_weight = (weight.astype(jnp.float32) - 0.002 * update).astype(jnp.bfloat16)
    return (new_weight, new_moment, new_second, new_domain_weights)


def solution(mesh):
    chips = mesh.shape["dom"] // 2
    flat = Mesh(mesh.devices.reshape(chips, 2, mesh.shape["fsdp"]), FLAT)
    row = P(FLAT, None)
    return jax.shard_map(
        on_device,
        mesh=flat,
        in_specs=(row, row, row, row, row, P(), P(), P()),
        out_specs=(row, row, row, P()),
        check_vma=False,
    )
```

time: 420 us -> 444 us (1.057)
  matrix products: 70.5 us -> 28.2 us
  waiting for transfers between devices: 241 us -> 281 us
  other arithmetic: 26.8 us -> 46.9 us
  local copies, waits for them, and re-layouts: 20.2 us -> 29.6 us
    all_gather x1, waiting for transfers between devices: 91.2 us -> 197 us  [on_device(): mine = lax.all_gather(cotangent, ('x', 'fsdp'), axis=0, tiled=True)]
    all_to_all x1, waiting for transfers between devices: 149 us -> 83.5 us  [on_device(): lax.all_to_all(shaped, FLAT, split_axis=1, concat_axis=0, tiled=True)]
    dot_general x2 -> x4, matrix products: 70.5 us -> 28.2 us  [the longest x1 14 us: on_device(): lax.dot_general(local_cols[groups // 2:], theirs, dims, preferred_element...]
    another operation x0 -> x4, other arithmetic: none -> 10.6 us  [on_device(): jnp.stack([jnp.stack([pairs[min(i, j), max(i, j)] for j in range(groups)]...]
    reduce_sum x0 -> x1, other arithmetic: none -> 9.15 us  [on_device(): jnp.sum(owned[i].astype(jnp.float32) * owned[j].astype(jnp.float32))]
    gather x0 -> x2, local copies, waits for them, and re-layouts: none -> 5.29 us  [the longest x1 4.65 us: on_device(): local_cols = jnp.take(columns, order, axis=0)]
    reshape x1 -> x2, local copies, waits for them, and re-layouts: 6.67 us -> 11.3 us  [on_device(): columns = columns.reshape(groups, group_tok, own_rows)]
  transfers between devices with their start and end apart: 2 -> 3, of which waited for: 2 -> 2; matrix products, arithmetic and copies ran while one was open for 5% -> 10% of each run, Pallas kernels for 0% -> 0%
where the time goes in v2:
time: 444 us; the launch traced here: 442 us
  waiting for transfers between devices  281 us (63%)
  other arithmetic  46.9 us (11%)
  blocking collectives  37.1 us (8%)
  local copies, waits for them, and re-layouts  29.6 us (7%)
  matrix products  28.2 us (6%)
  between operations  15.5 us (3%)
    all_gather x1, waiting for transfers between devices, on_device(): mine = lax.all_gather(cotangent, ('x', 'fsdp'), axis=0, tiled=True)  197 us
    all_to_all x1, waiting for transfers between devices, on_device(): lax.all_to_all(shaped, FLAT, split_axis=1, concat_axis=0, tiled=True)  83.5 us
    psum x1, blocking collectives, on_device(): gram = lax.psum(device_gram, FLAT)  37.1 us
    convert_element_type x1, other arithmetic, on_device(): (weight.astype(jnp.float32) - 0.002 * update).astype(jnp.bfloat16)  23.5 us
    dot_general x1, matrix products, on_device(): lax.dot_general(local_cols[groups // 2:], theirs, dims, preferred_element...  14 us
    dot_general x1, matrix products, on_device(): lax.dot_general(local_cols[:groups // 2], mine, dims, preferred_element_t...  13.8 us
    reshape x2, local copies, waits for them, and re-layouts, on_device(): columns = columns.reshape(groups, group_tok, own_rows)  11.3 us
    another operation x4, other arithmetic, on_device(): jnp.stack([jnp.stack([pairs[min(i, j), max(i, j)] for j in range(groups)]...  10.6 us
  transfers between devices with their start and end apart: 3, of which 2 were waited for; matrix products, arithmetic and copies ran while one was open for 10% of the time, Pallas kernels for 0%

profile of v2, /device:TPU:0, one launch (start us, length us, event | category | flops | bytes accessed | tf_op | source)
XLA Modules:
  0.0 442.3 jit_solution(5612027827097999883)
XLA Ops:
  7.2 0.0 all-gather.2.cloned.1.call-start
  7.2 0.7 all-gather.2.cloned.1.call-update
  7.9 197.2 %all-gather.2.cloned.1.call-done = bf16[2048,4096]{1,0:T(8,128)(2,1)} async-done(((bf16[128,4096]{1,0:T(8,128)(2,1)}), bf16[2048,4096]{1,0:T(8,128)(2,1)}) %all-gather.2.cloned.1.call-update) | async-done | bytes 16777232 | tf_op jit(solution)/shard_map/all_gather | solution.py:20
  205.1 6.0 %copy.12 = bf16[128,14336]{0,1:T(8,128)(2,1)} copy(bf16[128,14336]{1,0:T(8,128)(2,1)} %param.8) | data formatting | bytes 7340032 | tf_op args[0]
  211.2 3.5 all-to-all-start
  215.5 0.1 fusion.26
  215.6 0.1 compare_and_fusion
  215.7 83.5 %all-to-all-done = bf16[128,32,448]{0,2,1:T(8,128)(2,1)} async-done(((bf16[128,32,448]{0,2,1:T(8,128)(2,1)}), bf16[128,32,448]{0,2,1:T(8,128)(2,1)}, u32[]{:S(2)}, u32[]{:S(2)}) %all-to-all-start) | async-done | bytes 3670048 | tf_op jit(solution)/shard_map/all_to_all | solution.py:18
  299.2 6.2 %copy.13 = bf16[32,128,1,448]{1,0,3,2:T(8,128)(2,1)} copy(bf16[32,128,1,448]{1,3,0,2:T(8,128)(2,1)} %bitcast.2) | data formatting | bytes 7340032 | tf_op jit(solution)/shard_map/all_to_all | solution.py:18
  305.5 6.3 %reshape.125 = bf16[4,1024,448]{1,0,2:T(4,128)(2,1)} reshape(bf16[32,128,1,448]{1,0,3,2:T(8,128)(2,1)} %copy.13) | data formatting | bytes 7340032 | tf_op jit(solution)/shard_map/reshape | solution.py:19
  311.7 5.1 %copy.14 = bf16[4,1024,448]{1,2,0:T(8,128)(2,1)} copy(bf16[4,1024,448]{1,0,2:T(4,128)(2,1)} %reshape.125) | data formatting | bytes 7340032 | tf_op jit(solution)/shard_map/reshape | solution.py:19
  316.8 4.7 %gather_fusion = bf16[4,1024,448]{1,2,0:T(8,128)(2,1)} fusion(bf16[4,1024,448]{1,2,0:T(8,128)(2,1)} %copy.14, s32[1024]{0:T(1024)S(1)} %pad_clamp_fusion), kind=kCustom, calls=%fused_computation | custom fusion | bytes 7340048 | tf_op jit(solution)/shard_map/jit(_take)/gather | solution.py:25
  321.4 13.8 %convolution_convert_fusion.1 = bf16[2,448,4096]{2,1,0:T(8,128)(2,1)} fusion(bf16[2,1024,4096]{2,1,0:T(8,128)(2,1)} %bitcast.52, bf16[4,1024,448]{1,2,0:T(8,128)(2,1)} %gather_fusion, pred[4]{0:T(512)(128)(4,1)S(1)} %get-tuple-element.21), kind=kOutput, calls=%fused_computation.35 | convolution fusion | flops 7521697792 | bytes 27787268 | tf_op jit(solution)/shard_map/dot_general | solution.py:27
  335.2 14.0 %convolution_convert_fusion = bf16[2,448,4096]{2,1,0:T(8,128)(2,1)} fusion(bf16[2,1024,4096]{2,1,0:T(8,128)(2,1)} %collective-permute-done, bf16[4,1024,448]{1,2,0:T(8,128)(2,1)} %gather_fusion, pred[4]{0:T(512)(128)(4,1)S(1)} %get-tuple-element.21), kind=kOutput, calls=%fused_computation.34 | convolution fusion | flops 7521697792 | bytes 27787268 | tf_op jit(solution)/shard_map/dot_general | solution.py:28
  349.2 9.2 %fusion.8 = (f32[]{:T(128)}, f32[]{:T(128)}, f32[]{:T(128)}, f32[]{:T(128)}, f32[]{:T(128)}, /*index=5*/f32[]{:T(128)}, f32[]{:T(128)}, f32[]{:T(128)}, f32[]{:T(128)}, f32[]{:T(128)}) fusion(bf16[2,448,4096]{2,1,0:T(8,128)(2,1)} %convolution_convert_fusion, bf16[2,448,4096]{2,1,0:T(8,128)(2,1)} %convolution_convert_fusion.1), kind=kLoop, calls=%fused_computation.25 | loop fusion | flops 44040188 | bytes 14680104 | tf_op jit(solution)/shard_map/reduce_sum | solution.py:33
  358.4 2.6 maximum_bitcast_fusion
  360.9 2.6 maximum_bitcast_fusion.1
  363.6 2.7 maximum_bitcast_fusion.2
  366.3 2.7 maximum_bitcast_fusion.3
  368.9 0.2 fusion.15
  369.1 0.3 fusion.23
  369.4 37.1 %psum.7 = f32[4,4]{1,0:T(4,128)S(1)} all-reduce(f32[4,4]{1,0:T(4,128)S(1)} %fusion.23), channel_id=1, replica_groups=mesh['x'=2,'core'=2,'fsdp'=8] {'x','core','fsdp'}, use_global_device_ids=true, to_apply=%region_10.11 | all-reduce | flops 16 | bytes 128 | tf_op jit(solution)/shard_map/psum | solution.py:44
  406.5 0.6 select_reduce_fusion.2
  407.8 0.1 select_reduce_fusion.1
  407.9 0.6 fusion.31
  408.5 1.3 fusion.35
  409.8 0.6 broadcast_divide_fusion
  410.4 0.0 copy-start.2
  410.4 0.2 select_reduce_fusion
  410.6 0.6 gather_fusion.1
  411.3 0.7 fusion.36
  411.9 23.5 %subtract_convert_fusion = (bf16[448,4096]{1,0:T(8,128)(2,1)}, f32[448,4096]{1,0:T(8,128)}, f32[448,4096]{1,0:T(8,128)}) fusion(bf16[448,4096]{1,0:T(8,128)(2,1)} %param.10, f32[]{:T(128)} %bitcast.27, f32[]{:T(128)} %bitcast.26, bf16[2,448,4096]{2,1,0:T(8,128)(2,1)} %convolution_convert_fusion, f32[]{:T(128)} %bitcast.24, f32[]{:T(128)} %bitcast.23, ...), kind=kLoop, calls=%fused_computation.32 | loop fusion | flops 47710208 | bytes 51380248 | tf_op jit(solution)/shard_map/convert_element_type | solution.py:62
  (12 shorter events, 0.0 us)
Async XLA Ops:
  7.2 198.0 %all-gather.2.cloned.1.call-start = ((), (), s32[]{:S(2)}) async-start(), calls=%async_computation.1 | async-start | bytes 17825792 | tf_op jit(solution)/shard_map/all_gather | solution.py:20
  205.1 130.1 %collective-permute-start = (bf16[2,1024,4096]{2,1,0:T(8,128)(2,1)}, bf16[2,1024,4096]{2,1,0:T(8,128)(2,1)}, u32[]{:S(2)}, u32[]{:S(2)}) collective-permute-start(bf16[2,1024,4096]{2,1,0:T(8,128)(2,1)} %bitcast.51), channel_id=1, source_target_pairs={{0,8},{8,0},{1,9},{9,1},{2,10},{10,2},{3,11},{11,3},{4,12},{12,4},... | collective-permute-start | bytes 50331656 | tf_op jit(solution)/shard_map/ppermute | solution.py:22
  211.2 88.0 %all-to-all-start = ((bf16[128,32,448]{0,2,1:T(8,128)(2,1)}), bf16[128,32,448]{0,2,1:T(8,128)(2,1)}, u32[]{:S(2)}, u32[]{:S(2)}) async-start(bf16[128,32,448]{0,2,1:T(8,128)(2,1)} %bitcast.50), calls=%async_computation | async-start | bytes 7340032 | tf_op jit(solution)/shard_map/all_to_all | solution.py:18
  349.2 58.6 %copy-start.1 = (s32[4]{0:T(128)S(1)}, s32[4]{0:T(128)}, u32[]{:S(2)}) copy-start(s32[4]{0:T(128)} %param.14) | copy-start | bytes 52
  349.2 58.7 %copy-start = (f32[4]{0:T(128)S(1)}, f32[4]{0:T(128)}, u32[]{:S(2)}) copy-start(f32[4]{0:T(128)} %param.13) | copy-start | bytes 52
  410.4 25.0 %copy-start.2 = (f32[4]{0:T(128)}, f32[4]{0:T(128)S(1)}, u32[]{:S(2)}) copy-start(f32[4]{0:T(128)S(1)} %broadcast_divide_fusion) | copy-start | bytes 52
Sparse Core Ops, SparseCore 0:
  10.8 194.2 all-gather.1

commit v3 on v2

--- a/solution.py
+++ b/solution.py
@@ -4,29 +4,39 @@
 from jax.sharding import Mesh, PartitionSpec as P
 
 FLAT = ("x", "core", "fsdp")
+SAME_CORE = ("x", "fsdp")
 
 
 def on_device(acts, cotangent, weight, moment, second, log_weights, domain_ids, step_count):
-    groups = lax.axis_size("x") * lax.axis_size("core")
-    devices = lax.axis_size(FLAT)
+    chips_x = lax.axis_size("x")
+    members = lax.axis_size("fsdp")
+    groups = chips_x * 2
     tok_rows = acts.shape[0]
-    group_tok = devices // groups * tok_rows
+    group_tok = members * tok_rows
     width = cotangent.shape[1]
     own_rows = weight.shape[0]
     core = lax.axis_index("core")
-    shaped = acts.reshape(tok_rows, devices, own_rows)
-    columns = lax.all_to_all(shaped, FLAT, split_axis=1, concat_axis=0, tiled=True)
-    columns = columns.reshape(groups, group_tok, own_rows)
-    mine = lax.all_gather(cotangent, ("x", "fsdp"), axis=0, tiled=True)
-    mine = mine.reshape(groups // 2, group_tok, width)
-    theirs = lax.ppermute(mine, "core", [(0, 1), (1, 0)])
-    half = jnp.arange(groups // 2, dtype=jnp.int32) * 2
+    shaped = acts.reshape(tok_rows, chips_x, 2, members, own_rows).transpose(0, 1, 3, 2, 4)
+    shaped = shaped.reshape(tok_rows, chips_x * members, 2 * own_rows)
+    columns = lax.all_to_all(shaped, SAME_CORE, split_axis=1, concat_axis=0, tiled=True)
+    columns = columns.reshape(chips_x, group_tok, 2, own_rows)
+    mine = lax.all_gather(cotangent, SAME_CORE, axis=0, tiled=True)
+    mine = mine.reshape(chips_x, group_tok, width)
+    dims = (((1,), (1,)), ((0,), (0,)))
+    cols_partner = jnp.take(columns, 1 - core, axis=2)
+    cols_own = jnp.take(columns, core, axis=2)
+    g_partner = lax.dot_general(
+        cols_partner, mine, dims, preferred_element_type=jnp.float32
+    ).astype(jnp.bfloat16)
+    received = lax.ppermute(g_partner, "core", [(0, 1), (1, 0)])
+    g_own = lax.dot_general(
+        cols_own, mine, dims, preferred_element_type=jnp.float32
+    ).astype(jnp.bfloat16)
+    owned = jnp.concatenate([g_own, received])
+    half = jnp.arange(chips_x, dtype=jnp.int32) * 2
     order = jnp.concatenate([half + core, half + 1 - core])
-    local_cols = jnp.take(columns, order, axis=0)
-    dims = (((1,), (1,)), ((0,), (0,)))
-    g_mine = lax.dot_general(local_cols[: groups // 2], mine, dims, preferred_element_type=jnp.float32)
-    g_theirs = lax.dot_general(local_cols[groups // 2 :], theirs, dims, preferred_element_type=jnp.float32)
-    owned = jnp.concatenate([g_mine, g_theirs]).astype(jnp.bfloat16)
+    ids = jnp.arange(groups, dtype=jnp.int32)
+    pos = jnp.where(ids % 2 == core, ids // 2, chips_x + ids // 2)
     pairs = {}
     for i in range(groups):
         for j in range(i, groups):
@@ -36,12 +46,8 @@
     local_gram = jnp.stack(
         [jnp.stack([pairs[min(i, j), max(i, j)] for j in range(groups)]) for i in range(groups)]
     )
-    perm = (order[:, None] == jnp.arange(groups, dtype=jnp.int32)[None, :]).astype(jnp.float32)
-    device_gram = jnp.dot(
-        perm.T, jnp.dot(local_gram, perm, precision=lax.Precision.HIGHEST),
-        precision=lax.Precision.HIGHEST,
-    )
-    gram = lax.psum(device_gram, FLAT)
+    device_gram = jnp.take(jnp.take(local_gram, pos, axis=0), pos, axis=1)
+    gram = lax.psum(lax.psum(lax.psum(device_gram, "core"), "x"), "fsdp")
     score = jnp.sum(gram, axis=1) * (groups / jnp.trace(gram))
     onehot = (domain_ids[:, None] == jnp.arange(groups, dtype=jnp.int32)[None, :]).astype(
         jnp.float32

time: 444 us -> 385 us (0.87)
  waiting for transfers between devices: 281 us -> 225 us
  blocking collectives: 37.1 us -> 26.9 us
  starting transfers between devices: 3.59 us -> 8.4 us
    all_gather x1, waiting for transfers between devices: 197 us -> 82.7 us  [on_device(): mine = lax.all_gather(cotangent, SAME_CORE, axis=0, tiled=True)]
    all_to_all x1, waiting for transfers between devices: 83.5 us -> 141 us  [on_device(): lax.all_to_all(shaped, SAME_CORE, split_axis=1, concat_axis=0, tiled=True)]
    psum x1 -> x3, blocking collectives: 37.1 us -> 26.9 us  [on_device(): gram = lax.psum(lax.psum(lax.psum(device_gram, 'core'), 'x'), 'fsdp')]
    another operation x0 -> x1, local copies, waits for them, and re-layouts: none -> 5.83 us  [on_device(): cols_own = jnp.take(columns, core, axis=2)]
    all_to_all x1, starting transfers between devices: 3.55 us -> 8.36 us  [on_device(): lax.all_to_all(shaped, SAME_CORE, split_axis=1, concat_axis=0, tiled=True)]
    reshape x2 -> x1, local copies, waits for them, and re-layouts: 11.3 us -> 6.54 us  [on_device(): columns = columns.reshape(chips_x, group_tok, 2, own_rows)]
    dot_general x4 -> x2, matrix products: 28.2 us -> 30.3 us  [the longest x1 16.3 us: on_device(): lax.dot_general(cols_partner, mine, dims, preferred_element_type=jnp.floa...]
    another operation x4 -> x3, other arithmetic: 10.6 us -> 9.15 us  [on_device(): jnp.stack([jnp.stack([pairs[min(i, j), max(i, j)] for j in range(groups)]...]
  transfers between devices with their start and end apart: 3 -> 3, of which waited for: 2 -> 2; matrix products, arithmetic and copies ran while one was open for 10% -> 11% of each run, Pallas kernels for 0% -> 0%
where the time goes in v3:
time: 385 us; the launch traced here: 384 us
  waiting for transfers between devices  225 us (58%)
  other arithmetic  45.9 us (12%)
  local copies, waits for them, and re-layouts  31.8 us (8%)
  matrix products  30.3 us (8%)
  blocking collectives  26.9 us (7%)
  between operations  15.6 us (4%)
  starting transfers between devices  8.4 us (2%)
    all_to_all x1, waiting for transfers between devices, on_device(): lax.all_to_all(shaped, SAME_CORE, split_axis=1, concat_axis=0, tiled=True)  141 us
    all_gather x1, waiting for transfers between devices, on_device(): mine = lax.all_gather(cotangent, SAME_CORE, axis=0, tiled=True)  82.7 us
    psum x3, blocking collectives, on_device(): gram = lax.psum(lax.psum(lax.psum(device_gram, 'core'), 'x'), 'fsdp')  26.9 us
    convert_element_type x1, other arithmetic, on_device(): (weight.astype(jnp.float32) - 0.002 * update).astype(jnp.bfloat16)  23.4 us
    dot_general x1, matrix products, on_device(): lax.dot_general(cols_partner, mine, dims, preferred_element_type=jnp.floa...  16.3 us
    dot_general x1, matrix products, on_device(): lax.dot_general(cols_own, mine, dims, preferred_element_type=jnp.float32)  14 us
    reduce_sum x1, other arithmetic, on_device(): jnp.sum(owned[i].astype(jnp.float32) * owned[j].astype(jnp.float32))  9.65 us
    another operation x3, other arithmetic, on_device(): jnp.stack([jnp.stack([pairs[min(i, j), max(i, j)] for j in range(groups)]...  9.15 us
  transfers between devices with their start and end apart: 3, of which 2 were waited for; matrix products, arithmetic and copies ran while one was open for 11% of the time, Pallas kernels for 0%

profile of v3, /device:TPU:0, one launch (start us, length us, event | category | flops | bytes accessed | tf_op | source)
XLA Modules:
  0.0 383.8 jit_solution(543166230797677116)
XLA Ops:
  7.2 0.7 all-gather.2.cloned.1.call-update
  7.9 6.1 %copy.13 = bf16[128,14336]{0,1:T(8,128)(2,1)} copy(bf16[128,14336]{1,0:T(8,128)(2,1)} %param.10) | data formatting | bytes 7340032 | tf_op args[0]
  13.9 4.2 %copy.14 = bf16[128,2,8,2,448]{0,4,3,2,1:T(8,128)(2,1)} copy(bf16[128,2,8,2,448]{0,4,2,3,1:T(8,128)(2,1)} %bitcast.65) | data formatting | bytes 7340032 | tf_op jit(solution)/shard_map/transpose | solution.py:19
  18.1 8.4 %all-to-all-start = ((bf16[128,16,896]{0,2,1:T(8,128)(2,1)}), bf16[128,16,896]{0,2,1:T(8,128)(2,1)}, u32[]{:S(2)}, u32[]{:S(2)}) async-start(bf16[128,16,896]{0,2,1:T(8,128)(2,1)} %bitcast.64), calls=%async_computation | async-start | bytes 7340032 | tf_op jit(solution)/shard_map/all_to_all | solution.py:21
  26.5 141.5 %all-to-all-done = bf16[128,16,896]{0,2,1:T(8,128)(2,1)} async-done(((bf16[128,16,896]{0,2,1:T(8,128)(2,1)}), bf16[128,16,896]{0,2,1:T(8,128)(2,1)}, u32[]{:S(2)}, u32[]{:S(2)}) %all-to-all-start) | async-done | bytes 3670048 | tf_op jit(solution)/shard_map/all_to_all | solution.py:21
  168.0 6.7 %copy.15 = bf16[16,128,1,896]{1,0,3,2:T(8,128)(2,1)} copy(bf16[16,128,1,896]{1,3,0,2:T(8,128)(2,1)} %bitcast.4) | data formatting | bytes 7340032 | tf_op jit(solution)/shard_map/all_to_all | solution.py:21
  174.6 6.5 %reshape.201 = bf16[2,1024,2,448]{1,0,3,2:T(2,128)(2,1)} reshape(bf16[16,128,1,896]{1,0,3,2:T(8,128)(2,1)} %copy.15) | data formatting | bytes 7340032 | tf_op jit(solution)/shard_map/reshape | solution.py:22
  181.2 5.8 %constant_dynamic-slice_fusion.1 = (bf16[2,1024,1,448]{1,0,3,2:T(2,128)(2,1)S(1)}, bf16[2,1024,1,448]{1,0,3,2:T(2,128)(2,1)}) fusion(bf16[2,1024,2,448]{1,0,3,2:T(2,128)(2,1)} %reshape.201, s32[]{:T(128)S(6)} %select_n.129, s32[]{:T(128)S(6)} %select_n.131), kind=kLoop, calls=%fused_computation.80 | loop fusion | bytes 7340040 | tf_op jit(solution)/shard_map/jit(_take) | solution.py:27
  187.0 82.7 %all-gather.2.cloned.1.call-done = bf16[2048,4096]{1,0:T(8,128)(2,1)} async-done(((bf16[128,4096]{1,0:T(8,128)(2,1)}), bf16[2048,4096]{1,0:T(8,128)(2,1)}) %all-gather.2.cloned.1.call-update) | async-done | bytes 16777232 | tf_op jit(solution)/shard_map/all_gather | solution.py:23
  269.7 16.3 %convolution_convert_fusion = bf16[2,448,4096]{2,1,0:T(8,128)(2,1)} fusion(bf16[2,1024,4096]{2,1,0:T(8,128)(2,1)} %bitcast.62, bf16[2,1024,1,448]{1,0,3,2:T(2,128)(2,1)} %get-tuple-element.34, pred[]{:T(512)S(6)} %and.79), kind=kOutput, calls=%fused_computation.35 | convolution fusion | flops 7520780288 | bytes 25952256 | tf_op jit(solution)/shard_map/dot_general | solution.py:28
  286.8 0.1 fusion.24
  286.9 14.0 %convolution_convert_fusion.1 = bf16[2,448,4096]{2,1,0:T(8,128)(2,1)S(1)} fusion(bf16[2,1024,4096]{2,1,0:T(8,128)(2,1)} %bitcast.63, bf16[2,1024,1,448]{1,0,3,2:T(2,128)(2,1)S(1)} %get-tuple-element.33, pred[]{:T(512)S(6)} %and.78), kind=kOutput, calls=%fused_computation.36 | convolution fusion | flops 7520780288 | bytes 25952256 | tf_op jit(solution)/shard_map/dot_general | solution.py:32
  301.0 9.7 %fusion.8 = (f32[]{:T(128)}, f32[]{:T(128)}, f32[]{:T(128)}, f32[]{:T(128)}, f32[]{:T(128)}, /*index=5*/f32[]{:T(128)}, f32[]{:T(128)}, f32[]{:T(128)}, f32[]{:T(128)}, f32[]{:T(128)}) fusion(bf16[2,448,4096]{2,1,0:T(8,128)(2,1)} %collective-permute-done, bf16[2,448,4096]{2,1,0:T(8,128)(2,1)S(1)} %convolution_convert_fusion.1), kind=kLoop, calls=%fused_computation.26 | loop fusion | flops 44040188 | bytes 14680104 | tf_op jit(solution)/shard_map/reduce_sum | solution.py:43
  310.6 4.6 %maximum_bitcast_fusion = (f32[1,4]{1,0:T(1,128)S(1)}, f32[1,4]{1,0:T(1,128)S(1)}) fusion(f32[1]{0:T(128)} %bitcast.11, f32[1]{0:T(128)} %bitcast.10, f32[1]{0:T(128)} %bitcast.8, f32[1]{0:T(128)} %bitcast.7, f32[1]{0:T(128)} %bitcast.15, f32[1]{0:T(128)} %bitcast.14, f32[1]{0:T(128)} %bitcast.13), kind=kLoop, calls=%fused_computation.73 | loop fusion | flops 24 | bytes 60 | tf_op jit(solution)/shard_map/stack | solution.py:46
  315.2 4.5 %maximum_bitcast_fusion.2 = (f32[1,4]{1,0:T(1,128)S(1)}, f32[1,4]{1,0:T(1,128)S(1)}) fusion(f32[1]{0:T(128)} %bitcast.18, f32[1]{0:T(128)} %bitcast.17, f32[1]{0:T(128)} %bitcast.14, f32[1]{0:T(128)} %bitcast.10, f32[1]{0:T(128)} %bitcast.20, f32[1]{0:T(128)} %bitcast.15, f32[1]{0:T(128)} %bitcast.11), kind=kLoop, calls=%fused_computation.75 | loop fusion | flops 24 | bytes 60 | tf_op jit(solution)/shard_map/stack | solution.py:46
  319.8 0.6 gather_fusion
  320.3 0.1 broadcast_select_fusion
  320.4 0.1 copy.18
  320.5 0.6 gather_fusion.1
  321.1 2.6 psum.21
  323.8 4.9 %psum.22 = f32[4,4]{0,1:T(4,128)S(1)} all-reduce(f32[4,4]{0,1:T(4,128)S(1)} %psum.21), channel_id=1, replica_groups=mesh['x'=2,'core'=2,'fsdp'=8] {'x'}, use_global_device_ids=true, to_apply=%region_11.13 | all-reduce | flops 16 | bytes 128 | tf_op jit(solution)/shard_map/psum | solution.py:50
  328.7 19.4 %psum.23 = f32[4,4]{0,1:T(4,128)S(1)} all-reduce(f32[4,4]{0,1:T(4,128)S(1)} %psum.22), channel_id=1, replica_groups=mesh['x'=2,'core'=2,'fsdp'=8] {'fsdp'}, use_global_device_ids=true, to_apply=%region_12.14 | all-reduce | flops 16 | bytes 128 | tf_op jit(solution)/shard_map/psum | solution.py:50
  348.1 0.6 select_reduce_fusion.2
  349.4 0.1 select_reduce_fusion.1
  349.5 0.6 fusion.28
  350.1 1.3 fusion.32
  351.4 0.6 broadcast_divide_fusion
  352.1 0.1 select_reduce_fusion
  352.1 0.6 gather_fusion.2
  352.8 0.1 and_select_fusion.4
  352.9 0.7 fusion.33
  353.5 23.4 %subtract_convert_fusion = (bf16[448,4096]{1,0:T(8,128)(2,1)}, f32[448,4096]{1,0:T(8,128)}, f32[448,4096]{1,0:T(8,128)}) fusion(bf16[448,4096]{1,0:T(8,128)(2,1)} %param.12, f32[]{:T(128)} %bitcast.33, f32[]{:T(128)} %bitcast.32, bf16[2,448,4096]{2,1,0:T(8,128)(2,1)} %collective-permute-done, f32[]{:T(128)} %bitcast.30, f32[]{:T(128)} %bitcast.29, ...), kind=kLoop, calls=%fused_computation.33 | loop fusion | flops 47710208 | bytes 51380248 | tf_op jit(solution)/shard_map/convert_element_type | solution.py:68
  (20 shorter events, 0.2 us)
Async XLA Ops:
  7.2 262.6 %all-gather.2.cloned.1.call-start = ((), (), s32[]{:S(2)}) async-start(), calls=%async_computation.1 | async-start | bytes 17825792 | tf_op jit(solution)/shard_map/all_gather | solution.py:23
  18.1 149.9 %all-to-all-start = ((bf16[128,16,896]{0,2,1:T(8,128)(2,1)}), bf16[128,16,896]{0,2,1:T(8,128)(2,1)}, u32[]{:S(2)}, u32[]{:S(2)}) async-start(bf16[128,16,896]{0,2,1:T(8,128)(2,1)} %bitcast.64), calls=%async_computation | async-start | bytes 7340032 | tf_op jit(solution)/shard_map/all_to_all | solution.py:21
  286.0 15.0 %collective-permute-start = (bf16[2,448,4096]{2,1,0:T(8,128)(2,1)}, bf16[2,448,4096]{2,1,0:T(8,128)(2,1)}, u32[]{:S(2)}, u32[]{:S(2)}) collective-permute-start(bf16[2,448,4096]{2,1,0:T(8,128)(2,1)} %convolution_convert_fusion), channel_id=1, source_target_pairs={{0,8},{8,0},{1,9},{9,1},{2,10},{10,2},{3,11},{11,3},{4,12},{12,4},... | collective-permute-start | bytes 22020104 | tf_op jit(solution)/shard_map/ppermute | solution.py:31
  300.9 9.7 %copy-start = (bf16[2,448,4096]{2,1,0:T(8,128)(2,1)}, bf16[2,448,4096]{2,1,0:T(8,128)(2,1)S(1)}, u32[]{:S(2)}) copy-start(bf16[2,448,4096]{2,1,0:T(8,128)(2,1)S(1)} %convolution_convert_fusion.1) | copy-start | bytes 22020100
  300.9 48.5 %copy-start.2 = (s32[4]{0:T(128)S(1)}, s32[4]{0:T(128)}, u32[]{:S(2)}) copy-start(s32[4]{0:T(128)} %param.16) | copy-start | bytes 52
  301.0 48.6 %copy-start.1 = (f32[4]{0:T(128)S(1)}, f32[4]{0:T(128)}, u32[]{:S(2)}) copy-start(f32[4]{0:T(128)} %param.15) | copy-start | bytes 52
  352.0 24.9 %copy-start.3 = (f32[4]{0:T(128)}, f32[4]{0:T(128)S(1)}, u32[]{:S(2)}) copy-start(f32[4]{0:T(128)S(1)} %broadcast_divide_fusion) | copy-start | bytes 52
Sparse Core Ops, SparseCore 0:
  10.8 258.8 all-gather.1

commit v4 on v3

--- a/solution.py
+++ b/solution.py
@@ -35,18 +35,19 @@
     owned = jnp.concatenate([g_own, received])
     half = jnp.arange(chips_x, dtype=jnp.int32) * 2
     order = jnp.concatenate([half + core, half + 1 - core])
-    ids = jnp.arange(groups, dtype=jnp.int32)
-    pos = jnp.where(ids % 2 == core, ids // 2, chips_x + ids // 2)
     pairs = {}
     for i in range(groups):
         for j in range(i, groups):
             pairs[i, j] = jnp.sum(
                 owned[i].astype(jnp.float32) * owned[j].astype(jnp.float32)
             )
-    local_gram = jnp.stack(
-        [jnp.stack([pairs[min(i, j), max(i, j)] for j in range(groups)]) for i in range(groups)]
-    )
-    device_gram = jnp.take(jnp.take(local_gram, pos, axis=0), pos, axis=1)
+    ids_i = jnp.arange(groups, dtype=jnp.int32)[:, None]
+    ids_j = jnp.arange(groups, dtype=jnp.int32)[None, :]
+    device_gram = jnp.zeros((groups, groups), jnp.float32)
+    for (i, j), value in pairs.items():
+        gi, gj = order[i], order[j]
+        hit = ((ids_i == gi) & (ids_j == gj)) | ((ids_i == gj) & (ids_j == gi))
+        device_gram = device_gram + jnp.where(hit, value, 0.0)
     gram = lax.psum(lax.psum(lax.psum(device_gram, "core"), "x"), "fsdp")
     score = jnp.sum(gram, axis=1) * (groups / jnp.trace(gram))
     onehot = (domain_ids[:, None] == jnp.arange(groups, dtype=jnp.int32)[None, :]).astype(

time: 385 us -> 384 us (level)
    another operation x3 -> x0, other arithmetic: 9.15 us -> none  [on_device(): jnp.stack([jnp.stack([pairs[min(i, j), max(i, j)] for j in range(groups)]...]
    add x0 -> x1, other arithmetic: none -> 6.48 us  [on_device(): device_gram = device_gram + jnp.where(hit, value, 0.0)]
  transfers between devices with their start and end apart: 3 -> 3, of which waited for: 2 -> 2; matrix products, arithmetic and copies ran while one was open for 11% -> 12% of each run, Pallas kernels for 0% -> 0%
where the time goes in v4:
time: 384 us
  waiting for transfers between devices  225 us (59%)
  other arithmetic  45.7 us (12%)
  local copies, waits for them, and re-layouts  31.7 us (8%)
  matrix products  30.3 us (8%)
  blocking collectives  27 us (7%)
  between operations  15.6 us (4%)
  starting transfers between devices  8.4 us (2%)
    all_to_all x1, waiting for transfers between devices, on_device(): lax.all_to_all(shaped, SAME_CORE, split_axis=1, concat_axis=0, tiled=True)  141 us
    all_gather x1, waiting for transfers between devices, on_device(): mine = lax.all_gather(cotangent, SAME_CORE, axis=0, tiled=True)  82.7 us
    psum x3, blocking collectives, on_device(): gram = lax.psum(lax.psum(lax.psum(device_gram, 'core'), 'x'), 'fsdp')  27 us
    convert_element_type x1, other arithmetic, on_device(): (weight.astype(jnp.float32) - 0.002 * update).astype(jnp.bfloat16)  23.4 us
    dot_general x1, matrix products, on_device(): lax.dot_general(cols_partner, mine, dims, preferred_element_type=jnp.floa...  16.3 us
    dot_general x1, matrix products, on_device(): lax.dot_general(cols_own, mine, dims, preferred_element_type=jnp.float32)  14 us
    reduce_sum x1, other arithmetic, on_device(): jnp.sum(owned[i].astype(jnp.float32) * owned[j].astype(jnp.float32))  9.65 us
    all_to_all x1, starting transfers between devices, on_device(): lax.all_to_all(shaped, SAME_CORE, split_axis=1, concat_axis=0, tiled=True)  8.36 us
  transfers between devices with their start and end apart: 3, of which 2 were waited for; matrix products, arithmetic and copies ran while one was open for 12% of the time, Pallas kernels for 0%

profile of v4, /device:TPU:0, one launch (start us, length us, event | category | flops | bytes accessed | tf_op | source)
XLA Modules:
  0.0 383.6 jit_solution(14965175849700125393)
XLA Ops:
  7.2 0.7 all-gather.2.cloned.1.call-update
  7.9 6.1 %copy.17 = bf16[128,14336]{0,1:T(8,128)(2,1)} copy(bf16[128,14336]{1,0:T(8,128)(2,1)} %param.10) | data formatting | bytes 7340032 | tf_op args[0]
  13.9 4.2 %copy.18 = bf16[128,2,8,2,448]{0,4,3,2,1:T(8,128)(2,1)} copy(bf16[128,2,8,2,448]{0,4,2,3,1:T(8,128)(2,1)} %bitcast.47) | data formatting | bytes 7340032 | tf_op jit(solution)/shard_map/transpose | solution.py:19
  18.1 8.4 %all-to-all-start = ((bf16[128,16,896]{0,2,1:T(8,128)(2,1)}), bf16[128,16,896]{0,2,1:T(8,128)(2,1)}, u32[]{:S(2)}, u32[]{:S(2)}) async-start(bf16[128,16,896]{0,2,1:T(8,128)(2,1)} %bitcast.46), calls=%async_computation | async-start | bytes 7340032 | tf_op jit(solution)/shard_map/all_to_all | solution.py:21
  26.5 141.5 %all-to-all-done = bf16[128,16,896]{0,2,1:T(8,128)(2,1)} async-done(((bf16[128,16,896]{0,2,1:T(8,128)(2,1)}), bf16[128,16,896]{0,2,1:T(8,128)(2,1)}, u32[]{:S(2)}, u32[]{:S(2)}) %all-to-all-start) | async-done | bytes 3670048 | tf_op jit(solution)/shard_map/all_to_all | solution.py:21
  168.0 6.7 %copy.19 = bf16[16,128,1,896]{1,0,3,2:T(8,128)(2,1)} copy(bf16[16,128,1,896]{1,3,0,2:T(8,128)(2,1)} %bitcast.5) | data formatting | bytes 7340032 | tf_op jit(solution)/shard_map/all_to_all | solution.py:21
  174.6 6.5 %reshape.169 = bf16[2,1024,2,448]{1,0,3,2:T(2,128)(2,1)} reshape(bf16[16,128,1,896]{1,0,3,2:T(8,128)(2,1)} %copy.19) | data formatting | bytes 7340032 | tf_op jit(solution)/shard_map/reshape | solution.py:22
  181.2 5.8 %constant_dynamic-slice_fusion.1 = (bf16[2,1024,1,448]{1,0,3,2:T(2,128)(2,1)S(1)}, bf16[2,1024,1,448]{1,0,3,2:T(2,128)(2,1)}) fusion(bf16[2,1024,2,448]{1,0,3,2:T(2,128)(2,1)} %reshape.169, s32[]{:T(128)S(6)} %select_n.83, s32[]{:T(128)S(6)} %select_n.85), kind=kLoop, calls=%fused_computation.61 | loop fusion | bytes 7340040 | tf_op jit(solution)/shard_map/jit(_take) | solution.py:27
  187.0 82.7 %all-gather.2.cloned.1.call-done = bf16[2048,4096]{1,0:T(8,128)(2,1)} async-done(((bf16[128,4096]{1,0:T(8,128)(2,1)}), bf16[2048,4096]{1,0:T(8,128)(2,1)}) %all-gather.2.cloned.1.call-update) | async-done | bytes 16777232 | tf_op jit(solution)/shard_map/all_gather | solution.py:23
  269.7 16.3 %convolution_convert_fusion = bf16[2,448,4096]{2,1,0:T(8,128)(2,1)} fusion(bf16[2,1024,4096]{2,1,0:T(8,128)(2,1)} %bitcast.44, bf16[2,1024,1,448]{1,0,3,2:T(2,128)(2,1)} %get-tuple-element.34, pred[]{:T(512)S(6)} %and.87), kind=kOutput, calls=%fused_computation.33 | convolution fusion | flops 7520780288 | bytes 25952256 | tf_op jit(solution)/shard_map/dot_general | solution.py:28
  286.8 0.6 fusion.34
  287.3 0.6 iota_compare_fusion.3
  288.0 0.7 iota_compare_fusion.2
  288.7 0.6 fusion.33
  289.2 0.6 iota_compare_fusion.5
  289.9 0.7 iota_compare_fusion.4
  290.7 14.0 %convolution_convert_fusion.1 = bf16[2,448,4096]{2,1,0:T(8,128)(2,1)S(1)} fusion(bf16[2,1024,4096]{2,1,0:T(8,128)(2,1)} %bitcast.45, bf16[2,1024,1,448]{1,0,3,2:T(2,128)(2,1)S(1)} %get-tuple-element.33, pred[]{:T(512)S(6)} %and.86), kind=kOutput, calls=%fused_computation.34 | convolution fusion | flops 7520780288 | bytes 25952256 | tf_op jit(solution)/shard_map/dot_general | solution.py:32
  304.7 9.7 %fusion.8 = (f32[]{:T(128)}, f32[]{:T(128)}, f32[]{:T(128)}, f32[]{:T(128)}, f32[]{:T(128)}, /*index=5*/f32[]{:T(128)}, f32[]{:T(128)}, f32[]{:T(128)}, f32[]{:T(128)}, f32[]{:T(128)}) fusion(bf16[2,448,4096]{2,1,0:T(8,128)(2,1)} %collective-permute-done, bf16[2,448,4096]{2,1,0:T(8,128)(2,1)S(1)} %convolution_convert_fusion.1), kind=kLoop, calls=%fused_computation.24 | loop fusion | flops 44040188 | bytes 14680104 | tf_op jit(solution)/shard_map/reduce_sum | solution.py:41
  314.4 6.5 %select_add_fusion = f32[4,4]{1,0:T(4,128)S(1)} fusion(f32[]{:T(128)} %get-tuple-element.22, f32[]{:T(128)} %get-tuple-element.23, f32[]{:T(128)} %get-tuple-element.21, f32[]{:T(128)} %get-tuple-element.18, f32[]{:T(128)} %get-tuple-element.17, f32[]{:T(128)} %get-tuple-element.25, f32[]{:T(128)} %get-tuple-element.19, f32[]{:T(128)} %get-tuple-element.16, ...), kind=kLoop, calls=%fused_computation.50 | loop fusion | flops 720 | bytes 120 | tf_op jit(solution)/shard_map/add | solution.py:50
  320.9 2.6 psum.21
  323.5 4.9 %psum.22 = f32[4,4]{1,0:T(4,128)S(1)} all-reduce(f32[4,4]{1,0:T(4,128)S(1)} %psum.21), channel_id=1, replica_groups=mesh['x'=2,'core'=2,'fsdp'=8] {'x'}, use_global_device_ids=true, to_apply=%region_11.13 | all-reduce | flops 16 | bytes 128 | tf_op jit(solution)/shard_map/psum | solution.py:51
  328.4 19.4 %psum.23 = f32[4,4]{1,0:T(4,128)S(1)} all-reduce(f32[4,4]{1,0:T(4,128)S(1)} %psum.22), channel_id=1, replica_groups=mesh['x'=2,'core'=2,'fsdp'=8] {'fsdp'}, use_global_device_ids=true, to_apply=%region_12.14 | all-reduce | flops 16 | bytes 128 | tf_op jit(solution)/shard_map/psum | solution.py:51
  347.8 0.7 select_reduce_fusion.2
  349.2 0.1 select_reduce_fusion.1
  349.3 0.6 fusion.27
  349.9 1.3 fusion.31
  351.1 0.6 broadcast_divide_fusion
  351.8 0.2 select_reduce_fusion
  352.0 0.6 gather_fusion
  352.6 0.1 and_select_fusion
  352.7 0.7 fusion.32
  353.4 23.4 %subtract_convert_fusion = (bf16[448,4096]{1,0:T(8,128)(2,1)}, f32[448,4096]{1,0:T(8,128)}, f32[448,4096]{1,0:T(8,128)}) fusion(bf16[448,4096]{1,0:T(8,128)(2,1)} %param.12, f32[]{:T(128)} %bitcast.21, f32[]{:T(128)} %bitcast.20, bf16[2,448,4096]{2,1,0:T(8,128)(2,1)} %collective-permute-done, f32[]{:T(128)} %bitcast.18, f32[]{:T(128)} %bitcast.17, ...), kind=kLoop, calls=%fused_computation.31 | loop fusion | flops 47710208 | bytes 51380248 | tf_op jit(solution)/shard_map/convert_element_type | solution.py:69
  (16 shorter events, 0.2 us)
Async XLA Ops:
  7.2 262.6 %all-gather.2.cloned.1.call-start = ((), (), s32[]{:S(2)}) async-start(), calls=%async_computation.1 | async-start | bytes 17825792 | tf_op jit(solution)/shard_map/all_gather | solution.py:23
  18.1 149.9 %all-to-all-start = ((bf16[128,16,896]{0,2,1:T(8,128)(2,1)}), bf16[128,16,896]{0,2,1:T(8,128)(2,1)}, u32[]{:S(2)}, u32[]{:S(2)}) async-start(bf16[128,16,896]{0,2,1:T(8,128)(2,1)} %bitcast.46), calls=%async_computation | async-start | bytes 7340032 | tf_op jit(solution)/shard_map/all_to_all | solution.py:21
  286.0 18.7 %collective-permute-start = (bf16[2,448,4096]{2,1,0:T(8,128)(2,1)}, bf16[2,448,4096]{2,1,0:T(8,128)(2,1)}, u32[]{:S(2)}, u32[]{:S(2)}) collective-permute-start(bf16[2,448,4096]{2,1,0:T(8,128)(2,1)} %convolution_convert_fusion), channel_id=1, source_target_pairs={{0,8},{8,0},{1,9},{9,1},{2,10},{10,2},{3,11},{11,3},{4,12},{12,4},... | collective-permute-start | bytes 22020104 | tf_op jit(solution)/shard_map/ppermute | solution.py:31
  304.7 9.7 %copy-start = (bf16[2,448,4096]{2,1,0:T(8,128)(2,1)}, bf16[2,448,4096]{2,1,0:T(8,128)(2,1)S(1)}, u32[]{:S(2)}) copy-start(bf16[2,448,4096]{2,1,0:T(8,128)(2,1)S(1)} %convolution_convert_fusion.1) | copy-start | bytes 22020100
  304.7 44.5 %copy-start.2 = (s32[4]{0:T(128)S(1)}, s32[4]{0:T(128)}, u32[]{:S(2)}) copy-start(s32[4]{0:T(128)} %param.16) | copy-start | bytes 52
  304.7 44.6 %copy-start.1 = (f32[4]{0:T(128)S(1)}, f32[4]{0:T(128)}, u32[]{:S(2)}) copy-start(f32[4]{0:T(128)} %param.15) | copy-start | bytes 52
  351.8 25.0 %copy-start.3 = (f32[4]{0:T(128)}, f32[4]{0:T(128)S(1)}, u32[]{:S(2)}) copy-start(f32[4]{0:T(128)S(1)} %broadcast_divide_fusion) | copy-start | bytes 52
Sparse Core Ops, SparseCore 0:
  10.8 258.8 all-gather.1

commit v5 on v4

--- a/solution.py
+++ b/solution.py
@@ -3,13 +3,13 @@
 from jax import lax
 from jax.sharding import Mesh, PartitionSpec as P
 
-FLAT = ("x", "core", "fsdp")
-SAME_CORE = ("x", "fsdp")
+FLAT = ("x", "core", "fsdp", "pair")
+SAME_CORE = ("x", "fsdp", "pair")
 
 
 def on_device(acts, cotangent, weight, moment, second, log_weights, domain_ids, step_count):
     chips_x = lax.axis_size("x")
-    members = lax.axis_size("fsdp")
+    members = lax.axis_size("fsdp") * lax.axis_size("pair")
     groups = chips_x * 2
     tok_rows = acts.shape[0]
     group_tok = members * tok_rows
@@ -35,20 +35,24 @@
     owned = jnp.concatenate([g_own, received])
     half = jnp.arange(chips_x, dtype=jnp.int32) * 2
     order = jnp.concatenate([half + core, half + 1 - core])
-    pairs = {}
-    for i in range(groups):
-        for j in range(i, groups):
-            pairs[i, j] = jnp.sum(
-                owned[i].astype(jnp.float32) * owned[j].astype(jnp.float32)
-            )
+    keys = [(i, j) for i in range(groups) for j in range(i, groups)]
+    partial = jnp.stack(
+        [
+            jnp.sum(owned[i].astype(jnp.float32) * owned[j].astype(jnp.float32), axis=0)
+            for i, j in keys
+        ]
+    )
+    sums = jnp.sum(partial, axis=1)
     ids_i = jnp.arange(groups, dtype=jnp.int32)[:, None]
     ids_j = jnp.arange(groups, dtype=jnp.int32)[None, :]
     device_gram = jnp.zeros((groups, groups), jnp.float32)
-    for (i, j), value in pairs.items():
+    for n, (i, j) in enumerate(keys):
         gi, gj = order[i], order[j]
         hit = ((ids_i == gi) & (ids_j == gj)) | ((ids_i == gj) & (ids_j == gi))
-        device_gram = device_gram + jnp.where(hit, value, 0.0)
-    gram = lax.psum(lax.psum(lax.psum(device_gram, "core"), "x"), "fsdp")
+        device_gram = device_gram + jnp.where(hit, sums[n], 0.0)
+    gram = device_gram
+    for axis in ("core", "pair", "x", "fsdp"):
+        gram = lax.psum(gram, axis)
     score = jnp.sum(gram, axis=1) * (groups / jnp.trace(gram))
     onehot = (domain_ids[:, None] == jnp.arange(groups, dtype=jnp.int32)[None, :]).astype(
         jnp.float32
@@ -72,7 +76,7 @@
 
 def solution(mesh):
     chips = mesh.shape["dom"] // 2
-    flat = Mesh(mesh.devices.reshape(chips, 2, mesh.shape["fsdp"]), FLAT)
+    flat = Mesh(mesh.devices.reshape(chips, 2, mesh.shape["fsdp"] // 2, 2), FLAT)
     row = P(FLAT, None)
     return jax.shard_map(
         on_device,

time: 384 us -> 380 us (0.990)
  blocking collectives: 27 us -> 22.2 us
    psum x3 -> x4, blocking collectives: 27 us -> 22.2 us  [on_device(): gram = lax.psum(gram, axis)]
    reduce_sum x1 -> x2, other arithmetic: 9.65 us -> 9.35 us  [the longest x1 9.2 us: on_device(): jnp.sum(owned[i].astype(jnp.float32) * owned[j].astype(jnp.float32), axis=0)]
where the time goes in v5:
time: 380 us
  waiting for transfers between devices  225 us (59%)
  other arithmetic  45.5 us (12%)
  local copies, waits for them, and re-layouts  32.7 us (9%)
  matrix products  30.3 us (8%)
  blocking collectives  22.2 us (6%)
  between operations  15.6 us (4%)
  starting transfers between devices  8.4 us (2%)
    all_to_all x1, waiting for transfers between devices, on_device(): lax.all_to_all(shaped, SAME_CORE, split_axis=1, concat_axis=0, tiled=True)  141 us
    all_gather x1, waiting for transfers between devices, on_device(): mine = lax.all_gather(cotangent, SAME_CORE, axis=0, tiled=True)  82.7 us
    convert_element_type x1, other arithmetic, on_device(): (weight.astype(jnp.float32) - 0.002 * update).astype(jnp.bfloat16)  23.5 us
    psum x4, blocking collectives, on_device(): gram = lax.psum(gram, axis)  22.2 us
    dot_general x1, matrix products, on_device(): lax.dot_general(cols_partner, mine, dims, preferred_element_type=jnp.floa...  16.3 us
    dot_general x1, matrix products, on_device(): lax.dot_general(cols_own, mine, dims, preferred_element_type=jnp.float32)  14 us
    reduce_sum x1, other arithmetic, on_device(): jnp.sum(owned[i].astype(jnp.float32) * owned[j].astype(jnp.float32), axis=0)  9.2 us
    all_to_all x1, starting transfers between devices, on_device(): lax.all_to_all(shaped, SAME_CORE, split_axis=1, concat_axis=0, tiled=True)  8.36 us
  transfers between devices with their start and end apart: 3, of which 2 were waited for; matrix products, arithmetic and copies ran while one was open for 12% of the time, Pallas kernels for 0%

profile of v5, /device:TPU:0, one launch (start us, length us, event | category | flops | bytes accessed | tf_op | source)
XLA Modules:
  0.0 379.6 jit_solution(16266559170539779139)
XLA Ops:
  7.2 0.7 all-gather.2.cloned.1.call-update
  7.9 6.1 %copy.17 = bf16[128,14336]{0,1:T(8,128)(2,1)} copy(bf16[128,14336]{1,0:T(8,128)(2,1)} %param.10) | data formatting | bytes 7340032 | tf_op args[0]
  13.9 4.2 %copy.18 = bf16[128,2,8,2,448]{0,4,3,2,1:T(8,128)(2,1)} copy(bf16[128,2,8,2,448]{0,4,2,3,1:T(8,128)(2,1)} %bitcast.67) | data formatting | bytes 7340032 | tf_op jit(solution)/shard_map/transpose | solution.py:19
  18.1 8.4 %all-to-all-start = ((bf16[128,16,896]{0,2,1:T(8,128)(2,1)}), bf16[128,16,896]{0,2,1:T(8,128)(2,1)}, u32[]{:S(2)}, u32[]{:S(2)}) async-start(bf16[128,16,896]{0,2,1:T(8,128)(2,1)} %bitcast.66), calls=%async_computation | async-start | bytes 7340032 | tf_op jit(solution)/shard_map/all_to_all | solution.py:21
  26.5 141.5 %all-to-all-done = bf16[128,16,896]{0,2,1:T(8,128)(2,1)} async-done(((bf16[128,16,896]{0,2,1:T(8,128)(2,1)}), bf16[128,16,896]{0,2,1:T(8,128)(2,1)}, u32[]{:S(2)}, u32[]{:S(2)}) %all-to-all-start) | async-done | bytes 3670048 | tf_op jit(solution)/shard_map/all_to_all | solution.py:21
  168.0 6.7 %copy.19 = bf16[16,128,1,896]{1,0,3,2:T(8,128)(2,1)} copy(bf16[16,128,1,896]{1,3,0,2:T(8,128)(2,1)} %bitcast.5) | data formatting | bytes 7340032 | tf_op jit(solution)/shard_map/all_to_all | solution.py:21
  174.6 6.5 %reshape.169 = bf16[2,1024,2,448]{1,0,3,2:T(2,128)(2,1)} reshape(bf16[16,128,1,896]{1,0,3,2:T(8,128)(2,1)} %copy.19) | data formatting | bytes 7340032 | tf_op jit(solution)/shard_map/reshape | solution.py:22
  181.2 5.8 %constant_dynamic-slice_fusion.1 = (bf16[2,1024,1,448]{1,0,3,2:T(2,128)(2,1)S(1)}, bf16[2,1024,1,448]{1,0,3,2:T(2,128)(2,1)}) fusion(bf16[2,1024,2,448]{1,0,3,2:T(2,128)(2,1)} %reshape.169, s32[]{:T(128)S(6)} %select_n.83, s32[]{:T(128)S(6)} %select_n.85), kind=kLoop, calls=%fused_computation.61 | loop fusion | bytes 7340040 | tf_op jit(solution)/shard_map/jit(_take) | solution.py:27
  187.0 82.7 %all-gather.2.cloned.1.call-done = bf16[2048,4096]{1,0:T(8,128)(2,1)} async-done(((bf16[128,4096]{1,0:T(8,128)(2,1)}), bf16[2048,4096]{1,0:T(8,128)(2,1)}) %all-gather.2.cloned.1.call-update) | async-done | bytes 16777232 | tf_op jit(solution)/shard_map/all_gather | solution.py:23
  269.7 16.3 %convolution_convert_fusion = bf16[2,448,4096]{2,1,0:T(8,128)(2,1)} fusion(bf16[2,1024,4096]{2,1,0:T(8,128)(2,1)} %bitcast.64, bf16[2,1024,1,448]{1,0,3,2:T(2,128)(2,1)} %get-tuple-element.38, pred[]{:T(512)S(6)} %and.87), kind=kOutput, calls=%fused_computation.33 | convolution fusion | flops 7520780288 | bytes 25952256 | tf_op jit(solution)/shard_map/dot_general | solution.py:28
  286.8 0.6 fusion.34
  287.3 0.6 iota_compare_fusion.3
  288.0 0.7 iota_compare_fusion.2
  288.7 0.6 fusion.33
  289.2 0.6 iota_compare_fusion.5
  289.9 0.7 iota_compare_fusion.4
  290.7 14.0 %convolution_convert_fusion.1 = bf16[2,448,4096]{2,1,0:T(8,128)(2,1)S(1)} fusion(bf16[2,1024,4096]{2,1,0:T(8,128)(2,1)} %bitcast.65, bf16[2,1024,1,448]{1,0,3,2:T(2,128)(2,1)S(1)} %get-tuple-element.37, pred[]{:T(512)S(6)} %and.86), kind=kOutput, calls=%fused_computation.34 | convolution fusion | flops 7520780288 | bytes 25952256 | tf_op jit(solution)/shard_map/dot_general | solution.py:32
  304.7 9.2 %fusion.14 = (f32[4096]{0:T(1024)S(1)}, f32[4096]{0:T(1024)S(1)}, f32[4096]{0:T(1024)S(1)}, f32[4096]{0:T(1024)S(1)}, f32[4096]{0:T(1024)S(1)}, /*index=5*/f32[4...) fusion(bf16[2,448,4096]{2,1,0:T(8,128)(2,1)} %collective-permute-done, ...), kind=kLoop, calls=%fused_computation.30 | loop fusion | flops 43999232 | bytes 14843904 | tf_op jit(solution)/shard_map/reduce_sum | solution.py:41
  313.9 0.3 stack.43
  314.4 0.7 fusion.35
  315.0 6.5 %select_add_fusion = f32[4,4]{1,0:T(4,128)S(1)} fusion(f32[]{:T(128)} %bitcast.31, f32[]{:T(128)} %bitcast.30, f32[]{:T(128)} %bitcast.29, f32[]{:T(128)} %bitcast.28, f32[]{:T(128)} %bitcast.27, f32[]{:T(128)} %bitcast.26, f32[]{:T(128)} %bitcast.25, f32[]{:T(128)} %bitcast.23, f32[]{:T(128)} %bitcast.21, f32[]{:T(128)} %bitcast.19, ...), kind=kLoop, calls=%fused_computation.50 | loop fusion | flops 720 | bytes 120 | tf_op jit(solution)/shard_map/add | solution.py:52
  321.5 2.6 psum.28
  324.2 4.9 %psum.29 = f32[4,4]{1,0:T(4,128)S(1)} all-reduce(f32[4,4]{1,0:T(4,128)S(1)} %psum.28), channel_id=1, replica_groups=mesh['x'=2,'core'=2,'fsdp'=4,'pair'=2] {'pair'}, use_global_device_ids=true, to_apply=%region_12.14 | all-reduce | flops 16 | bytes 128 | tf_op jit(solution)/shard_map/psum | solution.py:55
  329.1 4.9 %psum.30 = f32[4,4]{1,0:T(4,128)S(1)} all-reduce(f32[4,4]{1,0:T(4,128)S(1)} %psum.29), channel_id=1, replica_groups=mesh['x'=2,'core'=2,'fsdp'=4,'pair'=2] {'x'}, use_global_device_ids=true, to_apply=%region_13.15 | all-reduce | flops 16 | bytes 128 | tf_op jit(solution)/shard_map/psum | solution.py:55
  334.0 9.7 %psum.31 = f32[4,4]{1,0:T(4,128)S(1)} all-reduce(f32[4,4]{1,0:T(4,128)S(1)} %psum.30), channel_id=1, replica_groups=mesh['x'=2,'core'=2,'fsdp'=4,'pair'=2] {'fsdp'}, use_global_device_ids=true, to_apply=%region_14.16 | all-reduce | flops 16 | bytes 128 | tf_op jit(solution)/shard_map/psum | solution.py:55
  343.7 0.7 select_reduce_fusion.2
  345.2 0.6 fusion.27
  345.8 1.3 fusion.31
  347.0 0.6 broadcast_divide_fusion
  347.9 0.6 gather_fusion
  348.6 0.7 fusion.32
  349.3 23.5 %subtract_convert_fusion = (bf16[448,4096]{1,0:T(8,128)(2,1)}, f32[448,4096]{1,0:T(8,128)}, f32[448,4096]{1,0:T(8,128)}) fusion(bf16[448,4096]{1,0:T(8,128)(2,1)} %param.12, f32[]{:T(128)} %bitcast.41, f32[]{:T(128)} %bitcast.40, bf16[2,448,4096]{2,1,0:T(8,128)(2,1)} %collective-permute-done, f32[]{:T(128)} %bitcast.38, f32[]{:T(128)} %bitcast.37, ...), kind=kLoop, calls=%fused_computation.31 | loop fusion | flops 47710208 | bytes 51380248 | tf_op jit(solution)/shard_map/convert_element_type | solution.py:73
  (20 shorter events, 0.7 us)
Async XLA Ops:
  7.2 262.6 %all-gather.2.cloned.1.call-start = ((), (), s32[]{:S(2)}) async-start(), calls=%async_computation.1 | async-start | bytes 17825792 | tf_op jit(solution)/shard_map/all_gather | solution.py:23
  18.1 149.9 %all-to-all-start = ((bf16[128,16,896]{0,2,1:T(8,128)(2,1)}), bf16[128,16,896]{0,2,1:T(8,128)(2,1)}, u32[]{:S(2)}, u32[]{:S(2)}) async-start(bf16[128,16,896]{0,2,1:T(8,128)(2,1)} %bitcast.66), calls=%async_computation | async-start | bytes 7340032 | tf_op jit(solution)/shard_map/all_to_all | solution.py:21
  286.0 18.7 %collective-permute-start = (bf16[2,448,4096]{2,1,0:T(8,128)(2,1)}, bf16[2,448,4096]{2,1,0:T(8,128)(2,1)}, u32[]{:S(2)}, u32[]{:S(2)}) collective-permute-start(bf16[2,448,4096]{2,1,0:T(8,128)(2,1)} %convolution_convert_fusion), channel_id=1, source_target_pairs={{0,8},{8,0},{1,9},{9,1},{2,10},{10,2},{3,11},{11,3},{4,12},{12,4},... | collective-permute-start | bytes 22020104 | tf_op jit(solution)/shard_map/ppermute | solution.py:31
  304.7 9.3 %copy-start = (bf16[2,448,4096]{2,1,0:T(8,128)(2,1)}, bf16[2,448,4096]{2,1,0:T(8,128)(2,1)S(1)}, u32[]{:S(2)}) copy-start(bf16[2,448,4096]{2,1,0:T(8,128)(2,1)S(1)} %convolution_convert_fusion.1) | copy-start | bytes 22020100
  304.7 40.4 %copy-start.2 = (s32[4]{0:T(128)S(1)}, s32[4]{0:T(128)}, u32[]{:S(2)}) copy-start(s32[4]{0:T(128)} %param.16) | copy-start | bytes 52
  304.7 40.5 %copy-start.1 = (f32[4]{0:T(128)S(1)}, f32[4]{0:T(128)}, u32[]{:S(2)}) copy-start(f32[4]{0:T(128)} %param.15) | copy-start | bytes 52
  347.7 25.0 %copy-start.3 = (f32[4]{0:T(128)}, f32[4]{0:T(128)S(1)}, u32[]{:S(2)}) copy-start(f32[4]{0:T(128)S(1)} %broadcast_divide_fusion) | copy-start | bytes 52
Sparse Core Ops, SparseCore 0:
  10.8 258.8 all-gather.1

commit v6 on v5

--- a/solution.py
+++ b/solution.py
@@ -43,13 +43,11 @@
         ]
     )
     sums = jnp.sum(partial, axis=1)
-    ids_i = jnp.arange(groups, dtype=jnp.int32)[:, None]
-    ids_j = jnp.arange(groups, dtype=jnp.int32)[None, :]
-    device_gram = jnp.zeros((groups, groups), jnp.float32)
-    for n, (i, j) in enumerate(keys):
-        gi, gj = order[i], order[j]
-        hit = ((ids_i == gi) & (ids_j == gj)) | ((ids_i == gj) & (ids_j == gi))
-        device_gram = device_gram + jnp.where(hit, sums[n], 0.0)
+    ids = jnp.arange(groups, dtype=jnp.int32)
+    pos = jnp.where(ids % 2 == core, ids // 2, chips_x + ids // 2)
+    lo = jnp.minimum(pos[:, None], pos[None, :])
+    hi = jnp.maximum(pos[:, None], pos[None, :])
+    device_gram = jnp.take(sums, lo * groups - lo * (lo - 1) // 2 + (hi - lo))
     gram = device_gram
     for axis in ("core", "pair", "x", "fsdp"):
         gram = lax.psum(gram, axis)

time: 380 us -> 370 us (0.974)
  other arithmetic: 45.5 us -> 36.6 us
    add x1 -> x0, other arithmetic: 6.48 us -> none  [on_device(): device_gram = device_gram + jnp.where(hit, sums[n], 0.0)]
where the time goes in v6:
time: 370 us
  waiting for transfers between devices  225 us (61%)
  other arithmetic  36.6 us (10%)
  local copies, waits for them, and re-layouts  31.6 us (9%)
  matrix products  30.3 us (8%)
  blocking collectives  22.2 us (6%)
  between operations  15.6 us (4%)
  starting transfers between devices  8.4 us (2%)
    all_to_all x1, waiting for transfers between devices, on_device(): lax.all_to_all(shaped, SAME_CORE, split_axis=1, concat_axis=0, tiled=True)  141 us
    all_gather x1, waiting for transfers between devices, on_device(): mine = lax.all_gather(cotangent, SAME_CORE, axis=0, tiled=True)  82.7 us
    convert_element_type x1, other arithmetic, on_device(): (weight.astype(jnp.float32) - 0.002 * update).astype(jnp.bfloat16)  23.5 us
    psum x4, blocking collectives, on_device(): gram = lax.psum(gram, axis)  22.2 us
    dot_general x1, matrix products, on_device(): lax.dot_general(cols_partner, mine, dims, preferred_element_type=jnp.floa...  16.3 us
    dot_general x1, matrix products, on_device(): lax.dot_general(cols_own, mine, dims, preferred_element_type=jnp.float32)  14 us
    reduce_sum x1, other arithmetic, on_device(): jnp.sum(owned[i].astype(jnp.float32) * owned[j].astype(jnp.float32), axis=0)  9.2 us
    all_to_all x1, starting transfers between devices, on_device(): lax.all_to_all(shaped, SAME_CORE, split_axis=1, concat_axis=0, tiled=True)  8.36 us
  transfers between devices with their start and end apart: 3, of which 2 were waited for; matrix products, arithmetic and copies ran while one was open for 12% of the time, Pallas kernels for 0%

profile of v6, /device:TPU:0, one launch (start us, length us, event | category | flops | bytes accessed | tf_op | source)
XLA Modules:
  0.0 369.7 jit_solution(9663655147516641778)
XLA Ops:
  7.2 0.7 all-gather.2.cloned.1.call-update
  7.9 6.1 %copy.17 = bf16[128,14336]{0,1:T(8,128)(2,1)} copy(bf16[128,14336]{1,0:T(8,128)(2,1)} %param.10) | data formatting | bytes 7340032 | tf_op args[0]
  13.9 4.2 %copy.18 = bf16[128,2,8,2,448]{0,4,3,2,1:T(8,128)(2,1)} copy(bf16[128,2,8,2,448]{0,4,2,3,1:T(8,128)(2,1)} %bitcast.55) | data formatting | bytes 7340032 | tf_op jit(solution)/shard_map/transpose | solution.py:19
  18.1 8.4 %all-to-all-start = ((bf16[128,16,896]{0,2,1:T(8,128)(2,1)}), bf16[128,16,896]{0,2,1:T(8,128)(2,1)}, u32[]{:S(2)}, u32[]{:S(2)}) async-start(bf16[128,16,896]{0,2,1:T(8,128)(2,1)} %bitcast.54), calls=%async_computation | async-start | bytes 7340032 | tf_op jit(solution)/shard_map/all_to_all | solution.py:21
  26.5 141.5 %all-to-all-done = bf16[128,16,896]{0,2,1:T(8,128)(2,1)} async-done(((bf16[128,16,896]{0,2,1:T(8,128)(2,1)}), bf16[128,16,896]{0,2,1:T(8,128)(2,1)}, u32[]{:S(2)}, u32[]{:S(2)}) %all-to-all-start) | async-done | bytes 3670048 | tf_op jit(solution)/shard_map/all_to_all | solution.py:21
  168.0 6.7 %copy.19 = bf16[16,128,1,896]{1,0,3,2:T(8,128)(2,1)} copy(bf16[16,128,1,896]{1,3,0,2:T(8,128)(2,1)} %bitcast.4) | data formatting | bytes 7340032 | tf_op jit(solution)/shard_map/all_to_all | solution.py:21
  174.6 6.5 %reshape.369 = bf16[2,1024,2,448]{1,0,3,2:T(2,128)(2,1)} reshape(bf16[16,128,1,896]{1,0,3,2:T(8,128)(2,1)} %copy.19) | data formatting | bytes 7340032 | tf_op jit(solution)/shard_map/reshape | solution.py:22
  181.2 5.8 %constant_dynamic-slice_fusion.1 = (bf16[2,1024,1,448]{1,0,3,2:T(2,128)(2,1)S(1)}, bf16[2,1024,1,448]{1,0,3,2:T(2,128)(2,1)}) fusion(bf16[2,1024,2,448]{1,0,3,2:T(2,128)(2,1)} %reshape.369, s32[]{:T(128)S(6)} %select_n.125, s32[]{:T(128)S(6)} %select_n.127), kind=kLoop, calls=%fused_computation.96 | loop fusion | bytes 7340040 | tf_op jit(solution)/shard_map/jit(_take) | solution.py:27
  187.0 82.7 %all-gather.2.cloned.1.call-done = bf16[2048,4096]{1,0:T(8,128)(2,1)} async-done(((bf16[128,4096]{1,0:T(8,128)(2,1)}), bf16[2048,4096]{1,0:T(8,128)(2,1)}) %all-gather.2.cloned.1.call-update) | async-done | bytes 16777232 | tf_op jit(solution)/shard_map/all_gather | solution.py:23
  269.7 16.3 %convolution_convert_fusion = bf16[2,448,4096]{2,1,0:T(8,128)(2,1)} fusion(bf16[2,1024,4096]{2,1,0:T(8,128)(2,1)} %bitcast.52, bf16[2,1024,1,448]{1,0,3,2:T(2,128)(2,1)} %get-tuple-element.38, pred[]{:T(512)S(6)} %and.97), kind=kOutput, calls=%fused_computation.34 | convolution fusion | flops 7520780288 | bytes 25952256 | tf_op jit(solution)/shard_map/dot_general | solution.py:28
  286.0 0.1 compare_select_fusion
  286.1 0.1 reshape.431
  287.0 14.0 %convolution_convert_fusion.1 = bf16[2,448,4096]{2,1,0:T(8,128)(2,1)S(1)} fusion(bf16[2,1024,4096]{2,1,0:T(8,128)(2,1)} %bitcast.53, bf16[2,1024,1,448]{1,0,3,2:T(2,128)(2,1)S(1)} %get-tuple-element.37, pred[]{:T(512)S(6)} %and.96), kind=kOutput, calls=%fused_computation.35 | convolution fusion | flops 7520780288 | bytes 25952256 | tf_op jit(solution)/shard_map/dot_general | solution.py:32
  301.1 9.2 %fusion.14 = (f32[4096]{0:T(1024)S(1)}, f32[4096]{0:T(1024)S(1)}, f32[4096]{0:T(1024)S(1)}, f32[4096]{0:T(1024)S(1)}, f32[4096]{0:T(1024)S(1)}, /*index=5*/f32[4...) fusion(bf16[2,448,4096]{2,1,0:T(8,128)(2,1)} %collective-permute-done, ...), kind=kLoop, calls=%fused_computation.31 | loop fusion | flops 43999232 | bytes 14843904 | tf_op jit(solution)/shard_map/reduce_sum | solution.py:41
  310.4 0.3 stack.43
  310.6 0.1 reduce_sum.155
  310.8 0.7 gather_fusion
  311.4 0.1 reshape.430
  311.5 0.1 and_select_fusion
  311.6 2.6 psum.28
  314.2 4.9 %psum.29 = f32[4,4]{1,0:T(4,128)S(1)} all-reduce(f32[4,4]{1,0:T(4,128)S(1)} %psum.28), channel_id=1, replica_groups=mesh['x'=2,'core'=2,'fsdp'=4,'pair'=2] {'pair'}, use_global_device_ids=true, to_apply=%region_12.14 | all-reduce | flops 16 | bytes 128 | tf_op jit(solution)/shard_map/psum | solution.py:53
  319.2 4.9 %psum.30 = f32[4,4]{1,0:T(4,128)S(1)} all-reduce(f32[4,4]{1,0:T(4,128)S(1)} %psum.29), channel_id=1, replica_groups=mesh['x'=2,'core'=2,'fsdp'=4,'pair'=2] {'x'}, use_global_device_ids=true, to_apply=%region_13.15 | all-reduce | flops 16 | bytes 128 | tf_op jit(solution)/shard_map/psum | solution.py:53
  324.1 9.7 %psum.31 = f32[4,4]{1,0:T(4,128)S(1)} all-reduce(f32[4,4]{1,0:T(4,128)S(1)} %psum.30), channel_id=1, replica_groups=mesh['x'=2,'core'=2,'fsdp'=4,'pair'=2] {'fsdp'}, use_global_device_ids=true, to_apply=%region_14.16 | all-reduce | flops 16 | bytes 128 | tf_op jit(solution)/shard_map/psum | solution.py:53
  333.8 0.7 select_reduce_fusion.2
  335.2 0.1 select_reduce_fusion.1
  335.3 0.6 fusion.41
  335.9 1.3 fusion.45
  337.1 0.6 broadcast_divide_fusion
  337.8 0.2 select_reduce_fusion
  338.0 0.6 gather_fusion.1
  338.7 0.7 fusion.46
  339.3 23.5 %subtract_convert_fusion = (bf16[448,4096]{1,0:T(8,128)(2,1)}, f32[448,4096]{1,0:T(8,128)}, f32[448,4096]{1,0:T(8,128)}) fusion(bf16[448,4096]{1,0:T(8,128)(2,1)} %param.12, f32[]{:T(128)} %bitcast.27, f32[]{:T(128)} %bitcast.26, bf16[2,448,4096]{2,1,0:T(8,128)(2,1)} %collective-permute-done, f32[]{:T(128)} %bitcast.24, f32[]{:T(128)} %bitcast.23, ...), kind=kLoop, calls=%fused_computation.32 | loop fusion | flops 47710208 | bytes 51380248 | tf_op jit(solution)/shard_map/convert_element_type | solution.py:71
  (19 shorter events, 0.3 us)
Async XLA Ops:
  7.2 262.6 %all-gather.2.cloned.1.call-start = ((), (), s32[]{:S(2)}) async-start(), calls=%async_computation.1 | async-start | bytes 17825792 | tf_op jit(solution)/shard_map/all_gather | solution.py:23
  18.1 149.9 %all-to-all-start = ((bf16[128,16,896]{0,2,1:T(8,128)(2,1)}), bf16[128,16,896]{0,2,1:T(8,128)(2,1)}, u32[]{:S(2)}, u32[]{:S(2)}) async-start(bf16[128,16,896]{0,2,1:T(8,128)(2,1)} %bitcast.54), calls=%async_computation | async-start | bytes 7340032 | tf_op jit(solution)/shard_map/all_to_all | solution.py:21
  286.0 15.1 %collective-permute-start = (bf16[2,448,4096]{2,1,0:T(8,128)(2,1)}, bf16[2,448,4096]{2,1,0:T(8,128)(2,1)}, u32[]{:S(2)}, u32[]{:S(2)}) collective-permute-start(bf16[2,448,4096]{2,1,0:T(8,128)(2,1)} %convolution_convert_fusion), channel_id=1, source_target_pairs={{0,8},{8,0},{1,9},{9,1},{2,10},{10,2},{3,11},{11,3},{4,12},{12,4},... | collective-permute-start | bytes 22020104 | tf_op jit(solution)/shard_map/ppermute | solution.py:31
  301.1 9.3 %copy-start = (bf16[2,448,4096]{2,1,0:T(8,128)(2,1)}, bf16[2,448,4096]{2,1,0:T(8,128)(2,1)S(1)}, u32[]{:S(2)}) copy-start(bf16[2,448,4096]{2,1,0:T(8,128)(2,1)S(1)} %convolution_convert_fusion.1) | copy-start | bytes 22020100
  301.1 34.1 %copy-start.2 = (s32[4]{0:T(128)S(1)}, s32[4]{0:T(128)}, u32[]{:S(2)}) copy-start(s32[4]{0:T(128)} %param.16) | copy-start | bytes 52
  301.1 34.1 %copy-start.1 = (f32[4]{0:T(128)S(1)}, f32[4]{0:T(128)}, u32[]{:S(2)}) copy-start(f32[4]{0:T(128)} %param.15) | copy-start | bytes 52
  337.8 25.0 %copy-start.3 = (f32[4]{0:T(128)}, f32[4]{0:T(128)S(1)}, u32[]{:S(2)}) copy-start(f32[4]{0:T(128)S(1)} %broadcast_divide_fusion) | copy-start | bytes 52
Sparse Core Ops, SparseCore 0:
  10.8 258.8 all-gather.1

commit v7 on v6

--- a/solution.py
+++ b/solution.py
@@ -49,8 +49,8 @@
     hi = jnp.maximum(pos[:, None], pos[None, :])
     device_gram = jnp.take(sums, lo * groups - lo * (lo - 1) // 2 + (hi - lo))
     gram = device_gram
-    for axis in ("core", "pair", "x", "fsdp"):
-        gram = lax.psum(gram, axis)
+    for axes in (("core",), ("pair", "x"), ("fsdp",)):
+        gram = lax.psum(gram, axes)
     score = jnp.sum(gram, axis=1) * (groups / jnp.trace(gram))
     onehot = (domain_ids[:, None] == jnp.arange(groups, dtype=jnp.int32)[None, :]).astype(
         jnp.float32

time: 370 us -> 369 us (level)
    psum x4 -> x3, blocking collectives: 22.2 us -> 21.3 us  [on_device(): gram = lax.psum(gram, axes)]
where the time goes in v7:
time: 369 us
  waiting for transfers between devices  225 us (61%)
  other arithmetic  36.5 us (10%)
  local copies, waits for them, and re-layouts  31.7 us (9%)
  matrix products  30.3 us (8%)
  blocking collectives  21.3 us (6%)
  between operations  15.6 us (4%)
  starting transfers between devices  8.4 us (2%)
    all_to_all x1, waiting for transfers between devices, on_device(): lax.all_to_all(shaped, SAME_CORE, split_axis=1, concat_axis=0, tiled=True)  141 us
    all_gather x1, waiting for transfers between devices, on_device(): mine = lax.all_gather(cotangent, SAME_CORE, axis=0, tiled=True)  82.7 us
    convert_element_type x1, other arithmetic, on_device(): (weight.astype(jnp.float32) - 0.002 * update).astype(jnp.bfloat16)  23.4 us
    psum x3, blocking collectives, on_device(): gram = lax.psum(gram, axes)  21.3 us
    dot_general x1, matrix products, on_device(): lax.dot_general(cols_partner, mine, dims, preferred_element_type=jnp.floa...  16.3 us
    dot_general x1, matrix products, on_device(): lax.dot_general(cols_own, mine, dims, preferred_element_type=jnp.float32)  14 us
    reduce_sum x1, other arithmetic, on_device(): jnp.sum(owned[i].astype(jnp.float32) * owned[j].astype(jnp.float32), axis=0)  9.2 us
    all_to_all x1, starting transfers between devices, on_device(): lax.all_to_all(shaped, SAME_CORE, split_axis=1, concat_axis=0, tiled=True)  8.36 us
  transfers between devices with their start and end apart: 3, of which 2 were waited for; matrix products, arithmetic and copies ran while one was open for 12% of the time, Pallas kernels for 0%

profile of v7, /device:TPU:0, one launch (start us, length us, event | category | flops | bytes accessed | tf_op | source)
XLA Modules:
  0.0 368.7 jit_solution(15167391554965113082)
XLA Ops:
  7.2 0.7 all-gather.2.cloned.1.call-update
  7.9 6.1 %copy.17 = bf16[128,14336]{0,1:T(8,128)(2,1)} copy(bf16[128,14336]{1,0:T(8,128)(2,1)} %param.10) | data formatting | bytes 7340032 | tf_op args[0]
  13.9 4.2 %copy.18 = bf16[128,2,8,2,448]{0,4,3,2,1:T(8,128)(2,1)} copy(bf16[128,2,8,2,448]{0,4,2,3,1:T(8,128)(2,1)} %bitcast.55) | data formatting | bytes 7340032 | tf_op jit(solution)/shard_map/transpose | solution.py:19
  18.1 8.4 %all-to-all-start = ((bf16[128,16,896]{0,2,1:T(8,128)(2,1)}), bf16[128,16,896]{0,2,1:T(8,128)(2,1)}, u32[]{:S(2)}, u32[]{:S(2)}) async-start(bf16[128,16,896]{0,2,1:T(8,128)(2,1)} %bitcast.54), calls=%async_computation | async-start | bytes 7340032 | tf_op jit(solution)/shard_map/all_to_all | solution.py:21
  26.5 141.5 %all-to-all-done = bf16[128,16,896]{0,2,1:T(8,128)(2,1)} async-done(((bf16[128,16,896]{0,2,1:T(8,128)(2,1)}), bf16[128,16,896]{0,2,1:T(8,128)(2,1)}, u32[]{:S(2)}, u32[]{:S(2)}) %all-to-all-start) | async-done | bytes 3670048 | tf_op jit(solution)/shard_map/all_to_all | solution.py:21
  168.0 6.7 %copy.19 = bf16[16,128,1,896]{1,0,3,2:T(8,128)(2,1)} copy(bf16[16,128,1,896]{1,3,0,2:T(8,128)(2,1)} %bitcast.4) | data formatting | bytes 7340032 | tf_op jit(solution)/shard_map/all_to_all | solution.py:21
  174.6 6.5 %reshape.369 = bf16[2,1024,2,448]{1,0,3,2:T(2,128)(2,1)} reshape(bf16[16,128,1,896]{1,0,3,2:T(8,128)(2,1)} %copy.19) | data formatting | bytes 7340032 | tf_op jit(solution)/shard_map/reshape | solution.py:22
  181.2 5.8 %constant_dynamic-slice_fusion.1 = (bf16[2,1024,1,448]{1,0,3,2:T(2,128)(2,1)S(1)}, bf16[2,1024,1,448]{1,0,3,2:T(2,128)(2,1)}) fusion(bf16[2,1024,2,448]{1,0,3,2:T(2,128)(2,1)} %reshape.369, s32[]{:T(128)S(6)} %select_n.125, s32[]{:T(128)S(6)} %select_n.127), kind=kLoop, calls=%fused_computation.96 | loop fusion | bytes 7340040 | tf_op jit(solution)/shard_map/jit(_take) | solution.py:27
  187.0 82.7 %all-gather.2.cloned.1.call-done = bf16[2048,4096]{1,0:T(8,128)(2,1)} async-done(((bf16[128,4096]{1,0:T(8,128)(2,1)}), bf16[2048,4096]{1,0:T(8,128)(2,1)}) %all-gather.2.cloned.1.call-update) | async-done | bytes 16777232 | tf_op jit(solution)/shard_map/all_gather | solution.py:23
  269.7 16.3 %convolution_convert_fusion = bf16[2,448,4096]{2,1,0:T(8,128)(2,1)} fusion(bf16[2,1024,4096]{2,1,0:T(8,128)(2,1)} %bitcast.52, bf16[2,1024,1,448]{1,0,3,2:T(2,128)(2,1)} %get-tuple-element.38, pred[]{:T(512)S(6)} %and.97), kind=kOutput, calls=%fused_computation.34 | convolution fusion | flops 7520780288 | bytes 25952256 | tf_op jit(solution)/shard_map/dot_general | solution.py:28
  286.0 0.1 compare_select_fusion
  286.1 0.1 reshape.431
  287.0 14.0 %convolution_convert_fusion.1 = bf16[2,448,4096]{2,1,0:T(8,128)(2,1)S(1)} fusion(bf16[2,1024,4096]{2,1,0:T(8,128)(2,1)} %bitcast.53, bf16[2,1024,1,448]{1,0,3,2:T(2,128)(2,1)S(1)} %get-tuple-element.37, pred[]{:T(512)S(6)} %and.96), kind=kOutput, calls=%fused_computation.35 | convolution fusion | flops 7520780288 | bytes 25952256 | tf_op jit(solution)/shard_map/dot_general | solution.py:32
  301.1 9.2 %fusion.14 = (f32[4096]{0:T(1024)S(1)}, f32[4096]{0:T(1024)S(1)}, f32[4096]{0:T(1024)S(1)}, f32[4096]{0:T(1024)S(1)}, f32[4096]{0:T(1024)S(1)}, /*index=5*/f32[4...) fusion(bf16[2,448,4096]{2,1,0:T(8,128)(2,1)} %collective-permute-done, ...), kind=kLoop, calls=%fused_computation.31 | loop fusion | flops 43999232 | bytes 14843904 | tf_op jit(solution)/shard_map/reduce_sum | solution.py:41
  310.4 0.3 stack.43
  310.6 0.1 reduce_sum.155
  310.8 0.7 gather_fusion
  311.4 0.1 reshape.430
  311.5 0.1 and_select_fusion
  311.6 2.6 psum.21
  314.2 8.9 %psum.22 = f32[4,4]{1,0:T(4,128)S(1)} all-reduce(f32[4,4]{1,0:T(4,128)S(1)} %psum.21), channel_id=1, replica_groups=mesh['x'=2,'core'=2,'fsdp'=4,'pair'=2] {'pair','x'}, use_global_device_ids=true, to_apply=%region_12.14 | all-reduce | flops 16 | bytes 128 | tf_op jit(solution)/shard_map/psum | solution.py:53
  323.1 9.7 %psum.23 = f32[4,4]{1,0:T(4,128)S(1)} all-reduce(f32[4,4]{1,0:T(4,128)S(1)} %psum.22), channel_id=1, replica_groups=mesh['x'=2,'core'=2,'fsdp'=4,'pair'=2] {'fsdp'}, use_global_device_ids=true, to_apply=%region_13.15 | all-reduce | flops 16 | bytes 128 | tf_op jit(solution)/shard_map/psum | solution.py:53
  332.9 0.7 select_reduce_fusion.2
  334.3 0.1 select_reduce_fusion.1
  334.3 0.6 fusion.41
  334.9 1.3 fusion.45
  336.2 0.6 broadcast_divide_fusion
  336.9 0.2 select_reduce_fusion
  337.0 0.6 gather_fusion.1
  337.7 0.1 and_select_fusion.3
  337.8 0.7 fusion.46
  338.4 23.4 %subtract_convert_fusion = (bf16[448,4096]{1,0:T(8,128)(2,1)}, f32[448,4096]{1,0:T(8,128)}, f32[448,4096]{1,0:T(8,128)}) fusion(bf16[448,4096]{1,0:T(8,128)(2,1)} %param.12, f32[]{:T(128)} %bitcast.27, f32[]{:T(128)} %bitcast.26, bf16[2,448,4096]{2,1,0:T(8,128)(2,1)} %collective-permute-done, f32[]{:T(128)} %bitcast.24, f32[]{:T(128)} %bitcast.23, ...), kind=kLoop, calls=%fused_computation.32 | loop fusion | flops 47710208 | bytes 51380248 | tf_op jit(solution)/shard_map/convert_element_type | solution.py:71
  (18 shorter events, 0.2 us)
Async XLA Ops:
  7.2 262.6 %all-gather.2.cloned.1.call-start = ((), (), s32[]{:S(2)}) async-start(), calls=%async_computation.1 | async-start | bytes 17825792 | tf_op jit(solution)/shard_map/all_gather | solution.py:23
  18.1 149.9 %all-to-all-start = ((bf16[128,16,896]{0,2,1:T(8,128)(2,1)}), bf16[128,16,896]{0,2,1:T(8,128)(2,1)}, u32[]{:S(2)}, u32[]{:S(2)}) async-start(bf16[128,16,896]{0,2,1:T(8,128)(2,1)} %bitcast.54), calls=%async_computation | async-start | bytes 7340032 | tf_op jit(solution)/shard_map/all_to_all | solution.py:21
  286.0 15.1 %collective-permute-start = (bf16[2,448,4096]{2,1,0:T(8,128)(2,1)}, bf16[2,448,4096]{2,1,0:T(8,128)(2,1)}, u32[]{:S(2)}, u32[]{:S(2)}) collective-permute-start(bf16[2,448,4096]{2,1,0:T(8,128)(2,1)} %convolution_convert_fusion), channel_id=1, source_target_pairs={{0,8},{8,0},{1,9},{9,1},{2,10},{10,2},{3,11},{11,3},{4,12},{12,4},... | collective-permute-start | bytes 22020104 | tf_op jit(solution)/shard_map/ppermute | solution.py:31
  301.1 9.3 %copy-start = (bf16[2,448,4096]{2,1,0:T(8,128)(2,1)}, bf16[2,448,4096]{2,1,0:T(8,128)(2,1)S(1)}, u32[]{:S(2)}) copy-start(bf16[2,448,4096]{2,1,0:T(8,128)(2,1)S(1)} %convolution_convert_fusion.1) | copy-start | bytes 22020100
  301.1 33.1 %copy-start.2 = (s32[4]{0:T(128)S(1)}, s32[4]{0:T(128)}, u32[]{:S(2)}) copy-start(s32[4]{0:T(128)} %param.16) | copy-start | bytes 52
  301.1 33.2 %copy-start.1 = (f32[4]{0:T(128)S(1)}, f32[4]{0:T(128)}, u32[]{:S(2)}) copy-start(f32[4]{0:T(128)} %param.15) | copy-start | bytes 52
  336.9 25.0 %copy-start.3 = (f32[4]{0:T(128)}, f32[4]{0:T(128)S(1)}, u32[]{:S(2)}) copy-start(f32[4]{0:T(128)S(1)} %broadcast_divide_fusion) | copy-start | bytes 52
Sparse Core Ops, SparseCore 0:
  10.8 258.8 all-gather.1

commit v8 on v7

--- a/solution.py
+++ b/solution.py
@@ -1,10 +1,58 @@
 import jax
 import jax.numpy as jnp
 from jax import lax
+from jax.experimental import pallas as pl
+from jax.experimental.pallas import tpu as pltpu
 from jax.sharding import Mesh, PartitionSpec as P
 
 FLAT = ("x", "core", "fsdp", "pair")
 SAME_CORE = ("x", "fsdp", "pair")
+
+
+def adam_kernel(scal_ref, own_ref, recv_ref, m_ref, s_ref, w_ref, nw_ref, nm_ref, ns_ref):
+    half = own_ref.shape[0]
+    combined = scal_ref[0] * own_ref[0].astype(jnp.float32)
+    for k in range(1, half):
+        combined = combined + scal_ref[k] * own_ref[k].astype(jnp.float32)
+    for k in range(half):
+        combined = combined + scal_ref[half + k] * recv_ref[k].astype(jnp.float32)
+    fix_one = scal_ref[2 * half]
+    fix_two = scal_ref[2 * half + 1]
+    new_moment = 0.9 * m_ref[...] + 0.1 * combined
+    new_second = 0.95 * s_ref[...] + 0.05 * combined * combined
+    update = new_moment / fix_one / (jnp.sqrt(new_second / fix_two) + 1e-08)
+    nw_ref[...] = (w_ref[...].astype(jnp.float32) - 0.002 * update).astype(nw_ref.dtype)
+    nm_ref[...] = new_moment
+    ns_ref[...] = new_second
+
+
+def adam_update(scal, g_own, received, moment, second, weight):
+    half, rows, width = g_own.shape
+    tile = next(t for t in (64, 32, 16, rows) if rows % t == 0)
+    grad_spec = pl.BlockSpec((half, tile, width), lambda i: (0, i, 0))
+    row_spec = pl.BlockSpec((tile, width), lambda i: (i, 0))
+    elems = rows * width
+    return pl.pallas_call(
+        adam_kernel,
+        grid=(rows // tile,),
+        in_specs=[
+            pl.BlockSpec(memory_space=pltpu.SMEM),
+            grad_spec,
+            grad_spec,
+            row_spec,
+            row_spec,
+            row_spec,
+        ],
+        out_specs=[row_spec, row_spec, row_spec],
+        out_shape=[
+            jax.ShapeDtypeStruct((rows, width), weight.dtype),
+            jax.ShapeDtypeStruct((rows, width), jnp.float32),
+            jax.ShapeDtypeStruct((rows, width), jnp.float32),
+        ],
+        cost_estimate=pl.CostEstimate(
+            flops=20 * elems, transcendentals=2 * elems, bytes_accessed=elems * (4 * half + 20)
+        ),
+    )(scal, g_own, received, moment, second, weight)
 
 
 def on_device(acts, cotangent, weight, moment, second, log_weights, domain_ids, step_count):
@@ -59,16 +107,11 @@
     new_domain_weights = jax.nn.softmax(logits)
     group_w = jnp.sum(onehot * new_domain_weights[None, :], axis=1)
     local_w = jnp.take(group_w, order)
-    combined = jnp.zeros((own_rows, width), jnp.float32)
-    for group in range(groups):
-        combined = combined + local_w[group] * owned[group].astype(jnp.float32)
     steps_f = step_count[0].astype(jnp.float32)
-    new_moment = 0.9 * moment + 0.1 * combined
-    new_second = 0.95 * second + 0.05 * combined * combined
     fix_one = 1.0 - jnp.exp(steps_f * jnp.log(jnp.float32(0.9)))
     fix_two = 1.0 - jnp.exp(steps_f * jnp.log(jnp.float32(0.95)))
-    update = new_moment / fix_one / (jnp.sqrt(new_second / fix_two) + 1e-08)
-    new_weight = (weight.astype(jnp.float32) - 0.002 * update).astype(jnp.bfloat16)
+    scal = jnp.concatenate([local_w, jnp.stack([fix_one, fix_two])])
+    new_weight, new_moment, new_second = adam_update(scal, g_own, received, moment, second, weight)
     return (new_weight, new_moment, new_second, new_domain_weights)
 
 

time: 369 us -> 366 us (level)
  other arithmetic: 36.5 us -> 13.8 us
  Pallas kernels: 0 us -> 20.5 us
    convert_element_type x1 -> x0, other arithmetic: 23.4 us -> none  [on_device(): (weight.astype(jnp.float32) - 0.002 * update).astype(jnp.bfloat16)]
    pallas_call x0 -> x1, Pallas kernels: none -> 20.5 us  [adam_update(): pl.pallas_call(adam_kernel, grid=(rows // tile,), in_specs=[pl.BlockSpec(...]
where the time goes in v8:
time: 366 us
  waiting for transfers between devices  225 us (61%)
  local copies, waits for them, and re-layouts  31 us (8%)
  matrix products  30.3 us (8%)
  blocking collectives  21.3 us (6%)
  Pallas kernels  20.5 us (6%)
  between operations  15.6 us (4%)
  other arithmetic  13.8 us (4%)
  starting transfers between devices  8.4 us (2%)
    all_to_all x1, waiting for transfers between devices, on_device(): lax.all_to_all(shaped, SAME_CORE, split_axis=1, concat_axis=0, tiled=True)  141 us
    all_gather x1, waiting for transfers between devices, on_device(): mine = lax.all_gather(cotangent, SAME_CORE, axis=0, tiled=True)  82.7 us
    psum x3, blocking collectives, on_device(): gram = lax.psum(gram, axes)  21.3 us
    pallas_call x1, Pallas kernels, adam_update(): pl.pallas_call(adam_kernel, grid=(rows // tile,), in_specs=[pl.BlockSpec(...  20.5 us
    dot_general x1, matrix products, on_device(): lax.dot_general(cols_partner, mine, dims, preferred_element_type=jnp.floa...  16.3 us
    dot_general x1, matrix products, on_device(): lax.dot_general(cols_own, mine, dims, preferred_element_type=jnp.float32)  14 us
    reduce_sum x1, other arithmetic, on_device(): jnp.sum(owned[i].astype(jnp.float32) * owned[j].astype(jnp.float32), axis=0)  9.2 us
    all_to_all x1, starting transfers between devices, on_device(): lax.all_to_all(shaped, SAME_CORE, split_axis=1, concat_axis=0, tiled=True)  8.36 us
  transfers between devices with their start and end apart: 3, of which 2 were waited for; matrix products, arithmetic and copies ran while one was open for 12% of the time, Pallas kernels for 0%

profile of v8, /device:TPU:0, one launch (start us, length us, event | category | flops | bytes accessed | tf_op | source)
XLA Modules:
  0.0 365.8 jit_solution(6227359056680988947)
XLA Ops:
  7.2 0.7 all-gather.2.cloned.1.call-update
  7.9 6.1 %copy.17 = bf16[128,14336]{0,1:T(8,128)(2,1)} copy(bf16[128,14336]{1,0:T(8,128)(2,1)} %param.10) | data formatting | bytes 7340032 | tf_op args[0]
  13.9 4.2 %copy.18 = bf16[128,2,8,2,448]{0,4,3,2,1:T(8,128)(2,1)} copy(bf16[128,2,8,2,448]{0,4,2,3,1:T(8,128)(2,1)} %bitcast.41) | data formatting | bytes 7340032 | tf_op jit(solution)/shard_map/transpose | solution.py:67
  18.1 8.4 %all-to-all-start = ((bf16[128,16,896]{0,2,1:T(8,128)(2,1)}), bf16[128,16,896]{0,2,1:T(8,128)(2,1)}, u32[]{:S(2)}, u32[]{:S(2)}) async-start(bf16[128,16,896]{0,2,1:T(8,128)(2,1)} %bitcast.40), calls=%async_computation | async-start | bytes 7340032 | tf_op jit(solution)/shard_map/all_to_all | solution.py:69
  26.5 141.5 %all-to-all-done = bf16[128,16,896]{0,2,1:T(8,128)(2,1)} async-done(((bf16[128,16,896]{0,2,1:T(8,128)(2,1)}), bf16[128,16,896]{0,2,1:T(8,128)(2,1)}, u32[]{:S(2)}, u32[]{:S(2)}) %all-to-all-start) | async-done | bytes 3670048 | tf_op jit(solution)/shard_map/all_to_all | solution.py:69
  168.0 6.7 %copy.19 = bf16[16,128,1,896]{1,0,3,2:T(8,128)(2,1)} copy(bf16[16,128,1,896]{1,3,0,2:T(8,128)(2,1)} %bitcast.4) | data formatting | bytes 7340032 | tf_op jit(solution)/shard_map/all_to_all | solution.py:69
  174.6 6.5 %reshape.361 = bf16[2,1024,2,448]{1,0,3,2:T(2,128)(2,1)} reshape(bf16[16,128,1,896]{1,0,3,2:T(8,128)(2,1)} %copy.19) | data formatting | bytes 7340032 | tf_op jit(solution)/shard_map/reshape | solution.py:70
  181.2 5.8 %constant_dynamic-slice_fusion.1 = (bf16[2,1024,1,448]{1,0,3,2:T(2,128)(2,1)S(1)}, bf16[2,1024,1,448]{1,0,3,2:T(2,128)(2,1)}) fusion(bf16[2,1024,2,448]{1,0,3,2:T(2,128)(2,1)} %reshape.361, s32[]{:T(128)S(6)} %select_n.125, s32[]{:T(128)S(6)} %select_n.127), kind=kLoop, calls=%fused_computation.85 | loop fusion | bytes 7340040 | tf_op jit(solution)/shard_map/jit(_take) | solution.py:75
  187.0 82.7 %all-gather.2.cloned.1.call-done = bf16[2048,4096]{1,0:T(8,128)(2,1)} async-done(((bf16[128,4096]{1,0:T(8,128)(2,1)}), bf16[2048,4096]{1,0:T(8,128)(2,1)}) %all-gather.2.cloned.1.call-update) | async-done | bytes 16777232 | tf_op jit(solution)/shard_map/all_gather | solution.py:71
  269.7 16.3 %convolution_convert_fusion = bf16[2,448,4096]{2,1,0:T(8,128)(2,1)} fusion(bf16[2,1024,4096]{2,1,0:T(8,128)(2,1)} %bitcast.38, bf16[2,1024,1,448]{1,0,3,2:T(2,128)(2,1)} %get-tuple-element.41, pred[]{:T(512)S(6)} %and.97), kind=kOutput, calls=%fused_computation.22 | convolution fusion | flops 7520780288 | bytes 25952256 | tf_op jit(solution)/shard_map/dot_general | solution.py:76
  286.0 0.1 compare_select_fusion
  286.1 0.1 reshape.422
  287.0 14.0 %convolution_convert_fusion.1.own_ref = bf16[2,448,4096]{2,1,0:T(8,128)(2,1)S(1)} fusion(bf16[2,1024,4096]{2,1,0:T(8,128)(2,1)} %bitcast.39, bf16[2,1024,1,448]{1,0,3,2:T(2,128)(2,1)S(1)} %get-tuple-element.40, pred[]{:T(512)S(6)} %and.96), kind=kOutput, calls=%fused_computation.23 | convolution fusion | flops 7520780288 | bytes 25952256 | tf_op jit(solution)/shard_map/dot_general | solution.py:80
  301.1 9.2 %fusion.9 = (f32[4096]{0:T(1024)S(1)}, f32[4096]{0:T(1024)S(1)}, f32[4096]{0:T(1024)S(1)}, f32[4096]{0:T(1024)S(1)}, f32[4096]{0:T(1024)S(1)}, /*index=5*/f32[40...) fusion(bf16[2,448,4096]{2,1,0:T(8,128)(2,1)} %collective-permute-done.recv_ref, ...), kind=kLoop, calls=%fused_computation.21 | loop fusion | flops 43999232 | bytes 14843904 | tf_op jit(solution)/shard_map/reduce_sum | solution.py:89
  310.4 0.3 stack.45
  310.6 0.1 reduce_sum.155
  310.8 0.7 gather_fusion
  311.4 0.1 reshape.421
  311.5 0.1 and_select_fusion
  311.6 2.6 psum.21
  314.2 8.9 %psum.22 = f32[4,4]{1,0:T(4,128)S(1)} all-reduce(f32[4,4]{1,0:T(4,128)S(1)} %psum.21), channel_id=1, replica_groups=mesh['x'=2,'core'=2,'fsdp'=4,'pair'=2] {'pair','x'}, use_global_device_ids=true, to_apply=%region_12.14 | all-reduce | flops 16 | bytes 128 | tf_op jit(solution)/shard_map/psum | solution.py:101
  323.1 9.7 %psum.23 = f32[4,4]{1,0:T(4,128)S(1)} all-reduce(f32[4,4]{1,0:T(4,128)S(1)} %psum.22), channel_id=1, replica_groups=mesh['x'=2,'core'=2,'fsdp'=4,'pair'=2] {'fsdp'}, use_global_device_ids=true, to_apply=%region_13.15 | all-reduce | flops 16 | bytes 128 | tf_op jit(solution)/shard_map/psum | solution.py:101
  332.9 0.7 select_reduce_fusion.2
  334.3 0.1 select_reduce_fusion.1
  334.3 0.6 fusion.36
  334.9 1.3 fusion.39
  336.2 0.6 broadcast_divide_fusion
  336.9 0.2 select_reduce_fusion
  337.0 0.6 gather_fusion.1
  337.7 0.1 and_select_fusion.3
  337.8 0.7 pad_maximum_fusion.scal_ref
  338.4 20.5 %shard_map.111 = (bf16[448,4096]{1,0:T(8,128)(2,1)}, f32[448,4096]{1,0:T(8,128)}, f32[448,4096]{1,0:T(8,128)}) custom-call(f32[6]{0:T(128)} %pad_maximum_fusion.scal_ref, bf16[2,448,4096]{2,1,0:T(8,128)(2,1)} %copy-done, bf16[2,448,4096]{2,1,0:T(8,128)(2,1)} %collective-permute-done.recv_ref, f32[448,4096]{1,0:T(8,128)} %m_ref.1, f32[448,4096]{1,0:T(8,128)} %s_ref.1, ...), custom_call_target="tpu_custom_call" | custom-call | flops 36700160 | bytes 51380224 | tf_op jit(solution)/shard_map/pallas_call | solution.py:35
  (18 shorter events, 0.2 us)
Async XLA Ops:
  7.2 262.6 %all-gather.2.cloned.1.call-start = ((), (), s32[]{:S(2)}) async-start(), calls=%async_computation.1 | async-start | bytes 17825792 | tf_op jit(solution)/shard_map/all_gather | solution.py:71
  18.1 149.9 %all-to-all-start = ((bf16[128,16,896]{0,2,1:T(8,128)(2,1)}), bf16[128,16,896]{0,2,1:T(8,128)(2,1)}, u32[]{:S(2)}, u32[]{:S(2)}) async-start(bf16[128,16,896]{0,2,1:T(8,128)(2,1)} %bitcast.40), calls=%async_computation | async-start | bytes 7340032 | tf_op jit(solution)/shard_map/all_to_all | solution.py:69
  286.0 15.1 %collective-permute-start = (bf16[2,448,4096]{2,1,0:T(8,128)(2,1)}, bf16[2,448,4096]{2,1,0:T(8,128)(2,1)}, u32[]{:S(2)}, u32[]{:S(2)}) collective-permute-start(bf16[2,448,4096]{2,1,0:T(8,128)(2,1)} %convolution_convert_fusion), channel_id=1, source_target_pairs={{0,8},{8,0},{1,9},{9,1},{2,10},{10,2},{3,11},{11,3},{4,12},{12,4},... | collective-permute-start | bytes 22020104 | tf_op jit(solution)/shard_map/ppermute | solution.py:79
  301.1 9.3 %copy-start = (bf16[2,448,4096]{2,1,0:T(8,128)(2,1)}, bf16[2,448,4096]{2,1,0:T(8,128)(2,1)S(1)}, u32[]{:S(2)}) copy-start(bf16[2,448,4096]{2,1,0:T(8,128)(2,1)S(1)} %convolution_convert_fusion.1.own_ref) | copy-start | bytes 22020100
  301.1 33.1 %copy-start.2 = (s32[4]{0:T(128)S(1)}, s32[4]{0:T(128)}, u32[]{:S(2)}) copy-start(s32[4]{0:T(128)} %param.16) | copy-start | bytes 52
  301.1 33.2 %copy-start.1 = (f32[4]{0:T(128)S(1)}, f32[4]{0:T(128)}, u32[]{:S(2)}) copy-start(f32[4]{0:T(128)} %param.15) | copy-start | bytes 52
  336.9 22.1 %copy-start.3 = (f32[4]{0:T(128)}, f32[4]{0:T(128)S(1)}, u32[]{:S(2)}) copy-start(f32[4]{0:T(128)S(1)} %broadcast_divide_fusion) | copy-start | bytes 52
Sparse Core Ops, SparseCore 0:
  10.8 258.8 all-gather.1

commit v9 on v8

--- a/solution.py
+++ b/solution.py
@@ -28,7 +28,7 @@
 
 def adam_update(scal, g_own, received, moment, second, weight):
     half, rows, width = g_own.shape
-    tile = next(t for t in (64, 32, 16, rows) if rows % t == 0)
+    tile = next(t for t in (112, 64, 32, 16, rows) if rows % t == 0)
     grad_spec = pl.BlockSpec((half, tile, width), lambda i: (0, i, 0))
     row_spec = pl.BlockSpec((tile, width), lambda i: (i, 0))
     elems = rows * width

time: 366 us -> 364 us (level)
  no operation moved by 1% of the time
where the time goes in v9:
time: 364 us; the launch traced here: 363 us
  waiting for transfers between devices  225 us (62%)
  local copies, waits for them, and re-layouts  31 us (9%)
  matrix products  30.3 us (8%)
  blocking collectives  21.3 us (6%)
  Pallas kernels  18.1 us (5%)
  between operations  15.6 us (4%)
  other arithmetic  13.8 us (4%)
  starting transfers between devices  8.4 us (2%)
    all_to_all x1, waiting for transfers between devices, on_device(): lax.all_to_all(shaped, SAME_CORE, split_axis=1, concat_axis=0, tiled=True)  141 us
    all_gather x1, waiting for transfers between devices, on_device(): mine = lax.all_gather(cotangent, SAME_CORE, axis=0, tiled=True)  82.7 us
    psum x3, blocking collectives, on_device(): gram = lax.psum(gram, axes)  21.3 us
    pallas_call x1, Pallas kernels, adam_update(): pl.pallas_call(adam_kernel, grid=(rows // tile,), in_specs=[pl.BlockSpec(...  18.1 us
    dot_general x1, matrix products, on_device(): lax.dot_general(cols_partner, mine, dims, preferred_element_type=jnp.floa...  16.3 us
    dot_general x1, matrix products, on_device(): lax.dot_general(cols_own, mine, dims, preferred_element_type=jnp.float32)  14 us
    reduce_sum x1, other arithmetic, on_device(): jnp.sum(owned[i].astype(jnp.float32) * owned[j].astype(jnp.float32), axis=0)  9.2 us
    all_to_all x1, starting transfers between devices, on_device(): lax.all_to_all(shaped, SAME_CORE, split_axis=1, concat_axis=0, tiled=True)  8.36 us
  transfers between devices with their start and end apart: 3, of which 2 were waited for; matrix products, arithmetic and copies ran while one was open for 12% of the time, Pallas kernels for 0%

profile of v9, /device:TPU:0, one launch (start us, length us, event | category | flops | bytes accessed | tf_op | source)
XLA Modules:
  0.0 363.4 jit_solution(2603986568274071)
XLA Ops:
  7.2 0.7 all-gather.2.cloned.1.call-update
  7.9 6.1 %copy.17 = bf16[128,14336]{0,1:T(8,128)(2,1)} copy(bf16[128,14336]{1,0:T(8,128)(2,1)} %param.10) | data formatting | bytes 7340032 | tf_op args[0]
  13.9 4.2 %copy.18 = bf16[128,2,8,2,448]{0,4,3,2,1:T(8,128)(2,1)} copy(bf16[128,2,8,2,448]{0,4,2,3,1:T(8,128)(2,1)} %bitcast.41) | data formatting | bytes 7340032 | tf_op jit(solution)/shard_map/transpose | solution.py:67
  18.1 8.4 %all-to-all-start = ((bf16[128,16,896]{0,2,1:T(8,128)(2,1)}), bf16[128,16,896]{0,2,1:T(8,128)(2,1)}, u32[]{:S(2)}, u32[]{:S(2)}) async-start(bf16[128,16,896]{0,2,1:T(8,128)(2,1)} %bitcast.40), calls=%async_computation | async-start | bytes 7340032 | tf_op jit(solution)/shard_map/all_to_all | solution.py:69
  26.5 141.5 %all-to-all-done = bf16[128,16,896]{0,2,1:T(8,128)(2,1)} async-done(((bf16[128,16,896]{0,2,1:T(8,128)(2,1)}), bf16[128,16,896]{0,2,1:T(8,128)(2,1)}, u32[]{:S(2)}, u32[]{:S(2)}) %all-to-all-start) | async-done | bytes 3670048 | tf_op jit(solution)/shard_map/all_to_all | solution.py:69
  168.0 6.7 %copy.19 = bf16[16,128,1,896]{1,0,3,2:T(8,128)(2,1)} copy(bf16[16,128,1,896]{1,3,0,2:T(8,128)(2,1)} %bitcast.4) | data formatting | bytes 7340032 | tf_op jit(solution)/shard_map/all_to_all | solution.py:69
  174.6 6.5 %reshape.361 = bf16[2,1024,2,448]{1,0,3,2:T(2,128)(2,1)} reshape(bf16[16,128,1,896]{1,0,3,2:T(8,128)(2,1)} %copy.19) | data formatting | bytes 7340032 | tf_op jit(solution)/shard_map/reshape | solution.py:70
  181.2 5.8 %constant_dynamic-slice_fusion.1 = (bf16[2,1024,1,448]{1,0,3,2:T(2,128)(2,1)S(1)}, bf16[2,1024,1,448]{1,0,3,2:T(2,128)(2,1)}) fusion(bf16[2,1024,2,448]{1,0,3,2:T(2,128)(2,1)} %reshape.361, s32[]{:T(128)S(6)} %select_n.125, s32[]{:T(128)S(6)} %select_n.127), kind=kLoop, calls=%fused_computation.85 | loop fusion | bytes 7340040 | tf_op jit(solution)/shard_map/jit(_take) | solution.py:75
  187.0 82.7 %all-gather.2.cloned.1.call-done = bf16[2048,4096]{1,0:T(8,128)(2,1)} async-done(((bf16[128,4096]{1,0:T(8,128)(2,1)}), bf16[2048,4096]{1,0:T(8,128)(2,1)}) %all-gather.2.cloned.1.call-update) | async-done | bytes 16777232 | tf_op jit(solution)/shard_map/all_gather | solution.py:71
  269.7 16.3 %convolution_convert_fusion = bf16[2,448,4096]{2,1,0:T(8,128)(2,1)} fusion(bf16[2,1024,4096]{2,1,0:T(8,128)(2,1)} %bitcast.38, bf16[2,1024,1,448]{1,0,3,2:T(2,128)(2,1)} %get-tuple-element.41, pred[]{:T(512)S(6)} %and.97), kind=kOutput, calls=%fused_computation.22 | convolution fusion | flops 7520780288 | bytes 25952256 | tf_op jit(solution)/shard_map/dot_general | solution.py:76
  286.0 0.1 compare_select_fusion
  286.1 0.1 reshape.422
  287.0 14.0 %convolution_convert_fusion.1.own_ref = bf16[2,448,4096]{2,1,0:T(8,128)(2,1)S(1)} fusion(bf16[2,1024,4096]{2,1,0:T(8,128)(2,1)} %bitcast.39, bf16[2,1024,1,448]{1,0,3,2:T(2,128)(2,1)S(1)} %get-tuple-element.40, pred[]{:T(512)S(6)} %and.96), kind=kOutput, calls=%fused_computation.23 | convolution fusion | flops 7520780288 | bytes 25952256 | tf_op jit(solution)/shard_map/dot_general | solution.py:80
  301.1 9.2 %fusion.9 = (f32[4096]{0:T(1024)S(1)}, f32[4096]{0:T(1024)S(1)}, f32[4096]{0:T(1024)S(1)}, f32[4096]{0:T(1024)S(1)}, f32[4096]{0:T(1024)S(1)}, /*index=5*/f32[40...) fusion(bf16[2,448,4096]{2,1,0:T(8,128)(2,1)} %collective-permute-done.recv_ref, ...), kind=kLoop, calls=%fused_computation.21 | loop fusion | flops 43999232 | bytes 14843904 | tf_op jit(solution)/shard_map/reduce_sum | solution.py:89
  310.4 0.3 stack.45
  310.6 0.1 reduce_sum.155
  310.8 0.7 gather_fusion
  311.4 0.1 reshape.421
  311.5 0.1 and_select_fusion
  311.6 2.6 psum.21
  314.2 8.9 %psum.22 = f32[4,4]{1,0:T(4,128)S(1)} all-reduce(f32[4,4]{1,0:T(4,128)S(1)} %psum.21), channel_id=1, replica_groups=mesh['x'=2,'core'=2,'fsdp'=4,'pair'=2] {'pair','x'}, use_global_device_ids=true, to_apply=%region_12.14 | all-reduce | flops 16 | bytes 128 | tf_op jit(solution)/shard_map/psum | solution.py:101
  323.1 9.7 %psum.23 = f32[4,4]{1,0:T(4,128)S(1)} all-reduce(f32[4,4]{1,0:T(4,128)S(1)} %psum.22), channel_id=1, replica_groups=mesh['x'=2,'core'=2,'fsdp'=4,'pair'=2] {'fsdp'}, use_global_device_ids=true, to_apply=%region_13.15 | all-reduce | flops 16 | bytes 128 | tf_op jit(solution)/shard_map/psum | solution.py:101
  332.9 0.7 select_reduce_fusion.2
  334.3 0.1 select_reduce_fusion.1
  334.3 0.6 fusion.36
  334.9 1.3 fusion.39
  336.2 0.6 broadcast_divide_fusion
  336.9 0.2 select_reduce_fusion
  337.0 0.6 gather_fusion.1
  337.7 0.1 and_select_fusion.3
  337.8 0.7 pad_maximum_fusion.scal_ref
  338.4 18.1 %shard_map.111 = (bf16[448,4096]{1,0:T(8,128)(2,1)}, f32[448,4096]{1,0:T(8,128)}, f32[448,4096]{1,0:T(8,128)}) custom-call(f32[6]{0:T(128)} %pad_maximum_fusion.scal_ref, bf16[2,448,4096]{2,1,0:T(8,128)(2,1)} %copy-done, bf16[2,448,4096]{2,1,0:T(8,128)(2,1)} %collective-permute-done.recv_ref, f32[448,4096]{1,0:T(8,128)} %m_ref.1, f32[448,4096]{1,0:T(8,128)} %s_ref.1, ...), custom_call_target="tpu_custom_call" | custom-call | flops 36700160 | bytes 51380224 | tf_op jit(solution)/shard_map/pallas_call | solution.py:35
  (18 shorter events, 0.2 us)
Async XLA Ops:
  7.2 262.6 %all-gather.2.cloned.1.call-start = ((), (), s32[]{:S(2)}) async-start(), calls=%async_computation.1 | async-start | bytes 17825792 | tf_op jit(solution)/shard_map/all_gather | solution.py:71
  18.1 149.9 %all-to-all-start = ((bf16[128,16,896]{0,2,1:T(8,128)(2,1)}), bf16[128,16,896]{0,2,1:T(8,128)(2,1)}, u32[]{:S(2)}, u32[]{:S(2)}) async-start(bf16[128,16,896]{0,2,1:T(8,128)(2,1)} %bitcast.40), calls=%async_computation | async-start | bytes 7340032 | tf_op jit(solution)/shard_map/all_to_all | solution.py:69
  286.0 15.1 %collective-permute-start = (bf16[2,448,4096]{2,1,0:T(8,128)(2,1)}, bf16[2,448,4096]{2,1,0:T(8,128)(2,1)}, u32[]{:S(2)}, u32[]{:S(2)}) collective-permute-start(bf16[2,448,4096]{2,1,0:T(8,128)(2,1)} %convolution_convert_fusion), channel_id=1, source_target_pairs={{0,8},{8,0},{1,9},{9,1},{2,10},{10,2},{3,11},{11,3},{4,12},{12,4},... | collective-permute-start | bytes 22020104 | tf_op jit(solution)/shard_map/ppermute | solution.py:79
  301.1 9.3 %copy-start = (bf16[2,448,4096]{2,1,0:T(8,128)(2,1)}, bf16[2,448,4096]{2,1,0:T(8,128)(2,1)S(1)}, u32[]{:S(2)}) copy-start(bf16[2,448,4096]{2,1,0:T(8,128)(2,1)S(1)} %convolution_convert_fusion.1.own_ref) | copy-start | bytes 22020100
  301.1 33.1 %copy-start.2 = (s32[4]{0:T(128)S(1)}, s32[4]{0:T(128)}, u32[]{:S(2)}) copy-start(s32[4]{0:T(128)} %param.16) | copy-start | bytes 52
  301.1 33.2 %copy-start.1 = (f32[4]{0:T(128)S(1)}, f32[4]{0:T(128)}, u32[]{:S(2)}) copy-start(f32[4]{0:T(128)} %param.15) | copy-start | bytes 52
  336.9 19.7 %copy-start.3 = (f32[4]{0:T(128)}, f32[4]{0:T(128)S(1)}, u32[]{:S(2)}) copy-start(f32[4]{0:T(128)S(1)} %broadcast_divide_fusion) | copy-start | bytes 52
Sparse Core Ops, SparseCore 0:
  10.8 258.8 all-gather.1

commit v10 on v9

--- a/solution.py
+++ b/solution.py
@@ -97,7 +97,7 @@
     hi = jnp.maximum(pos[:, None], pos[None, :])
     device_gram = jnp.take(sums, lo * groups - lo * (lo - 1) // 2 + (hi - lo))
     gram = device_gram
-    for axes in (("core",), ("pair", "x"), ("fsdp",)):
+    for axes in (("core", "pair", "x"), ("fsdp",)):
         gram = lax.psum(gram, axes)
     score = jnp.sum(gram, axis=1) * (groups / jnp.trace(gram))
     onehot = (domain_ids[:, None] == jnp.arange(groups, dtype=jnp.int32)[None, :]).astype(

time: 364 us -> 367 us (level)
    psum x3 -> x2, blocking collectives: 21.3 us -> 24 us  [on_device(): gram = lax.psum(gram, axes)]
where the time goes in v10:
time: 367 us; the launch traced here: 366 us
  waiting for transfers between devices  225 us (61%)
  local copies, waits for them, and re-layouts  31 us (8%)
  matrix products  30.3 us (8%)
  blocking collectives  24 us (7%)
  Pallas kernels  18.1 us (5%)
  between operations  15.6 us (4%)
  other arithmetic  13.8 us (4%)
  starting transfers between devices  8.4 us (2%)
    all_to_all x1, waiting for transfers between devices, on_device(): lax.all_to_all(shaped, SAME_CORE, split_axis=1, concat_axis=0, tiled=True)  141 us
    all_gather x1, waiting for transfers between devices, on_device(): mine = lax.all_gather(cotangent, SAME_CORE, axis=0, tiled=True)  82.7 us
    psum x2, blocking collectives, on_device(): gram = lax.psum(gram, axes)  24 us
    pallas_call x1, Pallas kernels, adam_update(): pl.pallas_call(adam_kernel, grid=(rows // tile,), in_specs=[pl.BlockSpec(...  18.1 us
    dot_general x1, matrix products, on_device(): lax.dot_general(cols_partner, mine, dims, preferred_element_type=jnp.floa...  16.3 us
    dot_general x1, matrix products, on_device(): lax.dot_general(cols_own, mine, dims, preferred_element_type=jnp.float32)  14 us
    reduce_sum x1, other arithmetic, on_device(): jnp.sum(owned[i].astype(jnp.float32) * owned[j].astype(jnp.float32), axis=0)  9.2 us
    all_to_all x1, starting transfers between devices, on_device(): lax.all_to_all(shaped, SAME_CORE, split_axis=1, concat_axis=0, tiled=True)  8.36 us
  transfers between devices with their start and end apart: 3, of which 2 were waited for; matrix products, arithmetic and copies ran while one was open for 12% of the time, Pallas kernels for 0%

profile of v10, /device:TPU:0, one launch (start us, length us, event | category | flops | bytes accessed | tf_op | source)
XLA Modules:
  0.0 366.1 jit_solution(4687156169858122697)
XLA Ops:
  7.2 0.7 all-gather.2.cloned.1.call-update
  7.9 6.1 %copy.17 = bf16[128,14336]{0,1:T(8,128)(2,1)} copy(bf16[128,14336]{1,0:T(8,128)(2,1)} %param.10) | data formatting | bytes 7340032 | tf_op args[0]
  13.9 4.2 %copy.18 = bf16[128,2,8,2,448]{0,4,3,2,1:T(8,128)(2,1)} copy(bf16[128,2,8,2,448]{0,4,2,3,1:T(8,128)(2,1)} %bitcast.41) | data formatting | bytes 7340032 | tf_op jit(solution)/shard_map/transpose | solution.py:67
  18.1 8.4 %all-to-all-start = ((bf16[128,16,896]{0,2,1:T(8,128)(2,1)}), bf16[128,16,896]{0,2,1:T(8,128)(2,1)}, u32[]{:S(2)}, u32[]{:S(2)}) async-start(bf16[128,16,896]{0,2,1:T(8,128)(2,1)} %bitcast.40), calls=%async_computation | async-start | bytes 7340032 | tf_op jit(solution)/shard_map/all_to_all | solution.py:69
  26.5 141.5 %all-to-all-done = bf16[128,16,896]{0,2,1:T(8,128)(2,1)} async-done(((bf16[128,16,896]{0,2,1:T(8,128)(2,1)}), bf16[128,16,896]{0,2,1:T(8,128)(2,1)}, u32[]{:S(2)}, u32[]{:S(2)}) %all-to-all-start) | async-done | bytes 3670048 | tf_op jit(solution)/shard_map/all_to_all | solution.py:69
  168.0 6.7 %copy.19 = bf16[16,128,1,896]{1,0,3,2:T(8,128)(2,1)} copy(bf16[16,128,1,896]{1,3,0,2:T(8,128)(2,1)} %bitcast.4) | data formatting | bytes 7340032 | tf_op jit(solution)/shard_map/all_to_all | solution.py:69
  174.6 6.5 %reshape.361 = bf16[2,1024,2,448]{1,0,3,2:T(2,128)(2,1)} reshape(bf16[16,128,1,896]{1,0,3,2:T(8,128)(2,1)} %copy.19) | data formatting | bytes 7340032 | tf_op jit(solution)/shard_map/reshape | solution.py:70
  181.2 5.8 %constant_dynamic-slice_fusion.1 = (bf16[2,1024,1,448]{1,0,3,2:T(2,128)(2,1)S(1)}, bf16[2,1024,1,448]{1,0,3,2:T(2,128)(2,1)}) fusion(bf16[2,1024,2,448]{1,0,3,2:T(2,128)(2,1)} %reshape.361, s32[]{:T(128)S(6)} %select_n.125, s32[]{:T(128)S(6)} %select_n.127), kind=kLoop, calls=%fused_computation.85 | loop fusion | bytes 7340040 | tf_op jit(solution)/shard_map/jit(_take) | solution.py:75
  187.0 82.7 %all-gather.2.cloned.1.call-done = bf16[2048,4096]{1,0:T(8,128)(2,1)} async-done(((bf16[128,4096]{1,0:T(8,128)(2,1)}), bf16[2048,4096]{1,0:T(8,128)(2,1)}) %all-gather.2.cloned.1.call-update) | async-done | bytes 16777232 | tf_op jit(solution)/shard_map/all_gather | solution.py:71
  269.7 16.3 %convolution_convert_fusion = bf16[2,448,4096]{2,1,0:T(8,128)(2,1)} fusion(bf16[2,1024,4096]{2,1,0:T(8,128)(2,1)} %bitcast.38, bf16[2,1024,1,448]{1,0,3,2:T(2,128)(2,1)} %get-tuple-element.41, pred[]{:T(512)S(6)} %and.97), kind=kOutput, calls=%fused_computation.22 | convolution fusion | flops 7520780288 | bytes 25952256 | tf_op jit(solution)/shard_map/dot_general | solution.py:76
  286.0 0.1 compare_select_fusion
  286.1 0.1 reshape.422
  286.9 0.1 fusion.32
  287.0 14.0 %convolution_convert_fusion.1.own_ref = bf16[2,448,4096]{2,1,0:T(8,128)(2,1)S(1)} fusion(bf16[2,1024,4096]{2,1,0:T(8,128)(2,1)} %bitcast.39, bf16[2,1024,1,448]{1,0,3,2:T(2,128)(2,1)S(1)} %get-tuple-element.40, pred[]{:T(512)S(6)} %and.96), kind=kOutput, calls=%fused_computation.23 | convolution fusion | flops 7520780288 | bytes 25952256 | tf_op jit(solution)/shard_map/dot_general | solution.py:80
  301.1 9.2 %fusion.9 = (f32[4096]{0:T(1024)S(1)}, f32[4096]{0:T(1024)S(1)}, f32[4096]{0:T(1024)S(1)}, f32[4096]{0:T(1024)S(1)}, f32[4096]{0:T(1024)S(1)}, /*index=5*/f32[40...) fusion(bf16[2,448,4096]{2,1,0:T(8,128)(2,1)} %collective-permute-done.recv_ref, ...), kind=kLoop, calls=%fused_computation.21 | loop fusion | flops 43999232 | bytes 14843904 | tf_op jit(solution)/shard_map/reduce_sum | solution.py:89
  310.4 0.3 stack.45
  310.6 0.1 reduce_sum.155
  310.8 0.7 gather_fusion
  311.4 0.1 reshape.421
  311.5 0.1 and_select_fusion
  311.6 14.2 %psum.14 = f32[4,4]{1,0:T(4,128)S(1)} all-reduce(f32[4,4]{1,0:T(4,128)S(1)} %and_select_fusion), channel_id=1, replica_groups=mesh['x'=2,'core'=2,'fsdp'=4,'pair'=2] {'core','pair','x'}, use_global_device_ids=true, to_apply=%region_11.13 | all-reduce | flops 16 | bytes 128 | tf_op jit(solution)/shard_map/psum | solution.py:101
  325.8 9.8 %psum.15 = f32[4,4]{1,0:T(4,128)S(1)} all-reduce(f32[4,4]{1,0:T(4,128)S(1)} %psum.14), channel_id=1, replica_groups=mesh['x'=2,'core'=2,'fsdp'=4,'pair'=2] {'fsdp'}, use_global_device_ids=true, to_apply=%region_12.14 | all-reduce | flops 16 | bytes 128 | tf_op jit(solution)/shard_map/psum | solution.py:101
  335.6 0.7 select_reduce_fusion.2
  337.0 0.1 select_reduce_fusion.1
  337.1 0.6 fusion.36
  337.7 1.3 fusion.39
  338.9 0.6 broadcast_divide_fusion
  339.6 0.2 select_reduce_fusion
  339.8 0.6 gather_fusion.1
  340.4 0.1 and_select_fusion.3
  340.5 0.7 pad_maximum_fusion.scal_ref
  341.2 18.1 %shard_map.111 = (bf16[448,4096]{1,0:T(8,128)(2,1)}, f32[448,4096]{1,0:T(8,128)}, f32[448,4096]{1,0:T(8,128)}) custom-call(f32[6]{0:T(128)} %pad_maximum_fusion.scal_ref, bf16[2,448,4096]{2,1,0:T(8,128)(2,1)} %copy-done, bf16[2,448,4096]{2,1,0:T(8,128)(2,1)} %collective-permute-done.recv_ref, f32[448,4096]{1,0:T(8,128)} %m_ref.1, f32[448,4096]{1,0:T(8,128)} %s_ref.1, ...), custom_call_target="tpu_custom_call" | custom-call | flops 36700160 | bytes 51380224 | tf_op jit(solution)/shard_map/pallas_call | solution.py:35
  (17 shorter events, 0.1 us)
Async XLA Ops:
  7.2 262.6 %all-gather.2.cloned.1.call-start = ((), (), s32[]{:S(2)}) async-start(), calls=%async_computation.1 | async-start | bytes 17825792 | tf_op jit(solution)/shard_map/all_gather | solution.py:71
  18.1 149.9 %all-to-all-start = ((bf16[128,16,896]{0,2,1:T(8,128)(2,1)}), bf16[128,16,896]{0,2,1:T(8,128)(2,1)}, u32[]{:S(2)}, u32[]{:S(2)}) async-start(bf16[128,16,896]{0,2,1:T(8,128)(2,1)} %bitcast.40), calls=%async_computation | async-start | bytes 7340032 | tf_op jit(solution)/shard_map/all_to_all | solution.py:69
  286.0 15.1 %collective-permute-start = (bf16[2,448,4096]{2,1,0:T(8,128)(2,1)}, bf16[2,448,4096]{2,1,0:T(8,128)(2,1)}, u32[]{:S(2)}, u32[]{:S(2)}) collective-permute-start(bf16[2,448,4096]{2,1,0:T(8,128)(2,1)} %convolution_convert_fusion), channel_id=1, source_target_pairs={{0,8},{8,0},{1,9},{9,1},{2,10},{10,2},{3,11},{11,3},{4,12},{12,4},... | collective-permute-start | bytes 22020104 | tf_op jit(solution)/shard_map/ppermute | solution.py:79
  301.1 9.3 %copy-start = (bf16[2,448,4096]{2,1,0:T(8,128)(2,1)}, bf16[2,448,4096]{2,1,0:T(8,128)(2,1)S(1)}, u32[]{:S(2)}) copy-start(bf16[2,448,4096]{2,1,0:T(8,128)(2,1)S(1)} %convolution_convert_fusion.1.own_ref) | copy-start | bytes 22020100
  301.1 35.9 %copy-start.2 = (s32[4]{0:T(128)S(1)}, s32[4]{0:T(128)}, u32[]{:S(2)}) copy-start(s32[4]{0:T(128)} %param.16) | copy-start | bytes 52
  301.1 36.0 %copy-start.1 = (f32[4]{0:T(128)S(1)}, f32[4]{0:T(128)}, u32[]{:S(2)}) copy-start(f32[4]{0:T(128)} %param.15) | copy-start | bytes 52
  339.6 19.7 %copy-start.3 = (f32[4]{0:T(128)}, f32[4]{0:T(128)S(1)}, u32[]{:S(2)}) copy-start(f32[4]{0:T(128)S(1)} %broadcast_divide_fusion) | copy-start | bytes 52
Sparse Core Ops, SparseCore 0:
  10.8 258.8 all-gather.1

commit v11 on v9

--- a/solution.py
+++ b/solution.py
@@ -86,7 +86,7 @@
     keys = [(i, j) for i in range(groups) for j in range(i, groups)]
     partial = jnp.stack(
         [
-            jnp.sum(owned[i].astype(jnp.float32) * owned[j].astype(jnp.float32), axis=0)
+            jnp.sum(owned[i].astype(jnp.float32) * owned[j].astype(jnp.float32), axis=1)
             for i, j in keys
         ]
     )

time: 364 us -> 365 us (level)
  no operation moved by 1% of the time
where the time goes in v11:
time: 365 us; the launch traced here: 364 us
  waiting for transfers between devices  225 us (62%)
  local copies, waits for them, and re-layouts  30.8 us (8%)
  matrix products  30.3 us (8%)
  blocking collectives  21.3 us (6%)
  Pallas kernels  18.1 us (5%)
  between operations  15.6 us (4%)
  other arithmetic  15 us (4%)
  starting transfers between devices  8.4 us (2%)
    all_to_all x1, waiting for transfers between devices, on_device(): lax.all_to_all(shaped, SAME_CORE, split_axis=1, concat_axis=0, tiled=True)  141 us
    all_gather x1, waiting for transfers between devices, on_device(): mine = lax.all_gather(cotangent, SAME_CORE, axis=0, tiled=True)  82.7 us
    psum x3, blocking collectives, on_device(): gram = lax.psum(gram, axes)  21.3 us
    pallas_call x1, Pallas kernels, adam_update(): pl.pallas_call(adam_kernel, grid=(rows // tile,), in_specs=[pl.BlockSpec(...  18.1 us
    dot_general x1, matrix products, on_device(): lax.dot_general(cols_partner, mine, dims, preferred_element_type=jnp.floa...  16.3 us
    dot_general x1, matrix products, on_device(): lax.dot_general(cols_own, mine, dims, preferred_element_type=jnp.float32)  14 us
    reduce_sum x1, other arithmetic, on_device(): jnp.sum(owned[i].astype(jnp.float32) * owned[j].astype(jnp.float32), axis=1)  10.4 us
    all_to_all x1, starting transfers between devices, on_device(): lax.all_to_all(shaped, SAME_CORE, split_axis=1, concat_axis=0, tiled=True)  8.36 us
  transfers between devices with their start and end apart: 3, of which 2 were waited for; matrix products, arithmetic and copies ran while one was open for 12% of the time, Pallas kernels for 0%

profile of v11, /device:TPU:0, one launch (start us, length us, event | category | flops | bytes accessed | tf_op | source)
XLA Modules:
  0.0 364.4 jit_solution(4558326979328964773)
XLA Ops:
  7.2 0.7 all-gather.2.cloned.1.call-update
  7.9 6.1 %copy.17 = bf16[128,14336]{0,1:T(8,128)(2,1)} copy(bf16[128,14336]{1,0:T(8,128)(2,1)} %param.10) | data formatting | bytes 7340032 | tf_op args[0]
  13.9 4.2 %copy.18 = bf16[128,2,8,2,448]{0,4,3,2,1:T(8,128)(2,1)} copy(bf16[128,2,8,2,448]{0,4,2,3,1:T(8,128)(2,1)} %bitcast.41) | data formatting | bytes 7340032 | tf_op jit(solution)/shard_map/transpose | solution.py:67
  18.1 8.4 %all-to-all-start = ((bf16[128,16,896]{0,2,1:T(8,128)(2,1)}), bf16[128,16,896]{0,2,1:T(8,128)(2,1)}, u32[]{:S(2)}, u32[]{:S(2)}) async-start(bf16[128,16,896]{0,2,1:T(8,128)(2,1)} %bitcast.40), calls=%async_computation | async-start | bytes 7340032 | tf_op jit(solution)/shard_map/all_to_all | solution.py:69
  26.5 141.5 %all-to-all-done = bf16[128,16,896]{0,2,1:T(8,128)(2,1)} async-done(((bf16[128,16,896]{0,2,1:T(8,128)(2,1)}), bf16[128,16,896]{0,2,1:T(8,128)(2,1)}, u32[]{:S(2)}, u32[]{:S(2)}) %all-to-all-start) | async-done | bytes 3670048 | tf_op jit(solution)/shard_map/all_to_all | solution.py:69
  168.0 6.7 %copy.19 = bf16[16,128,1,896]{1,0,3,2:T(8,128)(2,1)} copy(bf16[16,128,1,896]{1,3,0,2:T(8,128)(2,1)} %bitcast.4) | data formatting | bytes 7340032 | tf_op jit(solution)/shard_map/all_to_all | solution.py:69
  174.6 6.5 %reshape.361 = bf16[2,1024,2,448]{1,0,3,2:T(2,128)(2,1)} reshape(bf16[16,128,1,896]{1,0,3,2:T(8,128)(2,1)} %copy.19) | data formatting | bytes 7340032 | tf_op jit(solution)/shard_map/reshape | solution.py:70
  181.2 5.8 %constant_dynamic-slice_fusion.1 = (bf16[2,1024,1,448]{1,0,3,2:T(2,128)(2,1)S(1)}, bf16[2,1024,1,448]{1,0,3,2:T(2,128)(2,1)}) fusion(bf16[2,1024,2,448]{1,0,3,2:T(2,128)(2,1)} %reshape.361, s32[]{:T(128)S(6)} %select_n.125, s32[]{:T(128)S(6)} %select_n.127), kind=kLoop, calls=%fused_computation.85 | loop fusion | bytes 7340040 | tf_op jit(solution)/shard_map/jit(_take) | solution.py:75
  187.0 82.7 %all-gather.2.cloned.1.call-done = bf16[2048,4096]{1,0:T(8,128)(2,1)} async-done(((bf16[128,4096]{1,0:T(8,128)(2,1)}), bf16[2048,4096]{1,0:T(8,128)(2,1)}) %all-gather.2.cloned.1.call-update) | async-done | bytes 16777232 | tf_op jit(solution)/shard_map/all_gather | solution.py:71
  269.7 16.3 %convolution_convert_fusion = bf16[2,448,4096]{2,1,0:T(8,128)(2,1)} fusion(bf16[2,1024,4096]{2,1,0:T(8,128)(2,1)} %bitcast.38, bf16[2,1024,1,448]{1,0,3,2:T(2,128)(2,1)} %get-tuple-element.41, pred[]{:T(512)S(6)} %and.97), kind=kOutput, calls=%fused_computation.22 | convolution fusion | flops 7520780288 | bytes 25952256 | tf_op jit(solution)/shard_map/dot_general | solution.py:76
  286.0 0.1 compare_select_fusion
  286.1 0.1 reshape.422
  286.9 0.1 fusion.32
  287.0 14.0 %convolution_convert_fusion.1.own_ref = bf16[2,448,4096]{2,1,0:T(8,128)(2,1)S(1)} fusion(bf16[2,1024,4096]{2,1,0:T(8,128)(2,1)} %bitcast.39, bf16[2,1024,1,448]{1,0,3,2:T(2,128)(2,1)S(1)} %get-tuple-element.40, pred[]{:T(512)S(6)} %and.96), kind=kOutput, calls=%fused_computation.23 | convolution fusion | flops 7520780288 | bytes 25952256 | tf_op jit(solution)/shard_map/dot_general | solution.py:80
  301.1 10.4 %fusion.9 = (f32[448]{0:T(512)S(1)}, f32[448]{0:T(512)S(1)}, f32[448]{0:T(512)S(1)}, f32[448]{0:T(512)S(1)}, f32[448]{0:T(512)S(1)}, /*index=5*/f32[448]{0:T(512...) fusion(bf16[2,448,4096]{2,1,0:T(8,128)(2,1)} %collective-permute-done.recv_ref, ...), kind=kLoop, calls=%fused_computation.21 | loop fusion | flops 44035712 | bytes 14697984 | tf_op jit(solution)/shard_map/reduce_sum | solution.py:89
  311.7 0.1 reduce_sum.155
  311.8 0.7 gather_fusion
  312.4 0.1 reshape.421
  312.5 0.1 and_select_fusion
  312.6 2.6 psum.21
  315.3 8.9 %psum.22 = f32[4,4]{1,0:T(4,128)S(1)} all-reduce(f32[4,4]{1,0:T(4,128)S(1)} %psum.21), channel_id=1, replica_groups=mesh['x'=2,'core'=2,'fsdp'=4,'pair'=2] {'pair','x'}, use_global_device_ids=true, to_apply=%region_12.14 | all-reduce | flops 16 | bytes 128 | tf_op jit(solution)/shard_map/psum | solution.py:101
  324.2 9.7 %psum.23 = f32[4,4]{1,0:T(4,128)S(1)} all-reduce(f32[4,4]{1,0:T(4,128)S(1)} %psum.22), channel_id=1, replica_groups=mesh['x'=2,'core'=2,'fsdp'=4,'pair'=2] {'fsdp'}, use_global_device_ids=true, to_apply=%region_13.15 | all-reduce | flops 16 | bytes 128 | tf_op jit(solution)/shard_map/psum | solution.py:101
  333.9 0.7 select_reduce_fusion.2
  335.3 0.1 select_reduce_fusion.1
  335.4 0.6 fusion.36
  336.0 1.3 fusion.39
  337.2 0.6 broadcast_divide_fusion
  337.9 0.2 select_reduce_fusion
  338.1 0.6 gather_fusion.1
  338.7 0.1 and_select_fusion.3
  338.8 0.7 pad_maximum_fusion.scal_ref
  339.5 18.1 %shard_map.111 = (bf16[448,4096]{1,0:T(8,128)(2,1)}, f32[448,4096]{1,0:T(8,128)}, f32[448,4096]{1,0:T(8,128)}) custom-call(f32[6]{0:T(128)} %pad_maximum_fusion.scal_ref, bf16[2,448,4096]{2,1,0:T(8,128)(2,1)} %copy-done, bf16[2,448,4096]{2,1,0:T(8,128)(2,1)} %collective-permute-done.recv_ref, f32[448,4096]{1,0:T(8,128)} %m_ref.1, f32[448,4096]{1,0:T(8,128)} %s_ref.1, ...), custom_call_target="tpu_custom_call" | custom-call | flops 36700160 | bytes 51380224 | tf_op jit(solution)/shard_map/pallas_call | solution.py:35
  (18 shorter events, 0.2 us)
Async XLA Ops:
  7.2 262.6 %all-gather.2.cloned.1.call-start = ((), (), s32[]{:S(2)}) async-start(), calls=%async_computation.1 | async-start | bytes 17825792 | tf_op jit(solution)/shard_map/all_gather | solution.py:71
  18.1 149.9 %all-to-all-start = ((bf16[128,16,896]{0,2,1:T(8,128)(2,1)}), bf16[128,16,896]{0,2,1:T(8,128)(2,1)}, u32[]{:S(2)}, u32[]{:S(2)}) async-start(bf16[128,16,896]{0,2,1:T(8,128)(2,1)} %bitcast.40), calls=%async_computation | async-start | bytes 7340032 | tf_op jit(solution)/shard_map/all_to_all | solution.py:69
  286.0 15.1 %collective-permute-start = (bf16[2,448,4096]{2,1,0:T(8,128)(2,1)}, bf16[2,448,4096]{2,1,0:T(8,128)(2,1)}, u32[]{:S(2)}, u32[]{:S(2)}) collective-permute-start(bf16[2,448,4096]{2,1,0:T(8,128)(2,1)} %convolution_convert_fusion), channel_id=1, source_target_pairs={{0,8},{8,0},{1,9},{9,1},{2,10},{10,2},{3,11},{11,3},{4,12},{12,4},... | collective-permute-start | bytes 22020104 | tf_op jit(solution)/shard_map/ppermute | solution.py:79
  301.1 10.5 %copy-start = (bf16[2,448,4096]{2,1,0:T(8,128)(2,1)}, bf16[2,448,4096]{2,1,0:T(8,128)(2,1)S(1)}, u32[]{:S(2)}) copy-start(bf16[2,448,4096]{2,1,0:T(8,128)(2,1)S(1)} %convolution_convert_fusion.1.own_ref) | copy-start | bytes 22020100
  301.1 34.2 %copy-start.2 = (s32[4]{0:T(128)S(1)}, s32[4]{0:T(128)}, u32[]{:S(2)}) copy-start(s32[4]{0:T(128)} %param.16) | copy-start | bytes 52
  301.1 34.3 %copy-start.1 = (f32[4]{0:T(128)S(1)}, f32[4]{0:T(128)}, u32[]{:S(2)}) copy-start(f32[4]{0:T(128)} %param.15) | copy-start | bytes 52
  337.9 19.7 %copy-start.3 = (f32[4]{0:T(128)}, f32[4]{0:T(128)S(1)}, u32[]{:S(2)}) copy-start(f32[4]{0:T(128)S(1)} %broadcast_divide_fusion) | copy-start | bytes 52
Sparse Core Ops, SparseCore 0:
  10.8 258.8 all-gather.1

commit v12 on v9

--- a/solution.py
+++ b/solution.py
@@ -73,13 +73,19 @@
     dims = (((1,), (1,)), ((0,), (0,)))
     cols_partner = jnp.take(columns, 1 - core, axis=2)
     cols_own = jnp.take(columns, core, axis=2)
-    g_partner = lax.dot_general(
-        cols_partner, mine, dims, preferred_element_type=jnp.float32
-    ).astype(jnp.bfloat16)
+    dims = (((0,), (0,)), ((), ()))
+
+    def grads(cols):
+        return jnp.stack(
+            [
+                lax.dot_general(cols[x], mine[x], dims, preferred_element_type=jnp.float32)
+                for x in range(chips_x)
+            ]
+        ).astype(jnp.bfloat16)
+
+    g_partner = grads(cols_partner)
     received = lax.ppermute(g_partner, "core", [(0, 1), (1, 0)])
-    g_own = lax.dot_general(
-        cols_own, mine, dims, preferred_element_type=jnp.float32
-    ).astype(jnp.bfloat16)
+    g_own = grads(cols_own)
     owned = jnp.concatenate([g_own, received])
     half = jnp.arange(chips_x, dtype=jnp.int32) * 2
     order = jnp.concatenate([half + core, half + 1 - core])

time: 364 us -> 375 us (1.030)
  other arithmetic: 13.8 us -> 20.3 us
  matrix products: 30.3 us -> 36.6 us
    another operation x0 -> x2, other arithmetic: none -> 10.5 us  [grads(): jnp.stack([lax.dot_general(cols[x], mine[x], dims, preferred_element_type...]
    reduce_sum x1 -> x0, other arithmetic: 9.2 us -> none  [on_device(): jnp.sum(owned[i].astype(jnp.float32) * owned[j].astype(jnp.float32), axis=0)]
    dot_general x2 -> x4, matrix products: 30.3 us -> 36.6 us  [grads(): lax.dot_general(cols[x], mine[x], dims, preferred_element_type=jnp.float32)]
    another operation x1 -> x0, local copies, waits for them, and re-layouts: 5.83 us -> none  [on_device(): cols_own = jnp.take(columns, core, axis=2)]
    select_n x0 -> x1, other arithmetic: none -> 5.24 us  [on_device(): cols_own = jnp.take(columns, core, axis=2)]
  transfers between devices with their start and end apart: 3 -> 3, of which waited for: 2 -> 3; matrix products, arithmetic and copies ran while one was open for 12% -> 10% of each run, Pallas kernels for 0% -> 0%
where the time goes in v12:
time: 375 us; the launch traced here: 374 us
  waiting for transfers between devices  227 us (61%)
  matrix products  36.6 us (10%)
  local copies, waits for them, and re-layouts  27.4 us (7%)
  blocking collectives  21.1 us (6%)
  other arithmetic  20.3 us (5%)
  Pallas kernels  18.1 us (5%)
  between operations  15.6 us (4%)
  starting transfers between devices  8.4 us (2%)
    all_to_all x1, waiting for transfers between devices, on_device(): lax.all_to_all(shaped, SAME_CORE, split_axis=1, concat_axis=0, tiled=True)  141 us
    all_gather x1, waiting for transfers between devices, on_device(): mine = lax.all_gather(cotangent, SAME_CORE, axis=0, tiled=True)  81.6 us
    dot_general x4, matrix products, grads(): lax.dot_general(cols[x], mine[x], dims, preferred_element_type=jnp.float32)  36.6 us
    psum x3, blocking collectives, on_device(): gram = lax.psum(gram, axes)  21.1 us
    pallas_call x1, Pallas kernels, adam_update(): pl.pallas_call(adam_kernel, grid=(rows // tile,), in_specs=[pl.BlockSpec(...  18.1 us
    another operation x2, other arithmetic, grads(): jnp.stack([lax.dot_general(cols[x], mine[x], dims, preferred_element_type...  10.5 us
    all_to_all x1, starting transfers between devices, on_device(): lax.all_to_all(shaped, SAME_CORE, split_axis=1, concat_axis=0, tiled=True)  8.36 us
  transfers between devices with their start and end apart: 3, of which 3 were waited for; matrix products, arithmetic and copies ran while one was open for 10% of the time, Pallas kernels for 0%

profile of v12, /device:TPU:0, one launch (start us, length us, event | category | flops | bytes accessed | tf_op | source)
XLA Modules:
  0.0 374.1 jit_solution(9425241141742716675)
XLA Ops:
  7.2 0.7 all-gather.2.cloned.1.call-update
  7.9 6.1 %copy.17 = bf16[128,14336]{0,1:T(8,128)(2,1)} copy(bf16[128,14336]{1,0:T(8,128)(2,1)} %param.10) | data formatting | bytes 7340032 | tf_op args[0]
  13.9 4.2 %copy.18 = bf16[128,2,8,2,448]{0,4,3,2,1:T(8,128)(2,1)} copy(bf16[128,2,8,2,448]{0,4,2,3,1:T(8,128)(2,1)} %bitcast.58) | data formatting | bytes 7340032 | tf_op jit(solution)/shard_map/transpose | solution.py:67
  18.1 8.4 %all-to-all-start = ((bf16[128,16,896]{0,2,1:T(8,128)(2,1)}), bf16[128,16,896]{0,2,1:T(8,128)(2,1)}, u32[]{:S(2)}, u32[]{:S(2)}) async-start(bf16[128,16,896]{0,2,1:T(8,128)(2,1)} %bitcast.57), calls=%async_computation | async-start | bytes 7340032 | tf_op jit(solution)/shard_map/all_to_all | solution.py:69
  26.5 141.5 %all-to-all-done = bf16[128,16,896]{0,2,1:T(8,128)(2,1)} async-done(((bf16[128,16,896]{0,2,1:T(8,128)(2,1)}), bf16[128,16,896]{0,2,1:T(8,128)(2,1)}, u32[]{:S(2)}, u32[]{:S(2)}) %all-to-all-start) | async-done | bytes 3670048 | tf_op jit(solution)/shard_map/all_to_all | solution.py:69
  168.0 6.7 %copy.19 = bf16[16,128,1,896]{1,0,3,2:T(8,128)(2,1)} copy(bf16[16,128,1,896]{1,3,0,2:T(8,128)(2,1)} %bitcast.4) | data formatting | bytes 7340032 | tf_op jit(solution)/shard_map/all_to_all | solution.py:69
  174.6 6.5 %reshape.363 = bf16[2,1024,2,448]{1,0,3,2:T(2,128)(2,1)} reshape(bf16[16,128,1,896]{1,0,3,2:T(8,128)(2,1)} %copy.19) | data formatting | bytes 7340032 | tf_op jit(solution)/shard_map/reshape | solution.py:70
  181.2 5.2 %broadcast_select_fusion.1 = (bf16[2,1024,1,448]{1,0,3,2:T(2,128)(2,1)S(1)}, bf16[2,1024,1,448]{1,0,3,2:T(2,128)(2,1)S(1)}) fusion(pred[]{:T(512)S(6)} %and.96, bf16[2,1024,2,448]{1,0,3,2:T(2,128)(2,1)} %reshape.363, s32[]{:T(128)S(6)} %select_n.125, s32[]{:T(128)S(6)} %select_n.127, pred[]{:T(512)S(6)} %and.97), kind=kLoop, calls=%fused_computation.41 | loop fusion | flops 1835008 | bytes 7340042 | tf_op jit(solution)/shard_map/jit(_take)/select_n | solution.py:75
  186.4 1.8 copy.24
  188.2 81.6 %all-gather.2.cloned.1.call-done = bf16[2048,4096]{1,0:T(8,128)(2,1)} async-done(((bf16[128,4096]{1,0:T(8,128)(2,1)}), bf16[2048,4096]{1,0:T(8,128)(2,1)}) %all-gather.2.cloned.1.call-update) | async-done | bytes 16777232 | tf_op jit(solution)/shard_map/all_gather | solution.py:71
  269.7 7.8 %fusion.36 = bf16[1,448,4096]{2,1,0:T(8,128)(2,1)S(1)} fusion(bf16[2048,4096]{1,0:T(8,128)(2,1)} %all-gather.2.cloned.1.call-done, bf16[2,1024,448]{1,2,0:T(8,128)(2,1)} %bitcast.61), kind=kOutput, calls=%fused_computation.38 | convolution fusion | flops 3759931392 | bytes 12976128 | tf_op jit(solution)/shard_map/dot_general | solution.py:81
  277.5 7.7 %fusion.30 = bf16[1,448,4096]{2,1,0:T(8,128)(2,1)S(1)} fusion(bf16[2048,4096]{1,0:T(8,128)(2,1)} %all-gather.2.cloned.1.call-done, bf16[2,1024,448]{1,2,0:T(8,128)(2,1)S(1)} %bitcast.62), kind=kOutput, calls=%fused_computation.36 | convolution fusion | flops 3759931392 | bytes 12976128 | tf_op jit(solution)/shard_map/dot_general | solution.py:81
  285.3 3.7 pad_maximum_fusion
  290.0 0.5 copy.25
  290.5 7.6 %fusion.39 = bf16[1,448,4096]{2,1,0:T(8,128)(2,1)S(1)} fusion(bf16[2048,4096]{1,0:T(8,128)(2,1)} %all-gather.2.cloned.1.call-done, bf16[2,1024,448]{1,2,0:T(8,128)(2,1)S(1)} %bitcast.59), kind=kOutput, calls=%fused_computation.39 | convolution fusion | flops 3759931392 | bytes 12976128 | tf_op jit(solution)/shard_map/dot_general | solution.py:81
  298.1 2.8 collective-permute-done.recv_ref
  300.9 13.5 %fusion.17 = (f32[4096]{0:T(1024)S(1)}, f32[4096]{0:T(1024)S(1)}, f32[4096]{0:T(1024)S(1)}, f32[4096]{0:T(1024)S(1)}, f32[4096]{0:T(1024)S(1)}, /*index=5*/f32[4...) fusion(bf16[2,448,4096]{2,1,0:T(8,128)(2,1)} %collective-permut, ...), kind=kOutput, calls=%fused_computation.29 | convolution fusion | flops 3803930624 | bytes 24150016 | tf_op jit(solution)/shard_map/dot_general | solution.py:81
  314.4 0.3 stack.74
  314.7 0.1 reduce_sum.155
  314.8 0.7 gather_fusion
  315.6 2.5 psum.21
  318.1 6.8 %pad_maximum_fusion.1.own_ref = bf16[2,448,4096]{2,1,0:T(8,128)(2,1)} fusion(bf16[1,448,4096]{2,1,0:T(8,128)(2,1)} %get-tuple-element.42, bf16[1,448,4096]{2,1,0:T(8,128)(2,1)} %copy-done), kind=kLoop, calls=%fused_computation.31 | loop fusion | flops 3670016 | bytes 14680064 | tf_op jit(solution)/shard_map/stack | solution.py:79
  324.9 8.9 %psum.22 = f32[4,4]{1,0:T(4,128)S(1)} all-reduce(f32[4,4]{1,0:T(4,128)S(1)} %psum.21), channel_id=1, replica_groups=mesh['x'=2,'core'=2,'fsdp'=4,'pair'=2] {'pair','x'}, use_global_device_ids=true, to_apply=%region_12.14 | all-reduce | flops 16 | bytes 128 | tf_op jit(solution)/shard_map/psum | solution.py:107
  333.8 9.7 %psum.23 = f32[4,4]{1,0:T(4,128)S(1)} all-reduce(f32[4,4]{1,0:T(4,128)S(1)} %psum.22), channel_id=1, replica_groups=mesh['x'=2,'core'=2,'fsdp'=4,'pair'=2] {'fsdp'}, use_global_device_ids=true, to_apply=%region_13.15 | all-reduce | flops 16 | bytes 128 | tf_op jit(solution)/shard_map/psum | solution.py:107
  343.6 0.7 select_reduce_fusion.2
  345.0 0.6 fusion.58
  345.6 1.3 fusion.61
  346.9 0.6 broadcast_divide_fusion
  347.6 0.2 select_reduce_fusion
  347.7 0.6 gather_fusion.1
  348.5 0.7 pad_maximum_fusion.2.scal_ref
  349.1 18.1 %shard_map.111 = (bf16[448,4096]{1,0:T(8,128)(2,1)}, f32[448,4096]{1,0:T(8,128)}, f32[448,4096]{1,0:T(8,128)}) custom-call(f32[6]{0:T(128)} %pad_maximum_fusion.2.scal_ref, bf16[2,448,4096]{2,1,0:T(8,128)(2,1)} %pad_maximum_fusion.1.own_ref, bf16[2,448,4096]{2,1,0:T(8,128)(2,1)} %collective-permute-done.recv_ref, f32[448,4096]{1,0:T(8,128)} %m_ref.1, ...), custom_call_target="tpu_custom_call" | custom-call | flops 36700160 | bytes 51380224 | tf_op jit(solution)/shard_map/pallas_call | solution.py:35
  (25 shorter events, 0.7 us)
Async XLA Ops:
  7.2 262.6 %all-gather.2.cloned.1.call-start = ((), (), s32[]{:S(2)}) async-start(), calls=%async_computation.1 | async-start | bytes 17825792 | tf_op jit(solution)/shard_map/all_gather | solution.py:71
  18.1 149.9 %all-to-all-start = ((bf16[128,16,896]{0,2,1:T(8,128)(2,1)}), bf16[128,16,896]{0,2,1:T(8,128)(2,1)}, u32[]{:S(2)}, u32[]{:S(2)}) async-start(bf16[128,16,896]{0,2,1:T(8,128)(2,1)} %bitcast.57), calls=%async_computation | async-start | bytes 7340032 | tf_op jit(solution)/shard_map/all_to_all | solution.py:69
  269.7 7.8 %copy-start.1 = (bf16[2,1024,1,448]{1,3,2,0:T(8,128)(2,1)S(1)}, bf16[2,1024,1,448]{1,3,2,0:T(8,128)(2,1)}, u32[]{:S(2)}) copy-start(bf16[2,1024,1,448]{1,3,2,0:T(8,128)(2,1)} %copy.24) | copy-start | bytes 5505028
  288.9 12.0 %collective-permute-start = (bf16[2,448,4096]{2,1,0:T(8,128)(2,1)}, bf16[2,448,4096]{2,1,0:T(8,128)(2,1)}, u32[]{:S(2)}, u32[]{:S(2)}) collective-permute-start(bf16[2,448,4096]{2,1,0:T(8,128)(2,1)} %pad_maximum_fusion), channel_id=1, source_target_pairs={{0,8},{8,0},{1,9},{9,1},{2,10},{10,2},{3,11},{11,3},{4,12},{12,4},... | collective-permute-start | bytes 22020104 | tf_op jit(solution)/shard_map/ppermute | solution.py:87
  298.1 16.3 %copy-start = (bf16[1,448,4096]{2,1,0:T(8,128)(2,1)}, bf16[1,448,4096]{2,1,0:T(8,128)(2,1)S(1)}, u32[]{:S(2)}) copy-start(bf16[1,448,4096]{2,1,0:T(8,128)(2,1)S(1)} %fusion.39) | copy-start | bytes 11010052
  318.1 26.8 %copy-start.3 = (s32[4]{0:T(128)S(1)}, s32[4]{0:T(128)}, u32[]{:S(2)}) copy-start(s32[4]{0:T(128)} %param.16) | copy-start | bytes 52
  318.1 26.9 %copy-start.2 = (f32[4]{0:T(128)S(1)}, f32[4]{0:T(128)}, u32[]{:S(2)}) copy-start(f32[4]{0:T(128)} %param.15) | copy-start | bytes 52
  347.5 19.7 %copy-start.4 = (f32[4]{0:T(128)}, f32[4]{0:T(128)S(1)}, u32[]{:S(2)}) copy-start(f32[4]{0:T(128)S(1)} %broadcast_divide_fusion) | copy-start | bytes 52
Sparse Core Ops, SparseCore 0:
  10.8 258.8 all-gather.1

commit v13 on v11

--- a/solution.py
+++ b/solution.py
@@ -86,11 +86,16 @@
     keys = [(i, j) for i in range(groups) for j in range(i, groups)]
     partial = jnp.stack(
         [
-            jnp.sum(owned[i].astype(jnp.float32) * owned[j].astype(jnp.float32), axis=1)
+            jnp.sum(
+                (owned[i].astype(jnp.float32) * owned[j].astype(jnp.float32)).reshape(
+                    own_rows // 8, 8, width
+                ),
+                axis=0,
+            )
             for i, j in keys
         ]
     )
-    sums = jnp.sum(partial, axis=1)
+    sums = jnp.sum(lax.optimization_barrier(partial), axis=(1, 2))
     ids = jnp.arange(groups, dtype=jnp.int32)
     pos = jnp.where(ids % 2 == core, ids // 2, chips_x + ids // 2)
     lo = jnp.minimum(pos[:, None], pos[None, :])

time: 365 us -> 364 us (level)
  no operation moved by 1% of the time
where the time goes in v13:
time: 364 us; the launch traced here: 363 us
  waiting for transfers between devices  225 us (62%)
  local copies, waits for them, and re-layouts  30.9 us (8%)
  matrix products  30.3 us (8%)
  blocking collectives  21.3 us (6%)
  Pallas kernels  18.1 us (5%)
  between operations  15.7 us (4%)
  other arithmetic  13.6 us (4%)
  starting transfers between devices  8.4 us (2%)
    all_to_all x1, waiting for transfers between devices, on_device(): lax.all_to_all(shaped, SAME_CORE, split_axis=1, concat_axis=0, tiled=True)  141 us
    all_gather x1, waiting for transfers between devices, on_device(): mine = lax.all_gather(cotangent, SAME_CORE, axis=0, tiled=True)  82.7 us
    psum x3, blocking collectives, on_device(): gram = lax.psum(gram, axes)  21.3 us
    pallas_call x1, Pallas kernels, adam_update(): pl.pallas_call(adam_kernel, grid=(rows // tile,), in_specs=[pl.BlockSpec(...  18.1 us
    dot_general x1, matrix products, on_device(): lax.dot_general(cols_partner, mine, dims, preferred_element_type=jnp.floa...  16.3 us
    dot_general x1, matrix products, on_device(): lax.dot_general(cols_own, mine, dims, preferred_element_type=jnp.float32)  14 us
    reduce_sum x1, other arithmetic, on_device(): jnp.sum((owned[i].astype(jnp.float32) * owned[j].astype(jnp.float32)).res...  9 us
    all_to_all x1, starting transfers between devices, on_device(): lax.all_to_all(shaped, SAME_CORE, split_axis=1, concat_axis=0, tiled=True)  8.36 us
  transfers between devices with their start and end apart: 3, of which 2 were waited for; matrix products, arithmetic and copies ran while one was open for 12% of the time, Pallas kernels for 0%

profile of v13, /device:TPU:0, one launch (start us, length us, event | category | flops | bytes accessed | tf_op | source)
XLA Modules:
  0.0 363.1 jit_solution(8437319005517230157)
XLA Ops:
  7.2 0.7 all-gather.2.cloned.1.call-update
  7.9 6.1 %copy.12 = bf16[128,14336]{0,1:T(8,128)(2,1)} copy(bf16[128,14336]{1,0:T(8,128)(2,1)} %param.10) | data formatting | bytes 7340032 | tf_op args[0]
  13.9 4.2 %copy.13 = bf16[128,2,8,2,448]{0,4,3,2,1:T(8,128)(2,1)} copy(bf16[128,2,8,2,448]{0,4,2,3,1:T(8,128)(2,1)} %bitcast.91) | data formatting | bytes 7340032 | tf_op jit(solution)/shard_map/transpose | solution.py:67
  18.1 8.4 %all-to-all-start = ((bf16[128,16,896]{0,2,1:T(8,128)(2,1)}), bf16[128,16,896]{0,2,1:T(8,128)(2,1)}, u32[]{:S(2)}, u32[]{:S(2)}) async-start(bf16[128,16,896]{0,2,1:T(8,128)(2,1)} %bitcast.90), calls=%async_computation | async-start | bytes 7340032 | tf_op jit(solution)/shard_map/all_to_all | solution.py:69
  26.5 141.5 %all-to-all-done = bf16[128,16,896]{0,2,1:T(8,128)(2,1)} async-done(((bf16[128,16,896]{0,2,1:T(8,128)(2,1)}), bf16[128,16,896]{0,2,1:T(8,128)(2,1)}, u32[]{:S(2)}, u32[]{:S(2)}) %all-to-all-start) | async-done | bytes 3670048 | tf_op jit(solution)/shard_map/all_to_all | solution.py:69
  168.0 6.7 %copy.14 = bf16[16,128,1,896]{1,0,3,2:T(8,128)(2,1)} copy(bf16[16,128,1,896]{1,3,0,2:T(8,128)(2,1)} %bitcast.4) | data formatting | bytes 7340032 | tf_op jit(solution)/shard_map/all_to_all | solution.py:69
  174.6 6.5 %reshape.387 = bf16[2,1024,2,448]{1,0,3,2:T(2,128)(2,1)} reshape(bf16[16,128,1,896]{1,0,3,2:T(8,128)(2,1)} %copy.14) | data formatting | bytes 7340032 | tf_op jit(solution)/shard_map/reshape | solution.py:70
  181.2 5.8 %constant_dynamic-slice_fusion.1 = (bf16[2,1024,1,448]{1,0,3,2:T(2,128)(2,1)S(1)}, bf16[2,1024,1,448]{1,0,3,2:T(2,128)(2,1)}) fusion(bf16[2,1024,2,448]{1,0,3,2:T(2,128)(2,1)} %reshape.387, s32[]{:T(128)S(6)} %select_n.125, s32[]{:T(128)S(6)} %select_n.127), kind=kLoop, calls=%fused_computation.105 | loop fusion | bytes 7340040 | tf_op jit(solution)/shard_map/jit(_take) | solution.py:75
  187.0 82.7 %all-gather.2.cloned.1.call-done = bf16[2048,4096]{1,0:T(8,128)(2,1)} async-done(((bf16[128,4096]{1,0:T(8,128)(2,1)}), bf16[2048,4096]{1,0:T(8,128)(2,1)}) %all-gather.2.cloned.1.call-update) | async-done | bytes 16777232 | tf_op jit(solution)/shard_map/all_gather | solution.py:71
  269.7 16.3 %convolution_convert_fusion = bf16[2,448,4096]{2,1,0:T(8,128)(2,1)} fusion(bf16[2,1024,4096]{2,1,0:T(8,128)(2,1)} %bitcast.88, bf16[2,1024,1,448]{1,0,3,2:T(2,128)(2,1)} %get-tuple-element.41, pred[]{:T(512)S(6)} %and.97), kind=kOutput, calls=%fused_computation.32 | convolution fusion | flops 7520780288 | bytes 25952256 | tf_op jit(solution)/shard_map/dot_general | solution.py:76
  286.0 0.1 compare_select_fusion
  286.1 0.1 reshape.448
  286.9 0.1 fusion.42
  287.0 14.0 %convolution_convert_fusion.1.own_ref = bf16[2,448,4096]{2,1,0:T(8,128)(2,1)S(1)} fusion(bf16[2,1024,4096]{2,1,0:T(8,128)(2,1)} %bitcast.89, bf16[2,1024,1,448]{1,0,3,2:T(2,128)(2,1)S(1)} %get-tuple-element.40, pred[]{:T(512)S(6)} %and.96), kind=kOutput, calls=%fused_computation.33 | convolution fusion | flops 7520780288 | bytes 25952256 | tf_op jit(solution)/shard_map/dot_general | solution.py:80
  301.1 9.0 %fusion.19 = (f32[8,4096]{1,0:T(8,128)S(1)}, f32[8,4096]{1,0:T(8,128)S(1)}, f32[8,4096]{1,0:T(8,128)S(1)}, f32[8,4096]{1,0:T(8,128)S(1)}, f32[8,4096]{1,0:T(8,12...) fusion(bf16[2,448,4096]{2,1,0:T(8,128)(2,1)} %collective-permut, ...), kind=kLoop, calls=%fused_computation.31 | loop fusion | flops 43712512 | bytes 15990784 | tf_op jit(solution)/shard_map/reduce_sum | solution.py:89
  310.3 0.2 reduce_sum.155
  310.5 0.7 gather_fusion
  311.2 0.1 reshape.447
  311.3 0.1 and_select_fusion
  311.4 2.6 psum.21
  314.0 8.9 %psum.22 = f32[4,4]{1,0:T(4,128)S(1)} all-reduce(f32[4,4]{1,0:T(4,128)S(1)} %psum.21), channel_id=1, replica_groups=mesh['x'=2,'core'=2,'fsdp'=4,'pair'=2] {'pair','x'}, use_global_device_ids=true, to_apply=%region_12.14 | all-reduce | flops 16 | bytes 128 | tf_op jit(solution)/shard_map/psum | solution.py:106
  322.9 9.7 %psum.23 = f32[4,4]{1,0:T(4,128)S(1)} all-reduce(f32[4,4]{1,0:T(4,128)S(1)} %psum.22), channel_id=1, replica_groups=mesh['x'=2,'core'=2,'fsdp'=4,'pair'=2] {'fsdp'}, use_global_device_ids=true, to_apply=%region_13.15 | all-reduce | flops 16 | bytes 128 | tf_op jit(solution)/shard_map/psum | solution.py:106
  332.7 0.7 select_reduce_fusion.2
  334.0 0.1 select_reduce_fusion.1
  334.1 0.6 fusion.46
  334.7 1.3 fusion.49
  336.0 0.6 broadcast_divide_fusion
  336.6 0.2 select_reduce_fusion
  336.8 0.6 gather_fusion.1
  337.5 0.1 and_select_fusion.3
  337.5 0.7 pad_maximum_fusion.scal_ref
  338.2 18.1 %shard_map.111 = (bf16[448,4096]{1,0:T(8,128)(2,1)}, f32[448,4096]{1,0:T(8,128)}, f32[448,4096]{1,0:T(8,128)}) custom-call(f32[6]{0:T(128)} %pad_maximum_fusion.scal_ref, bf16[2,448,4096]{2,1,0:T(8,128)(2,1)} %copy-done, bf16[2,448,4096]{2,1,0:T(8,128)(2,1)} %collective-permute-done.recv_ref, f32[448,4096]{1,0:T(8,128)} %m_ref.1, f32[448,4096]{1,0:T(8,128)} %s_ref.1, ...), custom_call_target="tpu_custom_call" | custom-call | flops 36700160 | bytes 51380224 | tf_op jit(solution)/shard_map/pallas_call | solution.py:35
  (27 shorter events, 0.2 us)
Async XLA Ops:
  7.2 262.6 %all-gather.2.cloned.1.call-start = ((), (), s32[]{:S(2)}) async-start(), calls=%async_computation.1 | async-start | bytes 17825792 | tf_op jit(solution)/shard_map/all_gather | solution.py:71
  18.1 149.9 %all-to-all-start = ((bf16[128,16,896]{0,2,1:T(8,128)(2,1)}), bf16[128,16,896]{0,2,1:T(8,128)(2,1)}, u32[]{:S(2)}, u32[]{:S(2)}) async-start(bf16[128,16,896]{0,2,1:T(8,128)(2,1)} %bitcast.90), calls=%async_computation | async-start | bytes 7340032 | tf_op jit(solution)/shard_map/all_to_all | solution.py:69
  286.0 15.1 %collective-permute-start = (bf16[2,448,4096]{2,1,0:T(8,128)(2,1)}, bf16[2,448,4096]{2,1,0:T(8,128)(2,1)}, u32[]{:S(2)}, u32[]{:S(2)}) collective-permute-start(bf16[2,448,4096]{2,1,0:T(8,128)(2,1)} %convolution_convert_fusion), channel_id=1, source_target_pairs={{0,8},{8,0},{1,9},{9,1},{2,10},{10,2},{3,11},{11,3},{4,12},{12,4},... | collective-permute-start | bytes 22020104 | tf_op jit(solution)/shard_map/ppermute | solution.py:79
  301.1 9.0 %copy-start = (bf16[2,448,4096]{2,1,0:T(8,128)(2,1)}, bf16[2,448,4096]{2,1,0:T(8,128)(2,1)S(1)}, u32[]{:S(2)}) copy-start(bf16[2,448,4096]{2,1,0:T(8,128)(2,1)S(1)} %convolution_convert_fusion.1.own_ref) | copy-start | bytes 22020100
  310.1 23.9 %copy-start.2 = (s32[4]{0:T(128)S(1)}, s32[4]{0:T(128)}, u32[]{:S(2)}) copy-start(s32[4]{0:T(128)} %param.16) | copy-start | bytes 52
  310.1 24.0 %copy-start.1 = (f32[4]{0:T(128)S(1)}, f32[4]{0:T(128)}, u32[]{:S(2)}) copy-start(f32[4]{0:T(128)} %param.15) | copy-start | bytes 52
  336.6 19.7 %copy-start.3 = (f32[4]{0:T(128)}, f32[4]{0:T(128)S(1)}, u32[]{:S(2)}) copy-start(f32[4]{0:T(128)S(1)} %broadcast_divide_fusion) | copy-start | bytes 52
Sparse Core Ops, SparseCore 0:
  10.8 258.8 all-gather.1

commit v14 on v13

--- a/solution.py
+++ b/solution.py
@@ -102,7 +102,7 @@
     hi = jnp.maximum(pos[:, None], pos[None, :])
     device_gram = jnp.take(sums, lo * groups - lo * (lo - 1) // 2 + (hi - lo))
     gram = device_gram
-    for axes in (("core",), ("pair", "x"), ("fsdp",)):
+    for axes in (("core",), ("x",), ("fsdp", "pair")):
         gram = lax.psum(gram, axes)
     score = jnp.sum(gram, axis=1) * (groups / jnp.trace(gram))
     onehot = (domain_ids[:, None] == jnp.arange(groups, dtype=jnp.int32)[None, :]).astype(

time: 364 us -> 370 us (1.016)
  blocking collectives: 21.3 us -> 27 us
    psum x3, blocking collectives: 21.3 us -> 27 us  [on_device(): gram = lax.psum(gram, axes)]
where the time goes in v14:
time: 370 us; the launch traced here: 369 us
  waiting for transfers between devices  225 us (61%)
  local copies, waits for them, and re-layouts  30.9 us (8%)
  matrix products  30.3 us (8%)
  blocking collectives  27 us (7%)
  Pallas kernels  18.1 us (5%)
  between operations  15.7 us (4%)
  other arithmetic  13.6 us (4%)
  starting transfers between devices  8.4 us (2%)
    all_to_all x1, waiting for transfers between devices, on_device(): lax.all_to_all(shaped, SAME_CORE, split_axis=1, concat_axis=0, tiled=True)  141 us
    all_gather x1, waiting for transfers between devices, on_device(): mine = lax.all_gather(cotangent, SAME_CORE, axis=0, tiled=True)  82.7 us
    psum x3, blocking collectives, on_device(): gram = lax.psum(gram, axes)  27 us
    pallas_call x1, Pallas kernels, adam_update(): pl.pallas_call(adam_kernel, grid=(rows // tile,), in_specs=[pl.BlockSpec(...  18.1 us
    dot_general x1, matrix products, on_device(): lax.dot_general(cols_partner, mine, dims, preferred_element_type=jnp.floa...  16.3 us
    dot_general x1, matrix products, on_device(): lax.dot_general(cols_own, mine, dims, preferred_element_type=jnp.float32)  14 us
    reduce_sum x1, other arithmetic, on_device(): jnp.sum((owned[i].astype(jnp.float32) * owned[j].astype(jnp.float32)).res...  9 us
    all_to_all x1, starting transfers between devices, on_device(): lax.all_to_all(shaped, SAME_CORE, split_axis=1, concat_axis=0, tiled=True)  8.36 us
  transfers between devices with their start and end apart: 3, of which 2 were waited for; matrix products, arithmetic and copies ran while one was open for 12% of the time, Pallas kernels for 0%

profile of v14, /device:TPU:0, one launch (start us, length us, event | category | flops | bytes accessed | tf_op | source)
XLA Modules:
  0.0 368.8 jit_solution(16560651855670042319)
XLA Ops:
  7.2 0.7 all-gather.2.cloned.1.call-update
  7.9 6.1 %copy.12 = bf16[128,14336]{0,1:T(8,128)(2,1)} copy(bf16[128,14336]{1,0:T(8,128)(2,1)} %param.10) | data formatting | bytes 7340032 | tf_op args[0]
  13.9 4.2 %copy.13 = bf16[128,2,8,2,448]{0,4,3,2,1:T(8,128)(2,1)} copy(bf16[128,2,8,2,448]{0,4,2,3,1:T(8,128)(2,1)} %bitcast.91) | data formatting | bytes 7340032 | tf_op jit(solution)/shard_map/transpose | solution.py:67
  18.1 8.4 %all-to-all-start = ((bf16[128,16,896]{0,2,1:T(8,128)(2,1)}), bf16[128,16,896]{0,2,1:T(8,128)(2,1)}, u32[]{:S(2)}, u32[]{:S(2)}) async-start(bf16[128,16,896]{0,2,1:T(8,128)(2,1)} %bitcast.90), calls=%async_computation | async-start | bytes 7340032 | tf_op jit(solution)/shard_map/all_to_all | solution.py:69
  26.5 141.5 %all-to-all-done = bf16[128,16,896]{0,2,1:T(8,128)(2,1)} async-done(((bf16[128,16,896]{0,2,1:T(8,128)(2,1)}), bf16[128,16,896]{0,2,1:T(8,128)(2,1)}, u32[]{:S(2)}, u32[]{:S(2)}) %all-to-all-start) | async-done | bytes 3670048 | tf_op jit(solution)/shard_map/all_to_all | solution.py:69
  168.0 6.7 %copy.14 = bf16[16,128,1,896]{1,0,3,2:T(8,128)(2,1)} copy(bf16[16,128,1,896]{1,3,0,2:T(8,128)(2,1)} %bitcast.4) | data formatting | bytes 7340032 | tf_op jit(solution)/shard_map/all_to_all | solution.py:69
  174.6 6.5 %reshape.387 = bf16[2,1024,2,448]{1,0,3,2:T(2,128)(2,1)} reshape(bf16[16,128,1,896]{1,0,3,2:T(8,128)(2,1)} %copy.14) | data formatting | bytes 7340032 | tf_op jit(solution)/shard_map/reshape | solution.py:70
  181.2 5.8 %constant_dynamic-slice_fusion.1 = (bf16[2,1024,1,448]{1,0,3,2:T(2,128)(2,1)S(1)}, bf16[2,1024,1,448]{1,0,3,2:T(2,128)(2,1)}) fusion(bf16[2,1024,2,448]{1,0,3,2:T(2,128)(2,1)} %reshape.387, s32[]{:T(128)S(6)} %select_n.125, s32[]{:T(128)S(6)} %select_n.127), kind=kLoop, calls=%fused_computation.105 | loop fusion | bytes 7340040 | tf_op jit(solution)/shard_map/jit(_take) | solution.py:75
  187.0 82.7 %all-gather.2.cloned.1.call-done = bf16[2048,4096]{1,0:T(8,128)(2,1)} async-done(((bf16[128,4096]{1,0:T(8,128)(2,1)}), bf16[2048,4096]{1,0:T(8,128)(2,1)}) %all-gather.2.cloned.1.call-update) | async-done | bytes 16777232 | tf_op jit(solution)/shard_map/all_gather | solution.py:71
  269.7 16.3 %convolution_convert_fusion = bf16[2,448,4096]{2,1,0:T(8,128)(2,1)} fusion(bf16[2,1024,4096]{2,1,0:T(8,128)(2,1)} %bitcast.88, bf16[2,1024,1,448]{1,0,3,2:T(2,128)(2,1)} %get-tuple-element.41, pred[]{:T(512)S(6)} %and.97), kind=kOutput, calls=%fused_computation.32 | convolution fusion | flops 7520780288 | bytes 25952256 | tf_op jit(solution)/shard_map/dot_general | solution.py:76
  286.0 0.1 compare_select_fusion
  286.1 0.1 reshape.448
  286.9 0.1 fusion.42
  287.0 14.0 %convolution_convert_fusion.1.own_ref = bf16[2,448,4096]{2,1,0:T(8,128)(2,1)S(1)} fusion(bf16[2,1024,4096]{2,1,0:T(8,128)(2,1)} %bitcast.89, bf16[2,1024,1,448]{1,0,3,2:T(2,128)(2,1)S(1)} %get-tuple-element.40, pred[]{:T(512)S(6)} %and.96), kind=kOutput, calls=%fused_computation.33 | convolution fusion | flops 7520780288 | bytes 25952256 | tf_op jit(solution)/shard_map/dot_general | solution.py:80
  301.1 9.0 %fusion.19 = (f32[8,4096]{1,0:T(8,128)S(1)}, f32[8,4096]{1,0:T(8,128)S(1)}, f32[8,4096]{1,0:T(8,128)S(1)}, f32[8,4096]{1,0:T(8,128)S(1)}, f32[8,4096]{1,0:T(8,12...) fusion(bf16[2,448,4096]{2,1,0:T(8,128)(2,1)} %collective-permut, ...), kind=kLoop, calls=%fused_computation.31 | loop fusion | flops 43712512 | bytes 15990784 | tf_op jit(solution)/shard_map/reduce_sum | solution.py:89
  310.3 0.2 reduce_sum.155
  310.5 0.7 gather_fusion
  311.2 0.1 reshape.447
  311.3 0.1 and_select_fusion
  311.4 2.6 psum.21
  314.0 4.9 %psum.22 = f32[4,4]{1,0:T(4,128)S(1)} all-reduce(f32[4,4]{1,0:T(4,128)S(1)} %psum.21), channel_id=1, replica_groups=mesh['x'=2,'core'=2,'fsdp'=4,'pair'=2] {'x'}, use_global_device_ids=true, to_apply=%region_12.14 | all-reduce | flops 16 | bytes 128 | tf_op jit(solution)/shard_map/psum | solution.py:106
  318.9 19.4 %psum.23 = f32[4,4]{1,0:T(4,128)S(1)} all-reduce(f32[4,4]{1,0:T(4,128)S(1)} %psum.22), channel_id=1, replica_groups=mesh['x'=2,'core'=2,'fsdp'=4,'pair'=2] {'fsdp','pair'}, use_global_device_ids=true, to_apply=%region_13.15 | all-reduce | flops 16 | bytes 128 | tf_op jit(solution)/shard_map/psum | solution.py:106
  338.3 0.7 select_reduce_fusion.2
  339.7 0.1 select_reduce_fusion.1
  339.8 0.6 fusion.46
  340.4 1.3 fusion.49
  341.6 0.6 broadcast_divide_fusion
  342.3 0.2 select_reduce_fusion
  342.5 0.6 gather_fusion.1
  343.1 0.1 and_select_fusion.3
  343.2 0.7 pad_maximum_fusion.scal_ref
  343.9 18.1 %shard_map.111 = (bf16[448,4096]{1,0:T(8,128)(2,1)}, f32[448,4096]{1,0:T(8,128)}, f32[448,4096]{1,0:T(8,128)}) custom-call(f32[6]{0:T(128)} %pad_maximum_fusion.scal_ref, bf16[2,448,4096]{2,1,0:T(8,128)(2,1)} %copy-done, bf16[2,448,4096]{2,1,0:T(8,128)(2,1)} %collective-permute-done.recv_ref, f32[448,4096]{1,0:T(8,128)} %m_ref.1, f32[448,4096]{1,0:T(8,128)} %s_ref.1, ...), custom_call_target="tpu_custom_call" | custom-call | flops 36700160 | bytes 51380224 | tf_op jit(solution)/shard_map/pallas_call | solution.py:35
  (27 shorter events, 0.2 us)
Async XLA Ops:
  7.2 262.6 %all-gather.2.cloned.1.call-start = ((), (), s32[]{:S(2)}) async-start(), calls=%async_computation.1 | async-start | bytes 17825792 | tf_op jit(solution)/shard_map/all_gather | solution.py:71
  18.1 149.9 %all-to-all-start = ((bf16[128,16,896]{0,2,1:T(8,128)(2,1)}), bf16[128,16,896]{0,2,1:T(8,128)(2,1)}, u32[]{:S(2)}, u32[]{:S(2)}) async-start(bf16[128,16,896]{0,2,1:T(8,128)(2,1)} %bitcast.90), calls=%async_computation | async-start | bytes 7340032 | tf_op jit(solution)/shard_map/all_to_all | solution.py:69
  286.0 15.1 %collective-permute-start = (bf16[2,448,4096]{2,1,0:T(8,128)(2,1)}, bf16[2,448,4096]{2,1,0:T(8,128)(2,1)}, u32[]{:S(2)}, u32[]{:S(2)}) collective-permute-start(bf16[2,448,4096]{2,1,0:T(8,128)(2,1)} %convolution_convert_fusion), channel_id=1, source_target_pairs={{0,8},{8,0},{1,9},{9,1},{2,10},{10,2},{3,11},{11,3},{4,12},{12,4},... | collective-permute-start | bytes 22020104 | tf_op jit(solution)/shard_map/ppermute | solution.py:79
  301.1 9.0 %copy-start = (bf16[2,448,4096]{2,1,0:T(8,128)(2,1)}, bf16[2,448,4096]{2,1,0:T(8,128)(2,1)S(1)}, u32[]{:S(2)}) copy-start(bf16[2,448,4096]{2,1,0:T(8,128)(2,1)S(1)} %convolution_convert_fusion.1.own_ref) | copy-start | bytes 22020100
  310.1 29.6 %copy-start.2 = (s32[4]{0:T(128)S(1)}, s32[4]{0:T(128)}, u32[]{:S(2)}) copy-start(s32[4]{0:T(128)} %param.16) | copy-start | bytes 52
  310.1 29.7 %copy-start.1 = (f32[4]{0:T(128)S(1)}, f32[4]{0:T(128)}, u32[]{:S(2)}) copy-start(f32[4]{0:T(128)} %param.15) | copy-start | bytes 52
  342.3 19.7 %copy-start.3 = (f32[4]{0:T(128)}, f32[4]{0:T(128)S(1)}, u32[]{:S(2)}) copy-start(f32[4]{0:T(128)S(1)} %broadcast_divide_fusion) | copy-start | bytes 52
Sparse Core Ops, SparseCore 0:
  10.8 258.8 all-gather.1
